TPU v7x, 256 devices: a whole 4x4x8 slice. The times are simulated.
256 devices in a mesh: dp: 4 (over y_lo, core), seq: 64 (over x, y_hi, z).
Axes of the slice: x: 4, y: 4 (y_hi: 2, y_lo: 2; y = y_hi * 2 + y_lo), z: 8, core: 2. Of those that a mesh axis runs over, the one named last changes fastest.
Arguments:
- inputs: bfloat16 [8, 65536, 768], P('dp', 'seq'), may hold values from -6 to 6
- cotangent: bfloat16 [8, 65536, 768], P('dp', 'seq'), may hold values from -6 to 6
- control: int32 [8], P('dp'), may hold values from 0 to 15
- table_in: float32 [16, 768], replicated, may hold values from 0.3 to 3
- table_out: float32 [16, 768], replicated, may hold values from 0.3 to 3
- factor_one: bfloat16 [256, 256, 256], P('seq'), may hold values from -0.375 to 0.375
- second_block_factor: bfloat16 [256, 256, 256], P('seq'), may hold values from -0.375 to 0.375
Outputs:
- grad_inputs: bfloat16 [8, 65536, 768], P('dp', 'seq')
- grad_one: float32 [256, 256, 256], P('seq')
- second_factor_gradient: float32 [256, 256, 256], P('seq')
All inputs are finite; a program needn't handle non-finite values.
Results may differ from a plain program's by a relative error of at most 0.0072.
Values may be sent and summed in bfloat16 or wider, within the bound.
No kernel may reach another device: no remote copies, remote signals or barrier semaphores. Data moves between devices by JAX's collectives and lax.ppermute only.
A program may use at most 64 MiB of HBM per device.

v0:
```python
import jax
import jax.numpy as jnp
from jax import lax
from jax.sharding import PartitionSpec as P

CHUNKS = 2


def dp_sum(x, n_dp):
    step = 1
    while step < n_dp:
        perm = [(i, i ^ step) for i in range(n_dp)]
        x = x + lax.ppermute(x, "dp", perm)
        step *= 2
    return x


def dp_sum_halves(x, n_dp):
    if n_dp != 4 or x.shape[0] % 2:
        return dp_sum(x, n_dp)
    core = lax.axis_index("dp") % 2
    x = x + lax.ppermute(x, "dp", [(i, i ^ 1) for i in range(n_dp)])
    halves = x.reshape((2, x.shape[0] // 2) + x.shape[1:])
    mine = lax.dynamic_index_in_dim(halves, core, 0, keepdims=False)
    mine = mine + lax.ppermute(mine, "dp", [(i, i ^ 2) for i in range(n_dp)])
    other = lax.ppermute(mine, "dp", [(i, i ^ 1) for i in range(n_dp)])
    first = jnp.where(core == 0, mine, other)
    second = jnp.where(core == 0, other, mine)
    return jnp.concatenate([first, second], axis=0)


def on_device(inputs, cotangent, control, table_in, table_out, factor_one, second_block_factor, n_dp):
    f32, bf16 = jnp.float32, jnp.bfloat16
    images, rows, width = inputs.shape
    own, blocks, _ = factor_one.shape
    n_seq = blocks // own
    per = own // CHUNKS
    tables = table_in.shape[0]
    one_hot = (control[:, None] == jnp.arange(tables, dtype=jnp.int32)[None, :]).astype(f32)
    gate_in = jnp.dot(one_hot, table_in, precision=lax.Precision.HIGHEST)
    gate_out = jnp.dot(one_hot, table_out, precision=lax.Precision.HIGHEST)
    scaled = (
        inputs.reshape(images, own, blocks, width).astype(f32) * gate_in[:, None, None, :]
    ).astype(bf16)
    f1 = factor_one.reshape(own, n_seq, own, blocks)
    upstream = cotangent.reshape(images, own, blocks, width)

    recv1 = []
    for k in range(CHUNKS):
        mixed = jnp.einsum(
            "asjb,iabd->sajid", f1[:, :, k * per:(k + 1) * per, :], scaled, preferred_element_type=f32
        ).astype(bf16)
        recv1.append(lax.all_to_all(mixed, "seq", 0, 0, tiled=True))

    recv2 = []
    sfg = []
    for k in range(CHUNKS):
        got = recv1[k].reshape(blocks, per, images, width)
        f2 = second_block_factor[k * per:(k + 1) * per]
        mixed_b = jnp.einsum("jpa,ajid->jpid", f2, got, preferred_element_type=f32)
        logistic = jax.nn.sigmoid(mixed_b)
        up = jnp.transpose(upstream[:, k * per:(k + 1) * per], (1, 2, 0, 3))
        value_gradient = (
            up * gate_out[None, None, :, :] * logistic * (1.0 + mixed_b * (1.0 - logistic))
        ).astype(bf16)
        part = jnp.einsum("jpid,ajid->jpa", value_gradient, got, preferred_element_type=f32)
        send = jnp.einsum("jpa,jpid->ajid", f2, value_gradient, preferred_element_type=f32).astype(bf16)
        send = send.reshape(n_seq, own, per, images, width)
        part, send = lax.optimization_barrier((part, send))
        sfg.append(dp_sum_halves(part, n_dp))
        recv2.append(lax.all_to_all(send, "seq", 0, 0, tiled=True))

    grad_one = []
    back_sum = None
    for k in range(CHUNKS):
        part = jnp.einsum("sajid,iabd->asjb", recv2[k], scaled, preferred_element_type=f32)
        grad_one.append(dp_sum_halves(part, n_dp))
        term = jnp.einsum(
            "asjb,sajid->iabd", f1[:, :, k * per:(k + 1) * per, :], recv2[k], preferred_element_type=f32
        )
        back_sum = term if back_sum is None else back_sum + term
    grad_one = jnp.concatenate(grad_one, axis=2).reshape(own, blocks, blocks)
    grad_inputs = (
        (back_sum * gate_in[:, None, None, :]).astype(bf16).reshape(images, rows, width)
    )
    second_factor_gradient = jnp.concatenate(sfg, axis=0)
    return (grad_inputs, grad_one, second_factor_gradient)


def solution(mesh):
    n_dp = mesh.shape["dp"]

    def fn(*args):
        return on_device(*args, n_dp=n_dp)

    return jax.shard_map(
        fn,
        mesh=mesh,
        in_specs=(
            P("dp", "seq", None),
            P("dp", "seq", None),
            P("dp"),
            P(),
            P(),
            P("seq", None, None),
            P("seq", None, None),
        ),
        out_specs=(P("dp", "seq", None), P("seq", None, None), P("seq", None, None)),
        check_vma=False,
    )
```

profile of v0, /device:TPU:1, one launch (start us, length us, event | category | flops | bytes accessed | tf_op | source)
XLA Modules:
  0.0 232.9 jit_solution(9799337508155778602)
XLA Ops:
  3.2 2.6 %fusion.35 = bf16[64,4,2,2,768]{4,0,2,3,1:T(8,128)(2,1)S(1)} fusion(bf16[4,64,2,256]{3,0,2,1:T(4,128)(2,1)S(1)} %get-tuple-element.27, f32[2,768]{1,0:T(2,128)S(1)} %fusion.73, bf16[2,4,256,768]{3,2,1,0:T(8,128)(2,1)} %bitcast.183), kind=kOutput, calls=%fused_computation.41 | convolution fusion | flops 408158208 | bytes 4986880 | tf_op jit(solution)/shard_map/asjb,iabd->sajid/dot_general | solution.py:50
  5.8 2.8 %copy.86 = bf16[64,4,2,2,768]{4,2,3,1,0:T(2,128)(2,1)} copy(bf16[64,4,2,2,768]{4,0,2,3,1:T(8,128)(2,1)S(1)} %fusion.35) | data formatting | bytes 3145728 | tf_op jit(solution)/shard_map/convert_element_type | solution.py:52
  8.6 15.1 %all-to-all-start.2 = ((bf16[64,4,2,2,768]{4,2,3,1,0:T(2,128)(2,1)}), bf16[64,4,2,2,768]{4,2,3,1,0:T(2,128)(2,1)S(1)}, u32[]{:S(2)}, u32[]{:S(2)}) async-start(bf16[64,4,2,2,768]{4,2,3,1,0:T(2,128)(2,1)} %copy.86), calls=%async_computation.2 | async-start | bytes 3145728 | tf_op jit(solution)/shard_map/all_to_all | solution.py:53
  23.7 2.6 %fusion.38 = bf16[64,4,2,2,768]{4,0,2,3,1:T(8,128)(2,1)S(1)} fusion(bf16[4,64,2,256]{3,0,2,1:T(4,128)(2,1)S(1)} %get-tuple-element.28, f32[2,768]{1,0:T(2,128)S(1)} %fusion.73, bf16[2,4,256,768]{3,2,1,0:T(8,128)(2,1)} %bitcast.184), kind=kOutput, calls=%fused_computation.42 | convolution fusion | flops 408158208 | bytes 4986880 | tf_op jit(solution)/shard_map/asjb,iabd->sajid/dot_general | solution.py:50
  26.4 2.8 %copy.75 = bf16[64,4,2,2,768]{4,2,3,1,0:T(2,128)(2,1)} copy(bf16[64,4,2,2,768]{4,0,2,3,1:T(8,128)(2,1)S(1)} %fusion.38) | data formatting | bytes 3145728 | tf_op jit(solution)/shard_map/convert_element_type | solution.py:52
  29.2 33.2 %all-to-all-done.2 = bf16[64,4,2,2,768]{4,2,3,1,0:T(2,128)(2,1)S(1)} async-done(((bf16[64,4,2,2,768]{4,2,3,1,0:T(2,128)(2,1)}), bf16[64,4,2,2,768]{4,2,3,1,0:T(2,128)(2,1)S(1)}, u32[]{:S(2)}, u32[]{:S(2)}) %all-to-all-start.2) | async-done | bytes 1572896 | tf_op jit(solution)/shard_map/all_to_all | solution.py:53
  62.4 8.3 %all-to-all-start = ((bf16[64,4,2,2,768]{4,2,3,1,0:T(2,128)(2,1)}), bf16[64,4,2,2,768]{4,2,3,1,0:T(2,128)(2,1)S(1)}, u32[]{:S(2)}, u32[]{:S(2)}) async-start(bf16[64,4,2,2,768]{4,2,3,1,0:T(2,128)(2,1)} %copy.75), calls=%async_computation | async-start | bytes 3145728 | tf_op jit(solution)/shard_map/all_to_all | solution.py:53
  70.7 3.8 %fusion.77 = (bf16[2,2,256,768]{3,2,1,0:T(8,128)(2,1)}, bf16[2,2,256,768]{3,2,1,0:T(8,128)(2,1)}) fusion(bf16[2,4,256,768]{3,2,1,0:T(8,128)(2,1)} %bitcast.176), kind=kLoop, calls=%fused_computation.84 | loop fusion | bytes 6291456 | tf_op jit(solution)/shard_map/slice | solution.py:62
  74.5 2.6 %copy.128 = bf16[2,2,256,768]{2,3,0,1:T(8,128)(2,1)} copy(bf16[2,2,256,768]{3,2,1,0:T(8,128)(2,1)} %get-tuple-element.17) | data formatting | bytes 3145728
  77.3 3.0 %fusion.13 = bf16[2,256,2,768]{1,3,2,0:T(8,128)(2,1)S(1)} fusion(bf16[2,2,256,768]{2,3,0,1:T(8,128)(2,1)} %copy.128, f32[2,768]{1,0:T(2,128)S(1)} %fusion.74, bf16[256,2,2,768]{3,1,2,0:T(2,128)(2,1)S(1)} %bitcast.173, bf16[4,256,256]{2,1,0:T(8,128)(2,1)} %param.13), kind=kOutput, calls=%fused_computation.17 | convolution fusion | flops 411303936 | bytes 4986880 | tf_op jit(solution)/shard_map/jpa,ajid->jpid/dot_general | solution.py:60
  81.5 1.8 fusion.42
  83.3 3.9 %reshape.53 = bf16[64,4,2,2,768]{4,1,0,3,2:T(4,128)(2,1)} reshape(bf16[256,2,2,768]{3,0,2,1:T(8,128)(2,1)} %fusion.42) | data formatting | bytes 3145728 | tf_op jit(solution)/shard_map/reshape | solution.py:68
  87.2 3.1 %fusion.62 = f32[2,256,256]{2,1,0:T(8,128)} fusion(bf16[2,256,2,768]{1,3,2,0:T(8,128)(2,1)} %copy-done.2, bf16[256,2,2,768]{3,1,2,0:T(2,128)(2,1)S(1)} %bitcast.174), kind=kOutput, calls=%fused_computation.54 | convolution fusion | flops 402653184 | bytes 3670016 | tf_op jit(solution)/shard_map/jpid,ajid->jpa/dot_general | solution.py:66
  90.3 2.8 %copy.93 = bf16[64,4,2,2,768]{4,2,3,1,0:T(2,128)(2,1)} copy(bf16[64,4,2,2,768]{4,1,0,3,2:T(4,128)(2,1)S(1)} %copy-done.3) | data formatting | bytes 3145728 | tf_op jit(solution)/shard_map/optimization_barrier | solution.py:69
  93.0 14.9 %all-to-all-done = bf16[64,4,2,2,768]{4,2,3,1,0:T(2,128)(2,1)S(1)} async-done(((bf16[64,4,2,2,768]{4,2,3,1,0:T(2,128)(2,1)}), bf16[64,4,2,2,768]{4,2,3,1,0:T(2,128)(2,1)S(1)}, u32[]{:S(2)}, u32[]{:S(2)}) %all-to-all-start) | async-done | bytes 1572896 | tf_op jit(solution)/shard_map/all_to_all | solution.py:53
  108.0 9.1 %all-to-all-start.3 = ((bf16[64,4,2,2,768]{4,2,3,1,0:T(2,128)(2,1)}), bf16[64,4,2,2,768]{4,2,3,1,0:T(2,128)(2,1)}, u32[]{:S(2)}, u32[]{:S(2)}) async-start(bf16[64,4,2,2,768]{4,2,3,1,0:T(2,128)(2,1)} %copy.93), calls=%async_computation.3 | async-start | bytes 3145728 | tf_op jit(solution)/shard_map/all_to_all | solution.py:71
  118.7 3.1 %fusion.23 = bf16[2,256,2,768]{1,3,2,0:T(8,128)(2,1)S(1)} fusion(bf16[2,2,256,768]{2,3,0,1:T(8,128)(2,1)} %copy.126, f32[2,768]{1,0:T(2,128)S(1)} %fusion.74, bf16[256,2,2,768]{3,1,2,0:T(2,128)(2,1)S(1)} %bitcast.171, bf16[4,256,256]{2,1,0:T(8,128)(2,1)} %param.13), kind=kOutput, calls=%fused_computation.30 | convolution fusion | flops 411303936 | bytes 4986880 | tf_op jit(solution)/shard_map/jpa,ajid->jpid/dot_general | solution.py:60
  121.7 1.8 fusion.41
  123.5 3.9 %reshape.51 = bf16[64,4,2,2,768]{4,1,0,3,2:T(4,128)(2,1)} reshape(bf16[256,2,2,768]{3,0,2,1:T(8,128)(2,1)} %fusion.41) | data formatting | bytes 3145728 | tf_op jit(solution)/shard_map/reshape | solution.py:68
  128.9 2.8 %copy.82 = bf16[64,4,2,2,768]{4,2,3,1,0:T(2,128)(2,1)} copy(bf16[64,4,2,2,768]{4,1,0,3,2:T(4,128)(2,1)S(1)} %copy-done.4) | data formatting | bytes 3145728 | tf_op jit(solution)/shard_map/optimization_barrier | solution.py:69
  131.7 22.3 %all-to-all-done.3 = bf16[64,4,2,2,768]{4,2,3,1,0:T(2,128)(2,1)} async-done(((bf16[64,4,2,2,768]{4,2,3,1,0:T(2,128)(2,1)}), bf16[64,4,2,2,768]{4,2,3,1,0:T(2,128)(2,1)}, u32[]{:S(2)}, u32[]{:S(2)}) %all-to-all-start.3) | async-done | bytes 1572896 | tf_op jit(solution)/shard_map/all_to_all | solution.py:71
  153.9 8.6 %all-to-all-start.1 = ((bf16[64,4,2,2,768]{4,2,3,1,0:T(2,128)(2,1)}), bf16[64,4,2,2,768]{4,2,3,1,0:T(2,128)(2,1)S(1)}, u32[]{:S(2)}, u32[]{:S(2)}) async-start(bf16[64,4,2,2,768]{4,2,3,1,0:T(2,128)(2,1)} %copy.82), calls=%async_computation.1 | async-start | bytes 3145728 | tf_op jit(solution)/shard_map/all_to_all | solution.py:71
  162.6 3.3 %collective-permute-start.9 = (f32[2,256,256]{2,1,0:T(8,128)S(1)}, f32[2,256,256]{2,1,0:T(8,128)}, u32[]{:S(2)}, u32[]{:S(2)}) collective-permute-start(f32[2,256,256]{2,1,0:T(8,128)S(1)} %copy-done.6), channel_id=1, source_target_pairs={{0,64},{64,0},{128,192},{192,128},{1,65},{65,1},{129,193},{193,129... | collective-permute-start | bytes 1572872 | tf_op jit(solution)/shard_map/ppermute | solution.py:22
  171.1 10.4 %collective-permute-done.10 = f32[1,256,256]{2,1,0:T(8,128)S(1)} collective-permute-done((f32[1,256,256]{2,1,0:T(8,128)S(1)}, f32[1,256,256]{2,1,0:T(8,128)S(1)}, u32[]{:S(2)}, u32[]{:S(2)}) %collective-permute-start.10) | collective-permute-done | bytes 262176 | tf_op jit(solution)/shard_map/ppermute | solution.py:25
  182.8 9.0 %collective-permute-done.7 = f32[1,256,256]{2,1,0:T(8,128)S(1)} collective-permute-done((f32[1,256,256]{2,1,0:T(8,128)S(1)}, f32[1,256,256]{2,1,0:T(8,128)S(1)}, u32[]{:S(2)}, u32[]{:S(2)}) %collective-permute-start.7) | collective-permute-done | bytes 262176 | tf_op jit(solution)/shard_map/ppermute | solution.py:25
  192.9 4.4 %fusion.54 = f32[4,64,2,256]{3,1,2,0:T(8,128)} fusion(bf16[64,4,2,2,768]{4,2,3,1,0:T(2,128)(2,1)} %all-to-all-done.3, f32[2,768]{1,0:T(2,128)S(1)} %fusion.73, bf16[2,4,256,768]{3,2,1,0:T(8,128)(2,1)} %bitcast.185), kind=kOutput, calls=%fused_computation.52 | convolution fusion | flops 407371776 | bytes 5249024 | tf_op jit(solution)/shard_map/sajid,iabd->asjb/dot_general | solution.py:76
  197.8 3.1 %fusion.49 = f32[4,64,2,256]{3,1,2,0:T(8,128)S(1)} fusion(bf16[64,4,2,2,768]{4,2,3,1,0:T(2,128)(2,1)S(1)} %all-to-all-done.1, f32[2,768]{1,0:T(2,128)S(1)} %fusion.73, bf16[2,4,256,768]{3,2,1,0:T(8,128)(2,1)} %bitcast.186), kind=kOutput, calls=%fused_computation.51 | convolution fusion | flops 407371776 | bytes 5249024 | tf_op jit(solution)/shard_map/sajid,iabd->asjb/dot_general | solution.py:76
  200.9 6.9 %collective-permute-start = (f32[4,64,2,256]{3,1,2,0:T(8,128)S(1)}, f32[4,64,2,256]{3,1,2,0:T(8,128)S(1)}, u32[]{:S(2)}, u32[]{:S(2)}) collective-permute-start(f32[4,64,2,256]{3,1,2,0:T(8,128)S(1)} %fusion.49), channel_id=1, source_target_pairs={{0,64},{64,0},{128,192},{192,128},{1,65},{65,1},{129,193},{193,129... | collective-permute-start | bytes 1572872 | tf_op jit(solution)/shard_map/ppermute | solution.py:22
  214.1 5.2 %collective-permute-done.4 = f32[2,64,2,256]{3,1,2,0:T(8,128)S(1)} collective-permute-done((f32[2,64,2,256]{3,1,2,0:T(8,128)S(1)}, f32[2,64,2,256]{3,1,2,0:T(8,128)S(1)}, u32[]{:S(2)}, u32[]{:S(2)}) %collective-permute-start.4) | collective-permute-done | bytes 262176 | tf_op jit(solution)/shard_map/ppermute | solution.py:25
  220.6 4.3 %collective-permute-done.1 = f32[2,64,2,256]{3,1,2,0:T(8,128)S(1)} collective-permute-done((f32[2,64,2,256]{3,1,2,0:T(8,128)S(1)}, f32[2,64,2,256]{3,1,2,0:T(8,128)S(1)}, u32[]{:S(2)}, u32[]{:S(2)}) %collective-permute-start.1) | collective-permute-done | bytes 262176 | tf_op jit(solution)/shard_map/ppermute | solution.py:25
  226.1 2.9 %fusion.3 = bf16[2,4,256,768]{3,2,0,1:T(8,128)(2,1)S(1)} fusion(f32[4,2,768,256,1]{2,3,4,1,0:T(8,128)S(1)} %fusion.33, f32[2,768]{1,0:T(2,128)S(1)} %fusion.73, bf16[64,4,2,2,768]{4,2,3,1,0:T(2,128)(2,1)} %all-to-all-done.3, bf16[4,64,2,256]{3,0,2,1:T(4,128)(2,1)S(1)} %get-tuple-element.27), kind=kOutput, calls=%fused_computation.5 | convolution fusion | flops 407371776 | bytes 11278336 | tf_op jit(solution)/shard_map/asjb,sajid->iabd/dot_general | solution.py:78
  228.9 1.9 copy.95
  (72 shorter events, 26.0 us)
Async XLA Ops:
  0.6 1.7 copy-start
  2.3 21.4 %copy-start.8 = (bf16[4,64,2,256]{3,0,2,1:T(4,128)(2,1)}, bf16[4,64,2,256]{3,0,2,1:T(4,128)(2,1)S(1)}, u32[]{:S(2)}) copy-start(bf16[4,64,2,256]{3,0,2,1:T(4,128)(2,1)S(1)} %get-tuple-element.28) | copy-start | bytes 786436
  8.6 53.8 %all-to-all-start.2 = ((bf16[64,4,2,2,768]{4,2,3,1,0:T(2,128)(2,1)}), bf16[64,4,2,2,768]{4,2,3,1,0:T(2,128)(2,1)S(1)}, u32[]{:S(2)}, u32[]{:S(2)}) async-start(bf16[64,4,2,2,768]{4,2,3,1,0:T(2,128)(2,1)} %copy.86), calls=%async_computation.2 | async-start | bytes 3145728 | tf_op jit(solution)/shard_map/all_to_all | solution.py:53
  62.4 45.6 %all-to-all-start = ((bf16[64,4,2,2,768]{4,2,3,1,0:T(2,128)(2,1)}), bf16[64,4,2,2,768]{4,2,3,1,0:T(2,128)(2,1)S(1)}, u32[]{:S(2)}, u32[]{:S(2)}) async-start(bf16[64,4,2,2,768]{4,2,3,1,0:T(2,128)(2,1)} %copy.75), calls=%async_computation | async-start | bytes 3145728 | tf_op jit(solution)/shard_map/all_to_all | solution.py:53
  74.5 2.6 %copy-start.12 = (f32[16,768]{1,0:T(8,128)S(1)}, f32[16,768]{1,0:T(8,128)}, u32[]{:S(2)}) copy-start(f32[16,768]{1,0:T(8,128)} %param.11) | copy-start | bytes 147460
  74.5 2.6 %copy-start.13 = (s32[2]{0:T(128)S(1)}, s32[2]{0:T(128)}, u32[]{:S(2)}) copy-start(s32[2]{0:T(128)} %param.9) | copy-start | bytes 28
  77.3 4.3 %copy-start.10 = (bf16[4,256,256]{2,1,0:T(8,128)(2,1)S(1)}, bf16[4,256,256]{2,1,0:T(8,128)(2,1)}, u32[]{:S(2)}) copy-start(bf16[4,256,256]{2,1,0:T(8,128)(2,1)} %param.13) | copy-start | bytes 1572868
  80.3 1.2 copy-start.2
  87.2 3.1 %copy-start.3 = (bf16[64,4,2,2,768]{4,1,0,3,2:T(4,128)(2,1)S(1)}, bf16[64,4,2,2,768]{4,1,0,3,2:T(4,128)(2,1)}, u32[]{:S(2)}) copy-start(bf16[64,4,2,2,768]{4,1,0,3,2:T(4,128)(2,1)} %reshape.53) | copy-start | bytes 4718596
  90.3 26.8 %copy-start.5 = (bf16[2,2,256,768]{3,2,1,0:T(8,128)(2,1)S(1)}, bf16[2,2,256,768]{3,2,1,0:T(8,128)(2,1)}, u32[]{:S(2)}) copy-start(bf16[2,2,256,768]{3,2,1,0:T(8,128)(2,1)} %get-tuple-element.18) | copy-start | bytes 4718596
  108.0 46.0 %all-to-all-start.3 = ((bf16[64,4,2,2,768]{4,2,3,1,0:T(2,128)(2,1)}), bf16[64,4,2,2,768]{4,2,3,1,0:T(2,128)(2,1)}, u32[]{:S(2)}, u32[]{:S(2)}) async-start(bf16[64,4,2,2,768]{4,2,3,1,0:T(2,128)(2,1)} %copy.93), calls=%async_computation.3 | async-start | bytes 3145728 | tf_op jit(solution)/shard_map/all_to_all | solution.py:71
  118.7 3.1 %copy-start.11 = (bf16[4,256,256]{2,1,0:T(8,128)(2,1)S(1)}, bf16[4,256,256]{2,1,0:T(8,128)(2,1)}, u32[]{:S(2)}) copy-start(bf16[4,256,256]{2,1,0:T(8,128)(2,1)} %param.13) | copy-start | bytes 1572868
  127.4 1.5 copy-start.4
  128.9 33.6 %copy-start.6 = (f32[2,256,256]{2,1,0:T(8,128)S(1)}, f32[2,256,256]{2,1,0:T(8,128)}, u32[]{:S(2)}) copy-start(f32[2,256,256]{2,1,0:T(8,128)} %fusion.62) | copy-start | bytes 1572868
  128.9 36.9 %copy-start.7 = (f32[2,256,256]{2,1,0:T(8,128)S(1)}, f32[2,256,256]{2,1,0:T(8,128)}, u32[]{:S(2)}) copy-start(f32[2,256,256]{2,1,0:T(8,128)} %fusion.59) | copy-start | bytes 1572868
  153.9 43.9 %all-to-all-start.1 = ((bf16[64,4,2,2,768]{4,2,3,1,0:T(2,128)(2,1)}), bf16[64,4,2,2,768]{4,2,3,1,0:T(2,128)(2,1)S(1)}, u32[]{:S(2)}, u32[]{:S(2)}) async-start(bf16[64,4,2,2,768]{4,2,3,1,0:T(2,128)(2,1)} %copy.82), calls=%async_computation.1 | async-start | bytes 3145728 | tf_op jit(solution)/shard_map/all_to_all | solution.py:71
  162.6 4.9 %collective-permute-start.9 = (f32[2,256,256]{2,1,0:T(8,128)S(1)}, f32[2,256,256]{2,1,0:T(8,128)}, u32[]{:S(2)}, u32[]{:S(2)}) collective-permute-start(f32[2,256,256]{2,1,0:T(8,128)S(1)} %copy-done.6), channel_id=1, source_target_pairs={{0,64},{64,0},{128,192},{192,128},{1,65},{65,1},{129,193},{193,129... | collective-permute-start | bytes 1572872 | tf_op jit(solution)/shard_map/ppermute | solution.py:22
  165.8 3.3 %collective-permute-start.6 = (f32[2,256,256]{2,1,0:T(8,128)S(1)}, f32[2,256,256]{2,1,0:T(8,128)}, u32[]{:S(2)}, u32[]{:S(2)}) collective-permute-start(f32[2,256,256]{2,1,0:T(8,128)S(1)} %copy-done.7), channel_id=1, source_target_pairs={{0,64},{64,0},{128,192},{192,128},{1,65},{65,1},{129,193},{193,129... | collective-permute-start | bytes 1572872 | tf_op jit(solution)/shard_map/ppermute | solution.py:22
  168.5 13.0 %collective-permute-start.10 = (f32[1,256,256]{2,1,0:T(8,128)S(1)}, f32[1,256,256]{2,1,0:T(8,128)S(1)}, u32[]{:S(2)}, u32[]{:S(2)}) collective-permute-start(f32[1,256,256]{2,1,0:T(8,128)S(1)} %dynamic-slice_add_fusion), channel_id=1, source_target_pairs={{0,128},{64,192},{128,0},{192,64},{1,129},{65,193},{129,1},{193,65... | collective-permute-start | bytes 786440 | tf_op jit(solution)/shard_map/ppermute | solution.py:25
  170.1 21.8 %collective-permute-start.7 = (f32[1,256,256]{2,1,0:T(8,128)S(1)}, f32[1,256,256]{2,1,0:T(8,128)S(1)}, u32[]{:S(2)}, u32[]{:S(2)}) collective-permute-start(f32[1,256,256]{2,1,0:T(8,128)S(1)} %dynamic-slice_add_fusion.1), channel_id=1, source_target_pairs={{0,128},{64,192},{128,0},{192,64},{1,129},{65,193},{129,1},{193,65... | collective-permute-start | bytes 786440 | tf_op jit(solution)/shard_map/ppermute | solution.py:25
  181.6 26.3 %collective-permute-start.11 = (f32[1,256,256]{2,1,0:T(8,128)S(1)}, f32[1,256,256]{2,1,0:T(8,128)S(1)}, u32[]{:S(2)}, u32[]{:S(2)}) collective-permute-start(f32[1,256,256]{2,1,0:T(8,128)S(1)} %add.69), channel_id=1, source_target_pairs={{0,64},{64,0},{128,192},{192,128},{1,65},{65,1},{129,193},{193,129... | collective-permute-start | bytes 786440 | tf_op jit(solution)/shard_map/ppermute | solution.py:26
  191.9 16.0 %collective-permute-start.8 = (f32[1,256,256]{2,1,0:T(8,128)S(1)}, f32[1,256,256]{2,1,0:T(8,128)}, u32[]{:S(2)}, u32[]{:S(2)}) collective-permute-start(f32[1,256,256]{2,1,0:T(8,128)S(1)} %add.67), channel_id=1, source_target_pairs={{0,64},{64,0},{128,192},{192,128},{1,65},{65,1},{129,193},{193,129... | collective-permute-start | bytes 786440 | tf_op jit(solution)/shard_map/ppermute | solution.py:26
  197.3 12.7 %collective-permute-start.3 = (f32[4,64,2,256]{3,1,2,0:T(8,128)}, f32[4,64,2,256]{3,1,2,0:T(8,128)}, u32[]{:S(2)}, u32[]{:S(2)}) collective-permute-start(f32[4,64,2,256]{3,1,2,0:T(8,128)} %fusion.54), channel_id=1, source_target_pairs={{0,64},{64,0},{128,192},{192,128},{1,65},{65,1},{129,193},{193,129... | collective-permute-start | bytes 1572872 | tf_op jit(solution)/shard_map/ppermute | solution.py:22
  200.9 11.7 %collective-permute-start = (f32[4,64,2,256]{3,1,2,0:T(8,128)S(1)}, f32[4,64,2,256]{3,1,2,0:T(8,128)S(1)}, u32[]{:S(2)}, u32[]{:S(2)}) collective-permute-start(f32[4,64,2,256]{3,1,2,0:T(8,128)S(1)} %fusion.49), channel_id=1, source_target_pairs={{0,64},{64,0},{128,192},{192,128},{1,65},{65,1},{129,193},{193,129... | collective-permute-start | bytes 1572872 | tf_op jit(solution)/shard_map/ppermute | solution.py:22
  208.9 4.1 %copy-start.9 = (bf16[4,64,2,256]{3,0,2,1:T(4,128)(2,1)S(1)}, bf16[4,64,2,256]{3,0,2,1:T(4,128)(2,1)}, u32[]{:S(2)}) copy-start(bf16[4,64,2,256]{3,0,2,1:T(4,128)(2,1)} %copy-done.8) | copy-start | bytes 786436
  211.2 8.0 %collective-permute-start.4 = (f32[2,64,2,256]{3,1,2,0:T(8,128)S(1)}, f32[2,64,2,256]{3,1,2,0:T(8,128)S(1)}, u32[]{:S(2)}, u32[]{:S(2)}) collective-permute-start(f32[2,64,2,256]{3,1,2,0:T(8,128)S(1)} %dynamic-slice_bitcast_fusion), channel_id=1, source_target_pairs={{0,128},{64,192},{128,0},{192,64},{1,129},{65,193},{129,1},{193,65... | collective-permute-start | bytes 786440 | tf_op jit(solution)/shard_map/ppermute | solution.py:25
  212.7 12.1 %collective-permute-start.1 = (f32[2,64,2,256]{3,1,2,0:T(8,128)S(1)}, f32[2,64,2,256]{3,1,2,0:T(8,128)S(1)}, u32[]{:S(2)}, u32[]{:S(2)}) collective-permute-start(f32[2,64,2,256]{3,1,2,0:T(8,128)S(1)} %dynamic-slice_bitcast_fusion.1), channel_id=1, source_target_pairs={{0,128},{64,192},{128,0},{192,64},{1,129},{65,193},{129,1},{193,65... | collective-permute-start | bytes 786440 | tf_op jit(solution)/shard_map/ppermute | solution.py:25
  219.3 11.5 %collective-permute-start.5 = (f32[2,64,2,256]{3,1,2,0:T(8,128)S(1)}, f32[2,64,2,256]{3,1,2,0:T(8,128)S(1)}, u32[]{:S(2)}, u32[]{:S(2)}) collective-permute-start(f32[2,64,2,256]{3,1,2,0:T(8,128)S(1)} %fusion.86), channel_id=1, source_target_pairs={{0,64},{64,0},{128,192},{192,128},{1,65},{65,1},{129,193},{193,129... | collective-permute-start | bytes 786440 | tf_op jit(solution)/shard_map/ppermute | solution.py:26
  224.9 6.0 %collective-permute-start.2 = (f32[2,64,2,256]{3,1,2,0:T(8,128)S(1)}, f32[2,64,2,256]{3,1,2,0:T(8,128)S(1)}, u32[]{:S(2)}, u32[]{:S(2)}) collective-permute-start(f32[2,64,2,256]{3,1,2,0:T(8,128)S(1)} %fusion.85), channel_id=1, source_target_pairs={{0,64},{64,0},{128,192},{192,128},{1,65},{65,1},{129,193},{193,129... | collective-permute-start | bytes 786440 | tf_op jit(solution)/shard_map/ppermute | solution.py:26
  230.9 2.0 copy-start.1
where the time goes:
time: 234 us; the launch traced here: 233 us
  waiting for transfers between devices  101 us (43%)
  starting transfers between devices  59.5 us (25%)
  local copies, waits for them, and re-layouts  33.5 us (14%)
  matrix products  32 us (14%)
  other arithmetic  5.68 us (2%)
    all_to_all x2, waiting for transfers between devices, on_device(): recv1.append(lax.all_to_all(mixed, 'seq', 0, 0, tiled=True))  48.1 us
    ppermute x4, waiting for transfers between devices, dp_sum_halves(): mine = mine + lax.ppermute(mine, 'dp', [(i, i ^ 2) for i in range(n_dp)])  28.9 us
    all_to_all x2, starting transfers between devices, on_device(): recv1.append(lax.all_to_all(mixed, 'seq', 0, 0, tiled=True))  23.5 us
    all_to_all x2, waiting for transfers between devices, on_device(): recv2.append(lax.all_to_all(send, 'seq', 0, 0, tiled=True))  22.8 us
    all_to_all x2, starting transfers between devices, on_device(): recv2.append(lax.all_to_all(send, 'seq', 0, 0, tiled=True))  17.7 us
    ppermute x4, starting transfers between devices, dp_sum_halves(): x = x + lax.ppermute(x, 'dp', [(i, i ^ 1) for i in range(n_dp)])  10.3 us
    unnamed x32, local copies, waits for them, and re-layouts  8.07 us
    reshape x2, local copies, waits for them, and re-layouts, on_device(): send = send.reshape(n_seq, own, per, images, width)  7.74 us
  transfers between devices with their start and end apart: 16, of which 9 were waited for; matrix products, arithmetic and copies ran while one was open for 26% of the time, Pallas kernels for 0%

commit v1 on v0

--- a/solution.py
+++ b/solution.py
@@ -15,18 +15,20 @@
     return x
 
 
-def dp_sum_halves(x, n_dp):
+def dp_sum_halves(x, n_dp, hold=None):
     if n_dp != 4 or x.shape[0] % 2:
-        return dp_sum(x, n_dp)
+        return dp_sum(x, n_dp), hold
     core = lax.axis_index("dp") % 2
     x = x + lax.ppermute(x, "dp", [(i, i ^ 1) for i in range(n_dp)])
     halves = x.reshape((2, x.shape[0] // 2) + x.shape[1:])
     mine = lax.dynamic_index_in_dim(halves, core, 0, keepdims=False)
+    if hold is not None:
+        mine, hold = lax.optimization_barrier((mine, hold))
     mine = mine + lax.ppermute(mine, "dp", [(i, i ^ 2) for i in range(n_dp)])
     other = lax.ppermute(mine, "dp", [(i, i ^ 1) for i in range(n_dp)])
     first = jnp.where(core == 0, mine, other)
     second = jnp.where(core == 0, other, mine)
-    return jnp.concatenate([first, second], axis=0)
+    return jnp.concatenate([first, second], axis=0), hold
 
 
 def on_device(inputs, cotangent, control, table_in, table_out, factor_one, second_block_factor, n_dp):
@@ -67,16 +69,21 @@
         send = jnp.einsum("jpa,jpid->ajid", f2, value_gradient, preferred_element_type=f32).astype(bf16)
         send = send.reshape(n_seq, own, per, images, width)
         part, send = lax.optimization_barrier((part, send))
-        sfg.append(dp_sum_halves(part, n_dp))
+        sfg.append(dp_sum_halves(part, n_dp)[0])
         recv2.append(lax.all_to_all(send, "seq", 0, 0, tiled=True))
 
     grad_one = []
     back_sum = None
     for k in range(CHUNKS):
-        part = jnp.einsum("sajid,iabd->asjb", recv2[k], scaled, preferred_element_type=f32)
-        grad_one.append(dp_sum_halves(part, n_dp))
+        got = recv2[k]
+        part = jnp.einsum("sajid,iabd->asjb", got, scaled, preferred_element_type=f32)
+        if k == CHUNKS - 1:
+            reduced, got = dp_sum_halves(part, n_dp, hold=got)
+        else:
+            reduced, _ = dp_sum_halves(part, n_dp)
+        grad_one.append(reduced)
         term = jnp.einsum(
-            "asjb,sajid->iabd", f1[:, :, k * per:(k + 1) * per, :], recv2[k], preferred_element_type=f32
+            "asjb,sajid->iabd", f1[:, :, k * per:(k + 1) * per, :], got, preferred_element_type=f32
         )
         back_sum = term if back_sum is None else back_sum + term
     grad_one = jnp.concatenate(grad_one, axis=2).reshape(own, blocks, blocks)

time: 234 us -> 234 us (level)
  no operation moved by 1% of the time
where the time goes in v1:
time: 234 us; the launch traced here: 233 us
  waiting for transfers between devices  101 us (43%)
  starting transfers between devices  59.5 us (25%)
  local copies, waits for them, and re-layouts  33.5 us (14%)
  matrix products  31.8 us (14%)
  other arithmetic  5.68 us (2%)
    all_to_all x2, waiting for transfers between devices, on_device(): recv1.append(lax.all_to_all(mixed, 'seq', 0, 0, tiled=True))  48.1 us
    ppermute x4, waiting for transfers between devices, dp_sum_halves(): mine = mine + lax.ppermute(mine, 'dp', [(i, i ^ 2) for i in range(n_dp)])  28.9 us
    all_to_all x2, starting transfers between devices, on_device(): recv1.append(lax.all_to_all(mixed, 'seq', 0, 0, tiled=True))  23.5 us
    all_to_all x2, waiting for transfers between devices, on_device(): recv2.append(lax.all_to_all(send, 'seq', 0, 0, tiled=True))  22.7 us
    all_to_all x2, starting transfers between devices, on_device(): recv2.append(lax.all_to_all(send, 'seq', 0, 0, tiled=True))  17.7 us
    ppermute x4, starting transfers between devices, dp_sum_halves(): x = x + lax.ppermute(x, 'dp', [(i, i ^ 1) for i in range(n_dp)])  10.3 us
    unnamed x32, local copies, waits for them, and re-layouts  8.07 us
    reshape x2, local copies, waits for them, and re-layouts, on_device(): send = send.reshape(n_seq, own, per, images, width)  7.74 us
  transfers between devices with their start and end apart: 16, of which 9 were waited for; matrix products, arithmetic and copies ran while one was open for 26% of the time, Pallas kernels for 0%

profile of v1, /device:TPU:1, one launch (start us, length us, event | category | flops | bytes accessed | tf_op | source)
XLA Modules:
  0.0 232.6 jit_solution(2035310051979416554)
XLA Ops:
  3.2 2.6 %fusion.35 = bf16[64,4,2,2,768]{4,0,2,3,1:T(8,128)(2,1)S(1)} fusion(bf16[4,64,2,256]{3,0,2,1:T(4,128)(2,1)S(1)} %get-tuple-element.31, f32[2,768]{1,0:T(2,128)S(1)} %fusion.73, bf16[2,4,256,768]{3,2,1,0:T(8,128)(2,1)} %bitcast.180), kind=kOutput, calls=%fused_computation.41 | convolution fusion | flops 408158208 | bytes 4986880 | tf_op jit(solution)/shard_map/asjb,iabd->sajid/dot_general | solution.py:52
  5.8 2.8 %copy.86 = bf16[64,4,2,2,768]{4,2,3,1,0:T(2,128)(2,1)} copy(bf16[64,4,2,2,768]{4,0,2,3,1:T(8,128)(2,1)S(1)} %fusion.35) | data formatting | bytes 3145728 | tf_op jit(solution)/shard_map/convert_element_type | solution.py:54
  8.6 15.1 %all-to-all-start.2 = ((bf16[64,4,2,2,768]{4,2,3,1,0:T(2,128)(2,1)}), bf16[64,4,2,2,768]{4,2,3,1,0:T(2,128)(2,1)S(1)}, u32[]{:S(2)}, u32[]{:S(2)}) async-start(bf16[64,4,2,2,768]{4,2,3,1,0:T(2,128)(2,1)} %copy.86), calls=%async_computation.2 | async-start | bytes 3145728 | tf_op jit(solution)/shard_map/all_to_all | solution.py:55
  23.7 2.6 %fusion.38 = bf16[64,4,2,2,768]{4,0,2,3,1:T(8,128)(2,1)S(1)} fusion(bf16[4,64,2,256]{3,0,2,1:T(4,128)(2,1)S(1)} %get-tuple-element.32, f32[2,768]{1,0:T(2,128)S(1)} %fusion.73, bf16[2,4,256,768]{3,2,1,0:T(8,128)(2,1)} %bitcast.181), kind=kOutput, calls=%fused_computation.42 | convolution fusion | flops 408158208 | bytes 4986880 | tf_op jit(solution)/shard_map/asjb,iabd->sajid/dot_general | solution.py:52
  26.4 2.8 %copy.75 = bf16[64,4,2,2,768]{4,2,3,1,0:T(2,128)(2,1)} copy(bf16[64,4,2,2,768]{4,0,2,3,1:T(8,128)(2,1)S(1)} %fusion.38) | data formatting | bytes 3145728 | tf_op jit(solution)/shard_map/convert_element_type | solution.py:54
  29.2 33.2 %all-to-all-done.2 = bf16[64,4,2,2,768]{4,2,3,1,0:T(2,128)(2,1)S(1)} async-done(((bf16[64,4,2,2,768]{4,2,3,1,0:T(2,128)(2,1)}), bf16[64,4,2,2,768]{4,2,3,1,0:T(2,128)(2,1)S(1)}, u32[]{:S(2)}, u32[]{:S(2)}) %all-to-all-start.2) | async-done | bytes 1572896 | tf_op jit(solution)/shard_map/all_to_all | solution.py:55
  62.4 8.3 %all-to-all-start = ((bf16[64,4,2,2,768]{4,2,3,1,0:T(2,128)(2,1)}), bf16[64,4,2,2,768]{4,2,3,1,0:T(2,128)(2,1)S(1)}, u32[]{:S(2)}, u32[]{:S(2)}) async-start(bf16[64,4,2,2,768]{4,2,3,1,0:T(2,128)(2,1)} %copy.75), calls=%async_computation | async-start | bytes 3145728 | tf_op jit(solution)/shard_map/all_to_all | solution.py:55
  70.7 3.8 %fusion.77 = (bf16[2,2,256,768]{3,2,1,0:T(8,128)(2,1)}, bf16[2,2,256,768]{3,2,1,0:T(8,128)(2,1)}) fusion(bf16[2,4,256,768]{3,2,1,0:T(8,128)(2,1)} %bitcast.174), kind=kLoop, calls=%fused_computation.84 | loop fusion | bytes 6291456 | tf_op jit(solution)/shard_map/slice | solution.py:64
  74.5 2.6 %copy.128 = bf16[2,2,256,768]{2,3,0,1:T(8,128)(2,1)} copy(bf16[2,2,256,768]{3,2,1,0:T(8,128)(2,1)} %get-tuple-element.21) | data formatting | bytes 3145728
  77.3 3.0 %fusion.13 = bf16[2,256,2,768]{1,3,2,0:T(8,128)(2,1)S(1)} fusion(bf16[2,2,256,768]{2,3,0,1:T(8,128)(2,1)} %copy.128, f32[2,768]{1,0:T(2,128)S(1)} %fusion.74, bf16[256,2,2,768]{3,1,2,0:T(2,128)(2,1)S(1)} %bitcast.171, bf16[4,256,256]{2,1,0:T(8,128)(2,1)} %param.13), kind=kOutput, calls=%fused_computation.17 | convolution fusion | flops 411303936 | bytes 4986880 | tf_op jit(solution)/shard_map/jpa,ajid->jpid/dot_general | solution.py:62
  81.5 1.8 fusion.42
  83.3 3.9 %reshape.53 = bf16[64,4,2,2,768]{4,1,0,3,2:T(4,128)(2,1)} reshape(bf16[256,2,2,768]{3,0,2,1:T(8,128)(2,1)} %fusion.42) | data formatting | bytes 3145728 | tf_op jit(solution)/shard_map/reshape | solution.py:70
  87.2 3.1 %fusion.62 = f32[2,256,256]{2,1,0:T(8,128)} fusion(bf16[2,256,2,768]{1,3,2,0:T(8,128)(2,1)} %copy-done.2, bf16[256,2,2,768]{3,1,2,0:T(2,128)(2,1)S(1)} %bitcast.172), kind=kOutput, calls=%fused_computation.54 | convolution fusion | flops 402653184 | bytes 3670016 | tf_op jit(solution)/shard_map/jpid,ajid->jpa/dot_general | solution.py:68
  90.3 2.8 %copy.93 = bf16[64,4,2,2,768]{4,3,2,1,0:T(2,128)(2,1)} copy(bf16[64,4,2,2,768]{4,1,0,3,2:T(4,128)(2,1)S(1)} %copy-done.3) | data formatting | bytes 3145728 | tf_op jit(solution)/shard_map/optimization_barrier | solution.py:71
  93.0 14.9 %all-to-all-done = bf16[64,4,2,2,768]{4,2,3,1,0:T(2,128)(2,1)S(1)} async-done(((bf16[64,4,2,2,768]{4,2,3,1,0:T(2,128)(2,1)}), bf16[64,4,2,2,768]{4,2,3,1,0:T(2,128)(2,1)S(1)}, u32[]{:S(2)}, u32[]{:S(2)}) %all-to-all-start) | async-done | bytes 1572896 | tf_op jit(solution)/shard_map/all_to_all | solution.py:55
  108.0 9.1 %all-to-all-start.3 = ((bf16[64,4,2,2,768]{4,3,2,1,0:T(2,128)(2,1)}), bf16[64,4,2,2,768]{4,3,2,1,0:T(2,128)(2,1)}, u32[]{:S(2)}, u32[]{:S(2)}) async-start(bf16[64,4,2,2,768]{4,3,2,1,0:T(2,128)(2,1)} %copy.93), calls=%async_computation.3 | async-start | bytes 3145728 | tf_op jit(solution)/shard_map/all_to_all | solution.py:73
  118.7 3.1 %fusion.23 = bf16[2,256,2,768]{1,3,2,0:T(8,128)(2,1)S(1)} fusion(bf16[2,2,256,768]{2,3,0,1:T(8,128)(2,1)} %copy.126, f32[2,768]{1,0:T(2,128)S(1)} %fusion.74, bf16[256,2,2,768]{3,1,2,0:T(2,128)(2,1)S(1)} %bitcast.169, bf16[4,256,256]{2,1,0:T(8,128)(2,1)} %param.13), kind=kOutput, calls=%fused_computation.30 | convolution fusion | flops 411303936 | bytes 4986880 | tf_op jit(solution)/shard_map/jpa,ajid->jpid/dot_general | solution.py:62
  121.7 1.8 fusion.41
  123.5 3.9 %reshape.51 = bf16[64,4,2,2,768]{4,1,0,3,2:T(4,128)(2,1)} reshape(bf16[256,2,2,768]{3,0,2,1:T(8,128)(2,1)} %fusion.41) | data formatting | bytes 3145728 | tf_op jit(solution)/shard_map/reshape | solution.py:70
  128.9 2.8 %copy.82 = bf16[64,4,2,2,768]{4,2,3,1,0:T(2,128)(2,1)} copy(bf16[64,4,2,2,768]{4,1,0,3,2:T(4,128)(2,1)S(1)} %copy-done.4) | data formatting | bytes 3145728 | tf_op jit(solution)/shard_map/optimization_barrier | solution.py:71
  131.7 22.3 %all-to-all-done.3 = bf16[64,4,2,2,768]{4,3,2,1,0:T(2,128)(2,1)} async-done(((bf16[64,4,2,2,768]{4,3,2,1,0:T(2,128)(2,1)}), bf16[64,4,2,2,768]{4,3,2,1,0:T(2,128)(2,1)}, u32[]{:S(2)}, u32[]{:S(2)}) %all-to-all-start.3) | async-done | bytes 1572896 | tf_op jit(solution)/shard_map/all_to_all | solution.py:73
  153.9 8.6 %all-to-all-start.1 = ((bf16[64,4,2,2,768]{4,2,3,1,0:T(2,128)(2,1)}), bf16[64,4,2,2,768]{4,2,3,1,0:T(2,128)(2,1)S(1)}, u32[]{:S(2)}, u32[]{:S(2)}) async-start(bf16[64,4,2,2,768]{4,2,3,1,0:T(2,128)(2,1)} %copy.82), calls=%async_computation.1 | async-start | bytes 3145728 | tf_op jit(solution)/shard_map/all_to_all | solution.py:73
  162.6 3.3 %collective-permute-start.9 = (f32[2,256,256]{2,1,0:T(8,128)S(1)}, f32[2,256,256]{2,1,0:T(8,128)}, u32[]{:S(2)}, u32[]{:S(2)}) collective-permute-start(f32[2,256,256]{2,1,0:T(8,128)S(1)} %copy-done.6), channel_id=1, source_target_pairs={{0,64},{64,0},{128,192},{192,128},{1,65},{65,1},{129,193},{193,129... | collective-permute-start | bytes 1572872 | tf_op jit(solution)/shard_map/ppermute | solution.py:22
  171.1 10.4 %collective-permute-done.10 = f32[1,256,256]{2,1,0:T(8,128)S(1)} collective-permute-done((f32[1,256,256]{2,1,0:T(8,128)S(1)}, f32[1,256,256]{2,1,0:T(8,128)S(1)}, u32[]{:S(2)}, u32[]{:S(2)}) %collective-permute-start.10) | collective-permute-done | bytes 262176 | tf_op jit(solution)/shard_map/ppermute | solution.py:27
  182.8 9.0 %collective-permute-done.7 = f32[1,256,256]{2,1,0:T(8,128)S(1)} collective-permute-done((f32[1,256,256]{2,1,0:T(8,128)S(1)}, f32[1,256,256]{2,1,0:T(8,128)S(1)}, u32[]{:S(2)}, u32[]{:S(2)}) %collective-permute-start.7) | collective-permute-done | bytes 262176 | tf_op jit(solution)/shard_map/ppermute | solution.py:27
  192.9 4.5 %fusion.49 = f32[4,64,2,256]{3,1,2,0:T(8,128)} fusion(bf16[64,4,2,2,768]{4,3,2,1,0:T(2,128)(2,1)} %all-to-all-done.3, f32[2,768]{1,0:T(2,128)S(1)} %fusion.73, bf16[2,4,256,768]{3,2,1,0:T(8,128)(2,1)} %bitcast.182), kind=kOutput, calls=%fused_computation.51 | convolution fusion | flops 407371776 | bytes 5249024 | tf_op jit(solution)/shard_map/sajid,iabd->asjb/dot_general | solution.py:79
  197.8 3.1 %fusion.54 = f32[4,64,2,256]{3,1,2,0:T(8,128)S(1)} fusion(bf16[64,4,2,2,768]{4,2,3,1,0:T(2,128)(2,1)S(1)} %all-to-all-done.1, f32[2,768]{1,0:T(2,128)S(1)} %fusion.73, bf16[2,4,256,768]{3,2,1,0:T(8,128)(2,1)} %bitcast.183), kind=kOutput, calls=%fused_computation.52 | convolution fusion | flops 407371776 | bytes 5249024 | tf_op jit(solution)/shard_map/sajid,iabd->asjb/dot_general | solution.py:79
  200.9 6.9 %collective-permute-start.1 = (f32[4,64,2,256]{3,1,2,0:T(8,128)S(1)}, f32[4,64,2,256]{3,1,2,0:T(8,128)S(1)}, u32[]{:S(2)}, u32[]{:S(2)}) collective-permute-start(f32[4,64,2,256]{3,1,2,0:T(8,128)S(1)} %fusion.54), channel_id=1, source_target_pairs={{0,64},{64,0},{128,192},{192,128},{1,65},{65,1},{129,193},{193,129... | collective-permute-start | bytes 1572872 | tf_op jit(solution)/shard_map/ppermute | solution.py:22
  214.1 5.2 %collective-permute-done.4 = f32[2,64,2,256]{3,1,2,0:T(8,128)S(1)} collective-permute-done((f32[2,64,2,256]{3,1,2,0:T(8,128)S(1)}, f32[2,64,2,256]{3,1,2,0:T(8,128)S(1)}, u32[]{:S(2)}, u32[]{:S(2)}) %collective-permute-start.4) | collective-permute-done | bytes 262176 | tf_op jit(solution)/shard_map/ppermute | solution.py:27
  220.6 4.3 %collective-permute-done.2 = f32[2,64,2,256]{3,1,2,0:T(8,128)S(1)} collective-permute-done((f32[2,64,2,256]{3,1,2,0:T(8,128)S(1)}, f32[2,64,2,256]{3,1,2,0:T(8,128)S(1)}, u32[]{:S(2)}, u32[]{:S(2)}) %collective-permute-start.2) | collective-permute-done | bytes 262176 | tf_op jit(solution)/shard_map/ppermute | solution.py:27
  226.1 2.6 %fusion.3 = bf16[2,4,256,768]{3,2,0,1:T(8,128)(2,1)S(1)} fusion(f32[4,2,768,256,1]{2,3,4,1,0:T(8,128)S(1)} %fusion.33, f32[2,768]{1,0:T(2,128)S(1)} %fusion.73, bf16[64,4,2,2,768]{4,3,2,1,0:T(2,128)(2,1)} %all-to-all-done.3, bf16[4,64,2,256]{3,0,2,1:T(4,128)(2,1)S(1)} %get-tuple-element.31), kind=kOutput, calls=%fused_computation.5 | convolution fusion | flops 407371776 | bytes 11278336 | tf_op jit(solution)/shard_map/asjb,sajid->iabd/dot_general | solution.py:85
  228.6 1.9 copy.96
  (72 shorter events, 25.9 us)
Async XLA Ops:
  0.6 1.7 copy-start
  2.3 21.4 %copy-start.8 = (bf16[4,64,2,256]{3,0,2,1:T(4,128)(2,1)}, bf16[4,64,2,256]{3,0,2,1:T(4,128)(2,1)S(1)}, u32[]{:S(2)}) copy-start(bf16[4,64,2,256]{3,0,2,1:T(4,128)(2,1)S(1)} %get-tuple-element.32) | copy-start | bytes 786436
  8.6 53.8 %all-to-all-start.2 = ((bf16[64,4,2,2,768]{4,2,3,1,0:T(2,128)(2,1)}), bf16[64,4,2,2,768]{4,2,3,1,0:T(2,128)(2,1)S(1)}, u32[]{:S(2)}, u32[]{:S(2)}) async-start(bf16[64,4,2,2,768]{4,2,3,1,0:T(2,128)(2,1)} %copy.86), calls=%async_computation.2 | async-start | bytes 3145728 | tf_op jit(solution)/shard_map/all_to_all | solution.py:55
  62.4 45.6 %all-to-all-start = ((bf16[64,4,2,2,768]{4,2,3,1,0:T(2,128)(2,1)}), bf16[64,4,2,2,768]{4,2,3,1,0:T(2,128)(2,1)S(1)}, u32[]{:S(2)}, u32[]{:S(2)}) async-start(bf16[64,4,2,2,768]{4,2,3,1,0:T(2,128)(2,1)} %copy.75), calls=%async_computation | async-start | bytes 3145728 | tf_op jit(solution)/shard_map/all_to_all | solution.py:55
  74.5 2.6 %copy-start.12 = (f32[16,768]{1,0:T(8,128)S(1)}, f32[16,768]{1,0:T(8,128)}, u32[]{:S(2)}) copy-start(f32[16,768]{1,0:T(8,128)} %param.11) | copy-start | bytes 147460
  74.5 2.6 %copy-start.13 = (s32[2]{0:T(128)S(1)}, s32[2]{0:T(128)}, u32[]{:S(2)}) copy-start(s32[2]{0:T(128)} %param.9) | copy-start | bytes 28
  77.3 4.3 %copy-start.10 = (bf16[4,256,256]{2,1,0:T(8,128)(2,1)S(1)}, bf16[4,256,256]{2,1,0:T(8,128)(2,1)}, u32[]{:S(2)}) copy-start(bf16[4,256,256]{2,1,0:T(8,128)(2,1)} %param.13) | copy-start | bytes 1572868
  80.3 1.2 copy-start.2
  87.2 3.1 %copy-start.3 = (bf16[64,4,2,2,768]{4,1,0,3,2:T(4,128)(2,1)S(1)}, bf16[64,4,2,2,768]{4,1,0,3,2:T(4,128)(2,1)}, u32[]{:S(2)}) copy-start(bf16[64,4,2,2,768]{4,1,0,3,2:T(4,128)(2,1)} %reshape.53) | copy-start | bytes 4718596
  90.3 26.8 %copy-start.5 = (bf16[2,2,256,768]{3,2,1,0:T(8,128)(2,1)S(1)}, bf16[2,2,256,768]{3,2,1,0:T(8,128)(2,1)}, u32[]{:S(2)}) copy-start(bf16[2,2,256,768]{3,2,1,0:T(8,128)(2,1)} %get-tuple-element.22) | copy-start | bytes 4718596
  108.0 46.0 %all-to-all-start.3 = ((bf16[64,4,2,2,768]{4,3,2,1,0:T(2,128)(2,1)}), bf16[64,4,2,2,768]{4,3,2,1,0:T(2,128)(2,1)}, u32[]{:S(2)}, u32[]{:S(2)}) async-start(bf16[64,4,2,2,768]{4,3,2,1,0:T(2,128)(2,1)} %copy.93), calls=%async_computation.3 | async-start | bytes 3145728 | tf_op jit(solution)/shard_map/all_to_all | solution.py:73
  118.7 3.1 %copy-start.11 = (bf16[4,256,256]{2,1,0:T(8,128)(2,1)S(1)}, bf16[4,256,256]{2,1,0:T(8,128)(2,1)}, u32[]{:S(2)}) copy-start(bf16[4,256,256]{2,1,0:T(8,128)(2,1)} %param.13) | copy-start | bytes 1572868
  127.4 1.5 copy-start.4
  128.9 33.6 %copy-start.6 = (f32[2,256,256]{2,1,0:T(8,128)S(1)}, f32[2,256,256]{2,1,0:T(8,128)}, u32[]{:S(2)}) copy-start(f32[2,256,256]{2,1,0:T(8,128)} %fusion.62) | copy-start | bytes 1572868
  128.9 36.9 %copy-start.7 = (f32[2,256,256]{2,1,0:T(8,128)S(1)}, f32[2,256,256]{2,1,0:T(8,128)}, u32[]{:S(2)}) copy-start(f32[2,256,256]{2,1,0:T(8,128)} %fusion.59) | copy-start | bytes 1572868
  153.9 43.9 %all-to-all-start.1 = ((bf16[64,4,2,2,768]{4,2,3,1,0:T(2,128)(2,1)}), bf16[64,4,2,2,768]{4,2,3,1,0:T(2,128)(2,1)S(1)}, u32[]{:S(2)}, u32[]{:S(2)}) async-start(bf16[64,4,2,2,768]{4,2,3,1,0:T(2,128)(2,1)} %copy.82), calls=%async_computation.1 | async-start | bytes 3145728 | tf_op jit(solution)/shard_map/all_to_all | solution.py:73
  162.6 4.9 %collective-permute-start.9 = (f32[2,256,256]{2,1,0:T(8,128)S(1)}, f32[2,256,256]{2,1,0:T(8,128)}, u32[]{:S(2)}, u32[]{:S(2)}) collective-permute-start(f32[2,256,256]{2,1,0:T(8,128)S(1)} %copy-done.6), channel_id=1, source_target_pairs={{0,64},{64,0},{128,192},{192,128},{1,65},{65,1},{129,193},{193,129... | collective-permute-start | bytes 1572872 | tf_op jit(solution)/shard_map/ppermute | solution.py:22
  165.8 3.3 %collective-permute-start.6 = (f32[2,256,256]{2,1,0:T(8,128)S(1)}, f32[2,256,256]{2,1,0:T(8,128)}, u32[]{:S(2)}, u32[]{:S(2)}) collective-permute-start(f32[2,256,256]{2,1,0:T(8,128)S(1)} %copy-done.7), channel_id=1, source_target_pairs={{0,64},{64,0},{128,192},{192,128},{1,65},{65,1},{129,193},{193,129... | collective-permute-start | bytes 1572872 | tf_op jit(solution)/shard_map/ppermute | solution.py:22
  168.5 13.0 %collective-permute-start.10 = (f32[1,256,256]{2,1,0:T(8,128)S(1)}, f32[1,256,256]{2,1,0:T(8,128)S(1)}, u32[]{:S(2)}, u32[]{:S(2)}) collective-permute-start(f32[1,256,256]{2,1,0:T(8,128)S(1)} %dynamic-slice_add_fusion), channel_id=1, source_target_pairs={{0,128},{64,192},{128,0},{192,64},{1,129},{65,193},{129,1},{193,65... | collective-permute-start | bytes 786440 | tf_op jit(solution)/shard_map/ppermute | solution.py:27
  170.1 21.8 %collective-permute-start.7 = (f32[1,256,256]{2,1,0:T(8,128)S(1)}, f32[1,256,256]{2,1,0:T(8,128)S(1)}, u32[]{:S(2)}, u32[]{:S(2)}) collective-permute-start(f32[1,256,256]{2,1,0:T(8,128)S(1)} %dynamic-slice_add_fusion.1), channel_id=1, source_target_pairs={{0,128},{64,192},{128,0},{192,64},{1,129},{65,193},{129,1},{193,65... | collective-permute-start | bytes 786440 | tf_op jit(solution)/shard_map/ppermute | solution.py:27
  181.6 26.3 %collective-permute-start.11 = (f32[1,256,256]{2,1,0:T(8,128)S(1)}, f32[1,256,256]{2,1,0:T(8,128)S(1)}, u32[]{:S(2)}, u32[]{:S(2)}) collective-permute-start(f32[1,256,256]{2,1,0:T(8,128)S(1)} %add.69), channel_id=1, source_target_pairs={{0,64},{64,0},{128,192},{192,128},{1,65},{65,1},{129,193},{193,129... | collective-permute-start | bytes 786440 | tf_op jit(solution)/shard_map/ppermute | solution.py:28
  191.9 16.0 %collective-permute-start.8 = (f32[1,256,256]{2,1,0:T(8,128)S(1)}, f32[1,256,256]{2,1,0:T(8,128)}, u32[]{:S(2)}, u32[]{:S(2)}) collective-permute-start(f32[1,256,256]{2,1,0:T(8,128)S(1)} %add.67), channel_id=1, source_target_pairs={{0,64},{64,0},{128,192},{192,128},{1,65},{65,1},{129,193},{193,129... | collective-permute-start | bytes 786440 | tf_op jit(solution)/shard_map/ppermute | solution.py:28
  197.4 12.5 %collective-permute-start = (f32[4,64,2,256]{3,1,2,0:T(8,128)}, f32[4,64,2,256]{3,1,2,0:T(8,128)}, u32[]{:S(2)}, u32[]{:S(2)}) collective-permute-start(f32[4,64,2,256]{3,1,2,0:T(8,128)} %fusion.49), channel_id=1, source_target_pairs={{0,64},{64,0},{128,192},{192,128},{1,65},{65,1},{129,193},{193,129... | collective-permute-start | bytes 1572872 | tf_op jit(solution)/shard_map/ppermute | solution.py:22
  200.9 11.7 %collective-permute-start.1 = (f32[4,64,2,256]{3,1,2,0:T(8,128)S(1)}, f32[4,64,2,256]{3,1,2,0:T(8,128)S(1)}, u32[]{:S(2)}, u32[]{:S(2)}) collective-permute-start(f32[4,64,2,256]{3,1,2,0:T(8,128)S(1)} %fusion.54), channel_id=1, source_target_pairs={{0,64},{64,0},{128,192},{192,128},{1,65},{65,1},{129,193},{193,129... | collective-permute-start | bytes 1572872 | tf_op jit(solution)/shard_map/ppermute | solution.py:22
  208.9 4.1 %copy-start.9 = (bf16[4,64,2,256]{3,0,2,1:T(4,128)(2,1)S(1)}, bf16[4,64,2,256]{3,0,2,1:T(4,128)(2,1)}, u32[]{:S(2)}) copy-start(bf16[4,64,2,256]{3,0,2,1:T(4,128)(2,1)} %copy-done.8) | copy-start | bytes 786436
  211.2 8.0 %collective-permute-start.4 = (f32[2,64,2,256]{3,1,2,0:T(8,128)S(1)}, f32[2,64,2,256]{3,1,2,0:T(8,128)S(1)}, u32[]{:S(2)}, u32[]{:S(2)}) collective-permute-start(f32[2,64,2,256]{3,1,2,0:T(8,128)S(1)} %dynamic-slice_bitcast_fusion.1), channel_id=1, source_target_pairs={{0,128},{64,192},{128,0},{192,64},{1,129},{65,193},{129,1},{193,65... | collective-permute-start | bytes 786440 | tf_op jit(solution)/shard_map/ppermute | solution.py:27
  212.7 12.1 %collective-permute-start.2 = (f32[2,64,2,256]{3,1,2,0:T(8,128)S(1)}, f32[2,64,2,256]{3,1,2,0:T(8,128)S(1)}, u32[]{:S(2)}, u32[]{:S(2)}) collective-permute-start(f32[2,64,2,256]{3,1,2,0:T(8,128)S(1)} %dynamic-slice_bitcast_fusion), channel_id=1, source_target_pairs={{0,128},{64,192},{128,0},{192,64},{1,129},{65,193},{129,1},{193,65... | collective-permute-start | bytes 786440 | tf_op jit(solution)/shard_map/ppermute | solution.py:27
  219.3 11.2 %collective-permute-start.5 = (f32[2,64,2,256]{3,1,2,0:T(8,128)S(1)}, f32[2,64,2,256]{3,1,2,0:T(8,128)S(1)}, u32[]{:S(2)}, u32[]{:S(2)}) collective-permute-start(f32[2,64,2,256]{3,1,2,0:T(8,128)S(1)} %add.65), channel_id=1, source_target_pairs={{0,64},{64,0},{128,192},{192,128},{1,65},{65,1},{129,193},{193,129... | collective-permute-start | bytes 786440 | tf_op jit(solution)/shard_map/ppermute | solution.py:28
  224.9 5.7 %collective-permute-start.3 = (f32[2,64,2,256]{3,1,2,0:T(8,128)S(1)}, f32[2,64,2,256]{3,1,2,0:T(8,128)S(1)}, u32[]{:S(2)}, u32[]{:S(2)}) collective-permute-start(f32[2,64,2,256]{3,1,2,0:T(8,128)S(1)} %fusion.85), channel_id=1, source_target_pairs={{0,64},{64,0},{128,192},{192,128},{1,65},{65,1},{129,193},{193,129... | collective-permute-start | bytes 786440 | tf_op jit(solution)/shard_map/ppermute | solution.py:28
  230.6 2.0 copy-start.1

commit v2 on v1

--- a/solution.py
+++ b/solution.py
@@ -68,8 +68,13 @@
         part = jnp.einsum("jpid,ajid->jpa", value_gradient, got, preferred_element_type=f32)
         send = jnp.einsum("jpa,jpid->ajid", f2, value_gradient, preferred_element_type=f32).astype(bf16)
         send = send.reshape(n_seq, own, per, images, width)
-        part, send = lax.optimization_barrier((part, send))
-        sfg.append(dp_sum_halves(part, n_dp)[0])
+        if sfg:
+            part, send, sfg[-1] = lax.optimization_barrier((part, send, sfg[-1]))
+        else:
+            part, send = lax.optimization_barrier((part, send))
+        if k < CHUNKS - 1:
+            part = dp_sum_halves(part, n_dp)[0]
+        sfg.append(part)
         recv2.append(lax.all_to_all(send, "seq", 0, 0, tiled=True))
 
     grad_one = []
@@ -77,6 +82,9 @@
     for k in range(CHUNKS):
         got = recv2[k]
         part = jnp.einsum("sajid,iabd->asjb", got, scaled, preferred_element_type=f32)
+        if k == 0:
+            part, sfg[-1] = lax.optimization_barrier((part, sfg[-1]))
+            sfg[-1] = dp_sum_halves(sfg[-1], n_dp)[0]
         if k == CHUNKS - 1:
             reduced, got = dp_sum_halves(part, n_dp, hold=got)
         else:

time: 234 us -> 228 us (0.974)
  waiting for transfers between devices: 101 us -> 93.4 us
  starting transfers between devices: 59.5 us -> 62 us
    ppermute x4, waiting for transfers between devices: 28.9 us -> 21 us  [dp_sum_halves(): mine = mine + lax.ppermute(mine, 'dp', [(i, i ^ 2) for i in range(n_dp)])]
    optimization_barrier x0 -> x1, local copies, waits for them, and re-layouts: none -> 2.76 us  [on_device(): part, send, sfg[-1] = lax.optimization_barrier((part, send, sfg[-1]))]
    optimization_barrier x2 -> x1, local copies, waits for them, and re-layouts: 5.52 us -> 2.76 us  [on_device(): part, send = lax.optimization_barrier((part, send))]
    add x4, other arithmetic: 3.31 us -> 0.92 us  [dp_sum_halves(): x = x + lax.ppermute(x, 'dp', [(i, i ^ 1) for i in range(n_dp)])]
    ppermute x4, starting transfers between devices: 10.3 us -> 12.6 us  [dp_sum_halves(): x = x + lax.ppermute(x, 'dp', [(i, i ^ 1) for i in range(n_dp)])]
where the time goes in v2:
time: 228 us; the launch traced here: 227 us
  waiting for transfers between devices  93.4 us (41%)
  starting transfers between devices  62 us (27%)
  local copies, waits for them, and re-layouts  34.1 us (15%)
  matrix products  31.1 us (14%)
  other arithmetic  5.31 us (2%)
    all_to_all x2, waiting for transfers between devices, on_device(): recv1.append(lax.all_to_all(mixed, 'seq', 0, 0, tiled=True))  48.1 us
    all_to_all x2, starting transfers between devices, on_device(): recv1.append(lax.all_to_all(mixed, 'seq', 0, 0, tiled=True))  23.4 us
    all_to_all x2, waiting for transfers between devices, on_device(): recv2.append(lax.all_to_all(send, 'seq', 0, 0, tiled=True))  22.8 us
    ppermute x4, waiting for transfers between devices, dp_sum_halves(): mine = mine + lax.ppermute(mine, 'dp', [(i, i ^ 2) for i in range(n_dp)])  21 us
    all_to_all x2, starting transfers between devices, on_device(): recv2.append(lax.all_to_all(send, 'seq', 0, 0, tiled=True))  17.7 us
    ppermute x4, starting transfers between devices, dp_sum_halves(): x = x + lax.ppermute(x, 'dp', [(i, i ^ 1) for i in range(n_dp)])  12.6 us
    unnamed x32, local copies, waits for them, and re-layouts  8 us
    reshape x2, local copies, waits for them, and re-layouts, on_device(): send = send.reshape(n_seq, own, per, images, width)  7.76 us
  transfers between devices with their start and end apart: 16, of which 9 were waited for; matrix products, arithmetic and copies ran while one was open for 26% of the time, Pallas kernels for 0%

profile of v2, /device:TPU:1, one launch (start us, length us, event | category | flops | bytes accessed | tf_op | source)
XLA Modules:
  0.0 226.9 jit_solution(4903391633482825796)
XLA Ops:
  3.2 2.6 %fusion.38 = bf16[64,4,2,2,768]{4,0,2,3,1:T(8,128)(2,1)S(1)} fusion(bf16[4,64,2,256]{3,0,2,1:T(4,128)(2,1)S(1)} %get-tuple-element.38, f32[2,768]{1,0:T(2,128)S(1)} %fusion.73, bf16[2,4,256,768]{3,2,1,0:T(8,128)(2,1)} %bitcast.180), kind=kOutput, calls=%fused_computation.42 | convolution fusion | flops 408158208 | bytes 4986880 | tf_op jit(solution)/shard_map/asjb,iabd->sajid/dot_general | solution.py:52
  5.9 2.8 %copy.75 = bf16[64,4,2,2,768]{4,2,3,1,0:T(2,128)(2,1)} copy(bf16[64,4,2,2,768]{4,0,2,3,1:T(8,128)(2,1)S(1)} %fusion.38) | data formatting | bytes 3145728 | tf_op jit(solution)/shard_map/convert_element_type | solution.py:54
  8.6 15.1 %all-to-all-start = ((bf16[64,4,2,2,768]{4,2,3,1,0:T(2,128)(2,1)}), bf16[64,4,2,2,768]{4,2,3,1,0:T(2,128)(2,1)S(1)}, u32[]{:S(2)}, u32[]{:S(2)}) async-start(bf16[64,4,2,2,768]{4,2,3,1,0:T(2,128)(2,1)} %copy.75), calls=%async_computation | async-start | bytes 3145728 | tf_op jit(solution)/shard_map/all_to_all | solution.py:55
  23.7 2.6 %fusion.35 = bf16[64,4,2,2,768]{4,0,2,3,1:T(8,128)(2,1)S(1)} fusion(bf16[4,64,2,256]{3,0,2,1:T(4,128)(2,1)S(1)} %get-tuple-element.37, f32[2,768]{1,0:T(2,128)S(1)} %fusion.73, bf16[2,4,256,768]{3,2,1,0:T(8,128)(2,1)} %bitcast.181), kind=kOutput, calls=%fused_computation.41 | convolution fusion | flops 408158208 | bytes 4986880 | tf_op jit(solution)/shard_map/asjb,iabd->sajid/dot_general | solution.py:52
  26.4 2.8 %copy.86 = bf16[64,4,2,2,768]{4,2,3,1,0:T(2,128)(2,1)} copy(bf16[64,4,2,2,768]{4,0,2,3,1:T(8,128)(2,1)S(1)} %fusion.35) | data formatting | bytes 3145728 | tf_op jit(solution)/shard_map/convert_element_type | solution.py:54
  29.2 33.2 %all-to-all-done = bf16[64,4,2,2,768]{4,2,3,1,0:T(2,128)(2,1)S(1)} async-done(((bf16[64,4,2,2,768]{4,2,3,1,0:T(2,128)(2,1)}), bf16[64,4,2,2,768]{4,2,3,1,0:T(2,128)(2,1)S(1)}, u32[]{:S(2)}, u32[]{:S(2)}) %all-to-all-start) | async-done | bytes 1572896 | tf_op jit(solution)/shard_map/all_to_all | solution.py:55
  62.4 8.3 %all-to-all-start.2 = ((bf16[64,4,2,2,768]{4,2,3,1,0:T(2,128)(2,1)}), bf16[64,4,2,2,768]{4,2,3,1,0:T(2,128)(2,1)S(1)}, u32[]{:S(2)}, u32[]{:S(2)}) async-start(bf16[64,4,2,2,768]{4,2,3,1,0:T(2,128)(2,1)} %copy.86), calls=%async_computation.2 | async-start | bytes 3145728 | tf_op jit(solution)/shard_map/all_to_all | solution.py:55
  70.7 3.8 %fusion.77 = (bf16[2,2,256,768]{3,2,1,0:T(8,128)(2,1)}, bf16[2,2,256,768]{3,2,1,0:T(8,128)(2,1)}) fusion(bf16[2,4,256,768]{3,2,1,0:T(8,128)(2,1)} %bitcast.174), kind=kLoop, calls=%fused_computation.85 | loop fusion | bytes 6291456 | tf_op jit(solution)/shard_map/slice | solution.py:64
  74.5 2.6 %copy.126 = bf16[2,2,256,768]{2,3,0,1:T(8,128)(2,1)} copy(bf16[2,2,256,768]{3,2,1,0:T(8,128)(2,1)} %get-tuple-element.28) | data formatting | bytes 3145728
  77.3 3.0 %fusion.23 = bf16[2,256,2,768]{1,3,2,0:T(8,128)(2,1)S(1)} fusion(bf16[2,2,256,768]{2,3,0,1:T(8,128)(2,1)} %copy.126, f32[2,768]{1,0:T(2,128)S(1)} %fusion.74, bf16[256,2,2,768]{3,1,2,0:T(2,128)(2,1)S(1)} %bitcast.171, bf16[4,256,256]{2,1,0:T(8,128)(2,1)} %param.13), kind=kOutput, calls=%fused_computation.30 | convolution fusion | flops 411303936 | bytes 4986880 | tf_op jit(solution)/shard_map/jpa,ajid->jpid/dot_general | solution.py:62
  83.3 3.9 %reshape.51 = bf16[64,4,2,2,768]{4,1,0,3,2:T(4,128)(2,1)} reshape(bf16[256,2,2,768]{3,0,2,1:T(8,128)(2,1)} %fusion.41) | data formatting | bytes 3145728 | tf_op jit(solution)/shard_map/reshape | solution.py:70
  87.2 3.1 %fusion.59 = f32[2,256,256]{2,1,0:T(8,128)} fusion(bf16[2,256,2,768]{1,3,2,0:T(8,128)(2,1)} %copy-done.3, bf16[256,2,2,768]{3,1,2,0:T(2,128)(2,1)S(1)} %bitcast.172), kind=kOutput, calls=%fused_computation.53 | convolution fusion | flops 402653184 | bytes 3670016 | tf_op jit(solution)/shard_map/jpid,ajid->jpa/dot_general | solution.py:68
  90.3 2.8 %copy.82 = bf16[64,4,2,2,768]{4,2,3,1,0:T(2,128)(2,1)} copy(bf16[64,4,2,2,768]{4,1,0,3,2:T(4,128)(2,1)S(1)} %copy-done.4) | data formatting | bytes 3145728 | tf_op jit(solution)/shard_map/optimization_barrier | solution.py:74
  93.0 14.9 %all-to-all-done.2 = bf16[64,4,2,2,768]{4,2,3,1,0:T(2,128)(2,1)S(1)} async-done(((bf16[64,4,2,2,768]{4,2,3,1,0:T(2,128)(2,1)}), bf16[64,4,2,2,768]{4,2,3,1,0:T(2,128)(2,1)S(1)}, u32[]{:S(2)}, u32[]{:S(2)}) %all-to-all-start.2) | async-done | bytes 1572896 | tf_op jit(solution)/shard_map/all_to_all | solution.py:55
  108.0 9.1 %all-to-all-start.1 = ((bf16[64,4,2,2,768]{4,2,3,1,0:T(2,128)(2,1)}), bf16[64,4,2,2,768]{4,2,3,1,0:T(2,128)(2,1)}, u32[]{:S(2)}, u32[]{:S(2)}) async-start(bf16[64,4,2,2,768]{4,2,3,1,0:T(2,128)(2,1)} %copy.82), calls=%async_computation.1 | async-start | bytes 3145728 | tf_op jit(solution)/shard_map/all_to_all | solution.py:78
  118.7 2.4 %collective-permute-start = (f32[2,256,256]{2,1,0:T(8,128)}, f32[2,256,256]{2,1,0:T(8,128)S(1)}, u32[]{:S(2)}, u32[]{:S(2)}) collective-permute-start(f32[2,256,256]{2,1,0:T(8,128)} %fusion.59), channel_id=1, source_target_pairs={{0,64},{64,0},{128,192},{192,128},{1,65},{65,1},{129,193},{193,129... | collective-permute-start | bytes 1572872 | tf_op jit(solution)/shard_map/ppermute | solution.py:22
  121.1 3.0 %fusion.13 = bf16[2,256,2,768]{1,3,2,0:T(8,128)(2,1)S(1)} fusion(bf16[2,2,256,768]{2,3,0,1:T(8,128)(2,1)} %copy.128, f32[2,768]{1,0:T(2,128)S(1)} %fusion.74, bf16[256,2,2,768]{3,1,2,0:T(2,128)(2,1)S(1)} %bitcast.169, bf16[4,256,256]{2,1,0:T(8,128)(2,1)} %param.13), kind=kOutput, calls=%fused_computation.17 | convolution fusion | flops 411303936 | bytes 4986880 | tf_op jit(solution)/shard_map/jpa,ajid->jpid/dot_general | solution.py:62
  127.0 3.9 %reshape.53 = bf16[64,4,2,2,768]{4,1,0,3,2:T(4,128)(2,1)} reshape(bf16[256,2,2,768]{3,0,2,1:T(8,128)(2,1)} %fusion.42) | data formatting | bytes 3145728 | tf_op jit(solution)/shard_map/reshape | solution.py:70
  130.9 6.4 %collective-permute-done.1 = f32[1,256,256]{2,1,0:T(8,128)} collective-permute-done((f32[1,256,256]{2,1,0:T(8,128)}, f32[1,256,256]{2,1,0:T(8,128)}, u32[]{:S(2)}, u32[]{:S(2)}) %collective-permute-start.1) | collective-permute-done | bytes 262176 | tf_op jit(solution)/shard_map/ppermute | solution.py:27
  141.1 2.8 %copy.93 = bf16[64,4,2,2,768]{4,3,2,1,0:T(2,128)(2,1)} copy(bf16[64,4,2,2,768]{4,1,0,3,2:T(4,128)(2,1)S(1)} %copy-done.2) | data formatting | bytes 3145728 | tf_op jit(solution)/shard_map/optimization_barrier | solution.py:72
  143.9 10.0 %all-to-all-done.1 = bf16[64,4,2,2,768]{4,2,3,1,0:T(2,128)(2,1)} async-done(((bf16[64,4,2,2,768]{4,2,3,1,0:T(2,128)(2,1)}), bf16[64,4,2,2,768]{4,2,3,1,0:T(2,128)(2,1)}, u32[]{:S(2)}, u32[]{:S(2)}) %all-to-all-start.1) | async-done | bytes 1572896 | tf_op jit(solution)/shard_map/all_to_all | solution.py:78
  154.0 8.6 %all-to-all-start.3 = ((bf16[64,4,2,2,768]{4,3,2,1,0:T(2,128)(2,1)}), bf16[64,4,2,2,768]{4,3,2,1,0:T(2,128)(2,1)S(1)}, u32[]{:S(2)}, u32[]{:S(2)}) async-start(bf16[64,4,2,2,768]{4,3,2,1,0:T(2,128)(2,1)} %copy.93), calls=%async_computation.3 | async-start | bytes 3145728 | tf_op jit(solution)/shard_map/all_to_all | solution.py:78
  162.6 3.6 %fusion.54 = f32[4,64,2,256]{3,1,2,0:T(8,128)S(1)} fusion(bf16[64,4,2,2,768]{4,2,3,1,0:T(2,128)(2,1)} %all-to-all-done.1, f32[2,768]{1,0:T(2,128)S(1)} %fusion.73, bf16[2,4,256,768]{3,2,1,0:T(8,128)(2,1)} %bitcast.182), kind=kOutput, calls=%fused_computation.52 | convolution fusion | flops 407371776 | bytes 5249024 | tf_op jit(solution)/shard_map/sajid,iabd->asjb/dot_general | solution.py:84
  166.2 3.3 %collective-permute-start.9 = (f32[2,256,256]{2,1,0:T(8,128)S(1)}, f32[2,256,256]{2,1,0:T(8,128)S(1)}, u32[]{:S(2)}, u32[]{:S(2)}) collective-permute-start(f32[2,256,256]{2,1,0:T(8,128)S(1)} %copy-done.7), channel_id=1, source_target_pairs={{0,64},{64,0},{128,192},{192,128},{1,65},{65,1},{129,193},{193,129... | collective-permute-start | bytes 1572872 | tf_op jit(solution)/shard_map/ppermute | solution.py:22
  173.4 9.5 %collective-permute-done.10 = f32[1,256,256]{2,1,0:T(8,128)S(1)} collective-permute-done((f32[1,256,256]{2,1,0:T(8,128)S(1)}, f32[1,256,256]{2,1,0:T(8,128)S(1)}, u32[]{:S(2)}, u32[]{:S(2)}) %collective-permute-start.10) | collective-permute-done | bytes 262176 | tf_op jit(solution)/shard_map/ppermute | solution.py:27
  183.0 2.1 collective-permute-start.11
  185.1 12.8 %all-to-all-done.3 = bf16[64,4,2,2,768]{4,3,2,1,0:T(2,128)(2,1)S(1)} async-done(((bf16[64,4,2,2,768]{4,3,2,1,0:T(2,128)(2,1)}), bf16[64,4,2,2,768]{4,3,2,1,0:T(2,128)(2,1)S(1)}, u32[]{:S(2)}, u32[]{:S(2)}) %all-to-all-start.3) | async-done | bytes 1572896 | tf_op jit(solution)/shard_map/all_to_all | solution.py:78
  197.8 3.2 %fusion.49 = f32[4,64,2,256]{3,1,2,0:T(8,128)S(1)} fusion(bf16[64,4,2,2,768]{4,3,2,1,0:T(2,128)(2,1)S(1)} %all-to-all-done.3, f32[2,768]{1,0:T(2,128)S(1)} %fusion.73, bf16[2,4,256,768]{3,2,1,0:T(8,128)(2,1)} %bitcast.183), kind=kOutput, calls=%fused_computation.51 | convolution fusion | flops 407371776 | bytes 5249024 | tf_op jit(solution)/shard_map/sajid,iabd->asjb/dot_general | solution.py:84
  201.0 6.9 %collective-permute-start.3 = (f32[4,64,2,256]{3,1,2,0:T(8,128)S(1)}, f32[4,64,2,256]{3,1,2,0:T(8,128)S(1)}, u32[]{:S(2)}, u32[]{:S(2)}) collective-permute-start(f32[4,64,2,256]{3,1,2,0:T(8,128)S(1)} %fusion.49), channel_id=1, source_target_pairs={{0,64},{64,0},{128,192},{192,128},{1,65},{65,1},{129,193},{193,129... | collective-permute-start | bytes 1572872 | tf_op jit(solution)/shard_map/ppermute | solution.py:22
  208.0 2.5 %fusion.33 = f32[4,2,768,256,1]{2,3,4,1,0:T(8,128)S(1)} fusion(bf16[64,4,2,2,768]{4,2,3,1,0:T(2,128)(2,1)} %all-to-all-done.1, bf16[4,64,2,256]{3,0,2,1:T(4,128)(2,1)S(1)} %copy-done.9), kind=kOutput, calls=%fused_computation.39 | convolution fusion | flops 402653184 | bytes 8126464 | tf_op jit(solution)/shard_map/asjb,sajid->iabd/dot_general | solution.py:93
  215.2 5.0 %collective-permute-done.7 = f32[2,64,2,256]{3,1,2,0:T(8,128)S(1)} collective-permute-done((f32[2,64,2,256]{3,1,2,0:T(8,128)S(1)}, f32[2,64,2,256]{3,1,2,0:T(8,128)S(1)}, u32[]{:S(2)}, u32[]{:S(2)}) %collective-permute-start.7) | collective-permute-done | bytes 262176 | tf_op jit(solution)/shard_map/ppermute | solution.py:27
  223.0 1.9 copy.96
  (73 shorter events, 27.5 us)
Async XLA Ops:
  0.6 1.7 copy-start
  2.3 3.5 %copy-start.8 = (bf16[4,64,2,256]{3,0,2,1:T(4,128)(2,1)}, bf16[4,64,2,256]{3,0,2,1:T(4,128)(2,1)S(1)}, u32[]{:S(2)}) copy-start(bf16[4,64,2,256]{3,0,2,1:T(4,128)(2,1)S(1)} %get-tuple-element.38) | copy-start | bytes 786436
  8.6 53.8 %all-to-all-start = ((bf16[64,4,2,2,768]{4,2,3,1,0:T(2,128)(2,1)}), bf16[64,4,2,2,768]{4,2,3,1,0:T(2,128)(2,1)S(1)}, u32[]{:S(2)}, u32[]{:S(2)}) async-start(bf16[64,4,2,2,768]{4,2,3,1,0:T(2,128)(2,1)} %copy.75), calls=%async_computation | async-start | bytes 3145728 | tf_op jit(solution)/shard_map/all_to_all | solution.py:55
  62.4 45.6 %all-to-all-start.2 = ((bf16[64,4,2,2,768]{4,2,3,1,0:T(2,128)(2,1)}), bf16[64,4,2,2,768]{4,2,3,1,0:T(2,128)(2,1)S(1)}, u32[]{:S(2)}, u32[]{:S(2)}) async-start(bf16[64,4,2,2,768]{4,2,3,1,0:T(2,128)(2,1)} %copy.86), calls=%async_computation.2 | async-start | bytes 3145728 | tf_op jit(solution)/shard_map/all_to_all | solution.py:55
  74.5 2.6 %copy-start.12 = (f32[16,768]{1,0:T(8,128)S(1)}, f32[16,768]{1,0:T(8,128)}, u32[]{:S(2)}) copy-start(f32[16,768]{1,0:T(8,128)} %param.11) | copy-start | bytes 147460
  74.5 2.6 %copy-start.13 = (s32[2]{0:T(128)S(1)}, s32[2]{0:T(128)}, u32[]{:S(2)}) copy-start(s32[2]{0:T(128)} %param.9) | copy-start | bytes 28
  77.3 4.2 %copy-start.10 = (bf16[4,256,256]{2,1,0:T(8,128)(2,1)S(1)}, bf16[4,256,256]{2,1,0:T(8,128)(2,1)}, u32[]{:S(2)}) copy-start(bf16[4,256,256]{2,1,0:T(8,128)(2,1)} %param.13) | copy-start | bytes 1572868
  80.3 1.1 copy-start.3
  87.2 3.1 %copy-start.4 = (bf16[64,4,2,2,768]{4,1,0,3,2:T(4,128)(2,1)S(1)}, bf16[64,4,2,2,768]{4,1,0,3,2:T(4,128)(2,1)}, u32[]{:S(2)}) copy-start(bf16[64,4,2,2,768]{4,1,0,3,2:T(4,128)(2,1)} %reshape.51) | copy-start | bytes 4718596
  90.3 26.8 %copy-start.5 = (bf16[2,2,256,768]{3,2,1,0:T(8,128)(2,1)S(1)}, bf16[2,2,256,768]{3,2,1,0:T(8,128)(2,1)}, u32[]{:S(2)}) copy-start(bf16[2,2,256,768]{3,2,1,0:T(8,128)(2,1)} %get-tuple-element.27) | copy-start | bytes 4718596
  108.0 46.0 %all-to-all-start.1 = ((bf16[64,4,2,2,768]{4,2,3,1,0:T(2,128)(2,1)}), bf16[64,4,2,2,768]{4,2,3,1,0:T(2,128)(2,1)}, u32[]{:S(2)}, u32[]{:S(2)}) async-start(bf16[64,4,2,2,768]{4,2,3,1,0:T(2,128)(2,1)} %copy.82), calls=%async_computation.1 | async-start | bytes 3145728 | tf_op jit(solution)/shard_map/all_to_all | solution.py:78
  118.7 5.4 %collective-permute-start = (f32[2,256,256]{2,1,0:T(8,128)}, f32[2,256,256]{2,1,0:T(8,128)S(1)}, u32[]{:S(2)}, u32[]{:S(2)}) collective-permute-start(f32[2,256,256]{2,1,0:T(8,128)} %fusion.59), channel_id=1, source_target_pairs={{0,64},{64,0},{128,192},{192,128},{1,65},{65,1},{129,193},{193,129... | collective-permute-start | bytes 1572872 | tf_op jit(solution)/shard_map/ppermute | solution.py:22
  121.0 3.1 %copy-start.6 = (f32[2,256,256]{2,1,0:T(8,128)S(1)}, f32[2,256,256]{2,1,0:T(8,128)}, u32[]{:S(2)}) copy-start(f32[2,256,256]{2,1,0:T(8,128)} %fusion.59) | copy-start | bytes 1572868
  121.1 4.2 %copy-start.11 = (bf16[4,256,256]{2,1,0:T(8,128)(2,1)S(1)}, bf16[4,256,256]{2,1,0:T(8,128)(2,1)}, u32[]{:S(2)}) copy-start(bf16[4,256,256]{2,1,0:T(8,128)(2,1)} %param.13) | copy-start | bytes 1572868
  124.9 12.5 %collective-permute-start.1 = (f32[1,256,256]{2,1,0:T(8,128)}, f32[1,256,256]{2,1,0:T(8,128)}, u32[]{:S(2)}, u32[]{:S(2)}) collective-permute-start(f32[1,256,256]{2,1,0:T(8,128)} %dynamic-slice_add_fusion.1), channel_id=1, source_target_pairs={{0,128},{64,192},{128,0},{192,64},{1,129},{65,193},{129,1},{193,65... | collective-permute-start | bytes 786440 | tf_op jit(solution)/shard_map/ppermute | solution.py:27
  130.9 10.2 %copy-start.2 = (bf16[64,4,2,2,768]{4,1,0,3,2:T(4,128)(2,1)S(1)}, bf16[64,4,2,2,768]{4,1,0,3,2:T(4,128)(2,1)}, u32[]{:S(2)}) copy-start(bf16[64,4,2,2,768]{4,1,0,3,2:T(4,128)(2,1)} %reshape.53) | copy-start | bytes 4718596
  138.4 2.6 %collective-permute-start.2 = (f32[1,256,256]{2,1,0:T(8,128)S(1)}, f32[1,256,256]{2,1,0:T(8,128)S(1)}, u32[]{:S(2)}, u32[]{:S(2)}) collective-permute-start(f32[1,256,256]{2,1,0:T(8,128)S(1)} %add.62), channel_id=1, source_target_pairs={{0,64},{64,0},{128,192},{192,128},{1,65},{65,1},{129,193},{193,129... | collective-permute-start | bytes 786440 | tf_op jit(solution)/shard_map/ppermute | solution.py:28
  154.0 43.9 %all-to-all-start.3 = ((bf16[64,4,2,2,768]{4,3,2,1,0:T(2,128)(2,1)}), bf16[64,4,2,2,768]{4,3,2,1,0:T(2,128)(2,1)S(1)}, u32[]{:S(2)}, u32[]{:S(2)}) async-start(bf16[64,4,2,2,768]{4,3,2,1,0:T(2,128)(2,1)} %copy.93), calls=%async_computation.3 | async-start | bytes 3145728 | tf_op jit(solution)/shard_map/all_to_all | solution.py:78
  162.6 3.6 %copy-start.7 = (f32[2,256,256]{2,1,0:T(8,128)S(1)}, f32[2,256,256]{2,1,0:T(8,128)}, u32[]{:S(2)}) copy-start(f32[2,256,256]{2,1,0:T(8,128)} %fusion.62) | copy-start | bytes 1572868
  166.2 4.8 %collective-permute-start.9 = (f32[2,256,256]{2,1,0:T(8,128)S(1)}, f32[2,256,256]{2,1,0:T(8,128)S(1)}, u32[]{:S(2)}, u32[]{:S(2)}) collective-permute-start(f32[2,256,256]{2,1,0:T(8,128)S(1)} %copy-done.7), channel_id=1, source_target_pairs={{0,64},{64,0},{128,192},{192,128},{1,65},{65,1},{129,193},{193,129... | collective-permute-start | bytes 1572872 | tf_op jit(solution)/shard_map/ppermute | solution.py:22
  169.5 2.3 %collective-permute-start.4 = (f32[4,64,2,256]{3,1,2,0:T(8,128)S(1)}, f32[4,64,2,256]{3,1,2,0:T(8,128)S(1)}, u32[]{:S(2)}, u32[]{:S(2)}) collective-permute-start(f32[4,64,2,256]{3,1,2,0:T(8,128)S(1)} %fusion.54), channel_id=1, source_target_pairs={{0,64},{64,0},{128,192},{192,128},{1,65},{65,1},{129,193},{193,129... | collective-permute-start | bytes 1572872 | tf_op jit(solution)/shard_map/ppermute | solution.py:22
  171.0 11.9 %collective-permute-start.10 = (f32[1,256,256]{2,1,0:T(8,128)S(1)}, f32[1,256,256]{2,1,0:T(8,128)S(1)}, u32[]{:S(2)}, u32[]{:S(2)}) collective-permute-start(f32[1,256,256]{2,1,0:T(8,128)S(1)} %dynamic-slice_add_fusion), channel_id=1, source_target_pairs={{0,128},{64,192},{128,0},{192,64},{1,129},{65,193},{129,1},{193,65... | collective-permute-start | bytes 786440 | tf_op jit(solution)/shard_map/ppermute | solution.py:27
  172.6 37.9 %collective-permute-start.5 = (f32[2,64,2,256]{3,1,2,0:T(8,128)}, f32[2,64,2,256]{3,1,2,0:T(8,128)}, u32[]{:S(2)}, u32[]{:S(2)}) collective-permute-start(f32[2,64,2,256]{3,1,2,0:T(8,128)} %dynamic-slice_bitcast_fusion), channel_id=1, source_target_pairs={{0,128},{64,192},{128,0},{192,64},{1,129},{65,193},{129,1},{193,65... | collective-permute-start | bytes 786440 | tf_op jit(solution)/shard_map/ppermute | solution.py:27
  183.0 25.0 %copy-start.9 = (bf16[4,64,2,256]{3,0,2,1:T(4,128)(2,1)S(1)}, bf16[4,64,2,256]{3,0,2,1:T(4,128)(2,1)}, u32[]{:S(2)}) copy-start(bf16[4,64,2,256]{3,0,2,1:T(4,128)(2,1)} %copy-done.8) | copy-start | bytes 786436
  183.0 28.6 %collective-permute-start.11 = (f32[1,256,256]{2,1,0:T(8,128)S(1)}, f32[1,256,256]{2,1,0:T(8,128)}, u32[]{:S(2)}, u32[]{:S(2)}) collective-permute-start(f32[1,256,256]{2,1,0:T(8,128)S(1)} %add.69), channel_id=1, source_target_pairs={{0,64},{64,0},{128,192},{192,128},{1,65},{65,1},{129,193},{193,129... | collective-permute-start | bytes 786440 | tf_op jit(solution)/shard_map/ppermute | solution.py:28
  201.0 11.5 %collective-permute-start.3 = (f32[4,64,2,256]{3,1,2,0:T(8,128)S(1)}, f32[4,64,2,256]{3,1,2,0:T(8,128)S(1)}, u32[]{:S(2)}, u32[]{:S(2)}) collective-permute-start(f32[4,64,2,256]{3,1,2,0:T(8,128)S(1)} %fusion.49), channel_id=1, source_target_pairs={{0,64},{64,0},{128,192},{192,128},{1,65},{65,1},{129,193},{193,129... | collective-permute-start | bytes 1572872 | tf_op jit(solution)/shard_map/ppermute | solution.py:22
  211.5 3.7 %collective-permute-start.6 = (f32[2,64,2,256]{3,1,2,0:T(8,128)S(1)}, f32[2,64,2,256]{3,1,2,0:T(8,128)S(1)}, u32[]{:S(2)}, u32[]{:S(2)}) collective-permute-start(f32[2,64,2,256]{3,1,2,0:T(8,128)S(1)} %fusion.85), channel_id=1, source_target_pairs={{0,64},{64,0},{128,192},{192,128},{1,65},{65,1},{129,193},{193,129... | collective-permute-start | bytes 786440 | tf_op jit(solution)/shard_map/ppermute | solution.py:28
  212.7 7.5 %collective-permute-start.7 = (f32[2,64,2,256]{3,1,2,0:T(8,128)S(1)}, f32[2,64,2,256]{3,1,2,0:T(8,128)S(1)}, u32[]{:S(2)}, u32[]{:S(2)}) collective-permute-start(f32[2,64,2,256]{3,1,2,0:T(8,128)S(1)} %dynamic-slice_bitcast_fusion.1), channel_id=1, source_target_pairs={{0,128},{64,192},{128,0},{192,64},{1,129},{65,193},{129,1},{193,65... | collective-permute-start | bytes 786440 | tf_op jit(solution)/shard_map/ppermute | solution.py:27
  220.2 4.7 %collective-permute-start.8 = (f32[2,64,2,256]{3,1,2,0:T(8,128)S(1)}, f32[2,64,2,256]{3,1,2,0:T(8,128)S(1)}, u32[]{:S(2)}, u32[]{:S(2)}) collective-permute-start(f32[2,64,2,256]{3,1,2,0:T(8,128)S(1)} %add.67), channel_id=1, source_target_pairs={{0,64},{64,0},{128,192},{192,128},{1,65},{65,1},{129,193},{193,129... | collective-permute-start | bytes 786440 | tf_op jit(solution)/shard_map/ppermute | solution.py:28
  225.0 1.9 copy-start.1

commit v3 on v2

--- a/solution.py
+++ b/solution.py
@@ -81,15 +81,17 @@
     back_sum = None
     for k in range(CHUNKS):
         got = recv2[k]
-        part = jnp.einsum("sajid,iabd->asjb", got, scaled, preferred_element_type=f32)
-        if k == 0:
-            part, sfg[-1] = lax.optimization_barrier((part, sfg[-1]))
-            sfg[-1] = dp_sum_halves(sfg[-1], n_dp)[0]
-        if k == CHUNKS - 1:
+        if k < CHUNKS - 1:
+            part = jnp.einsum("sajid,iabd->asjb", got, scaled, preferred_element_type=f32)
+            if k == 0:
+                part, sfg[-1] = lax.optimization_barrier((part, sfg[-1]))
+                sfg[-1] = dp_sum_halves(sfg[-1], n_dp)[0]
+            grad_one.append(dp_sum_halves(part, n_dp)[0])
+        else:
+            got, grad_one[:], sfg[:] = lax.optimization_barrier((got, list(grad_one), list(sfg)))
+            part = jnp.einsum("sajid,iabd->asjb", got, scaled, preferred_element_type=f32)
             reduced, got = dp_sum_halves(part, n_dp, hold=got)
-        else:
-            reduced, _ = dp_sum_halves(part, n_dp)
-        grad_one.append(reduced)
+            grad_one.append(reduced)
         term = jnp.einsum(
             "asjb,sajid->iabd", f1[:, :, k * per:(k + 1) * per, :], got, preferred_element_type=f32
         )

time: 228 us -> 225 us (0.987)
    all_to_all x2, waiting for transfers between devices: 22.8 us -> 11.5 us  [on_device(): recv2.append(lax.all_to_all(send, 'seq', 0, 0, tiled=True))]
    ppermute x4, waiting for transfers between devices: 21 us -> 28.1 us  [dp_sum_halves(): mine = mine + lax.ppermute(mine, 'dp', [(i, i ^ 2) for i in range(n_dp)])]
  transfers between devices with their start and end apart: 16 -> 16, of which waited for: 9 -> 11; matrix products, arithmetic and copies ran while one was open for 26% -> 24% of each run, Pallas kernels for 0% -> 0%
where the time goes in v3:
time: 225 us; the launch traced here: 224 us
  waiting for transfers between devices  91.8 us (41%)
  starting transfers between devices  63.1 us (28%)
  local copies, waits for them, and re-layouts  33.4 us (15%)
  matrix products  31.3 us (14%)
  other arithmetic  3.48 us (2%)
    all_to_all x2, waiting for transfers between devices, on_device(): recv1.append(lax.all_to_all(mixed, 'seq', 0, 0, tiled=True))  48.1 us
    ppermute x4, waiting for transfers between devices, dp_sum_halves(): mine = mine + lax.ppermute(mine, 'dp', [(i, i ^ 2) for i in range(n_dp)])  28.1 us
    all_to_all x2, starting transfers between devices, on_device(): recv1.append(lax.all_to_all(mixed, 'seq', 0, 0, tiled=True))  23.4 us
    all_to_all x2, starting transfers between devices, on_device(): recv2.append(lax.all_to_all(send, 'seq', 0, 0, tiled=True))  17.7 us
    ppermute x4, starting transfers between devices, dp_sum_halves(): x = x + lax.ppermute(x, 'dp', [(i, i ^ 1) for i in range(n_dp)])  12.6 us
    all_to_all x2, waiting for transfers between devices, on_device(): recv2.append(lax.all_to_all(send, 'seq', 0, 0, tiled=True))  11.5 us
    unnamed x32, local copies, waits for them, and re-layouts  8 us
    reshape x2, local copies, waits for them, and re-layouts, on_device(): send = send.reshape(n_seq, own, per, images, width)  7.76 us
  transfers between devices with their start and end apart: 16, of which 11 were waited for; matrix products, arithmetic and copies ran while one was open for 24% of the time, Pallas kernels for 0%

profile of v3, /device:TPU:1, one launch (start us, length us, event | category | flops | bytes accessed | tf_op | source)
XLA Modules:
  0.0 224.1 jit_solution(18074013898260313676)
XLA Ops:
  3.2 2.6 %fusion.38 = bf16[64,4,2,2,768]{4,0,2,3,1:T(8,128)(2,1)S(1)} fusion(bf16[4,64,2,256]{3,0,2,1:T(4,128)(2,1)S(1)} %get-tuple-element.46, f32[2,768]{1,0:T(2,128)S(1)} %fusion.73, bf16[2,4,256,768]{3,2,1,0:T(8,128)(2,1)} %bitcast.180), kind=kOutput, calls=%fused_computation.42 | convolution fusion | flops 408158208 | bytes 4986880 | tf_op jit(solution)/shard_map/asjb,iabd->sajid/dot_general | solution.py:52
  5.9 2.8 %copy.75 = bf16[64,4,2,2,768]{4,2,3,1,0:T(2,128)(2,1)} copy(bf16[64,4,2,2,768]{4,0,2,3,1:T(8,128)(2,1)S(1)} %fusion.38) | data formatting | bytes 3145728 | tf_op jit(solution)/shard_map/convert_element_type | solution.py:54
  8.6 15.1 %all-to-all-start = ((bf16[64,4,2,2,768]{4,2,3,1,0:T(2,128)(2,1)}), bf16[64,4,2,2,768]{4,2,3,1,0:T(2,128)(2,1)S(1)}, u32[]{:S(2)}, u32[]{:S(2)}) async-start(bf16[64,4,2,2,768]{4,2,3,1,0:T(2,128)(2,1)} %copy.75), calls=%async_computation | async-start | bytes 3145728 | tf_op jit(solution)/shard_map/all_to_all | solution.py:55
  23.7 2.6 %fusion.35 = bf16[64,4,2,2,768]{4,0,2,3,1:T(8,128)(2,1)S(1)} fusion(bf16[4,64,2,256]{3,0,2,1:T(4,128)(2,1)S(1)} %get-tuple-element.45, f32[2,768]{1,0:T(2,128)S(1)} %fusion.73, bf16[2,4,256,768]{3,2,1,0:T(8,128)(2,1)} %bitcast.181), kind=kOutput, calls=%fused_computation.41 | convolution fusion | flops 408158208 | bytes 4986880 | tf_op jit(solution)/shard_map/asjb,iabd->sajid/dot_general | solution.py:52
  26.4 2.8 %copy.86 = bf16[64,4,2,2,768]{4,2,3,1,0:T(2,128)(2,1)} copy(bf16[64,4,2,2,768]{4,0,2,3,1:T(8,128)(2,1)S(1)} %fusion.35) | data formatting | bytes 3145728 | tf_op jit(solution)/shard_map/convert_element_type | solution.py:54
  29.2 33.2 %all-to-all-done = bf16[64,4,2,2,768]{4,2,3,1,0:T(2,128)(2,1)S(1)} async-done(((bf16[64,4,2,2,768]{4,2,3,1,0:T(2,128)(2,1)}), bf16[64,4,2,2,768]{4,2,3,1,0:T(2,128)(2,1)S(1)}, u32[]{:S(2)}, u32[]{:S(2)}) %all-to-all-start) | async-done | bytes 1572896 | tf_op jit(solution)/shard_map/all_to_all | solution.py:55
  62.4 8.3 %all-to-all-start.2 = ((bf16[64,4,2,2,768]{4,2,3,1,0:T(2,128)(2,1)}), bf16[64,4,2,2,768]{4,2,3,1,0:T(2,128)(2,1)S(1)}, u32[]{:S(2)}, u32[]{:S(2)}) async-start(bf16[64,4,2,2,768]{4,2,3,1,0:T(2,128)(2,1)} %copy.86), calls=%async_computation.2 | async-start | bytes 3145728 | tf_op jit(solution)/shard_map/all_to_all | solution.py:55
  70.7 3.8 %fusion.77 = (bf16[2,2,256,768]{3,2,1,0:T(8,128)(2,1)}, bf16[2,2,256,768]{3,2,1,0:T(8,128)(2,1)}) fusion(bf16[2,4,256,768]{3,2,1,0:T(8,128)(2,1)} %bitcast.174), kind=kLoop, calls=%fused_computation.87 | loop fusion | bytes 6291456 | tf_op jit(solution)/shard_map/slice | solution.py:64
  74.5 2.6 %copy.126 = bf16[2,2,256,768]{2,3,0,1:T(8,128)(2,1)} copy(bf16[2,2,256,768]{3,2,1,0:T(8,128)(2,1)} %get-tuple-element.36) | data formatting | bytes 3145728
  77.3 3.0 %fusion.23 = bf16[2,256,2,768]{1,3,2,0:T(8,128)(2,1)S(1)} fusion(bf16[2,2,256,768]{2,3,0,1:T(8,128)(2,1)} %copy.126, f32[2,768]{1,0:T(2,128)S(1)} %fusion.74, bf16[256,2,2,768]{3,1,2,0:T(2,128)(2,1)S(1)} %bitcast.171, bf16[4,256,256]{2,1,0:T(8,128)(2,1)} %param.13), kind=kOutput, calls=%fused_computation.30 | convolution fusion | flops 411303936 | bytes 4986880 | tf_op jit(solution)/shard_map/jpa,ajid->jpid/dot_general | solution.py:62
  83.3 3.9 %reshape.51 = bf16[64,4,2,2,768]{4,1,0,3,2:T(4,128)(2,1)} reshape(bf16[256,2,2,768]{3,0,2,1:T(8,128)(2,1)} %fusion.41) | data formatting | bytes 3145728 | tf_op jit(solution)/shard_map/reshape | solution.py:70
  87.2 3.1 %fusion.59 = f32[2,256,256]{2,1,0:T(8,128)} fusion(bf16[2,256,2,768]{1,3,2,0:T(8,128)(2,1)} %copy-done.3, bf16[256,2,2,768]{3,1,2,0:T(2,128)(2,1)S(1)} %bitcast.172), kind=kOutput, calls=%fused_computation.53 | convolution fusion | flops 402653184 | bytes 3670016 | tf_op jit(solution)/shard_map/jpid,ajid->jpa/dot_general | solution.py:68
  90.3 2.8 %copy.82 = bf16[64,4,2,2,768]{4,2,3,1,0:T(2,128)(2,1)} copy(bf16[64,4,2,2,768]{4,1,0,3,2:T(4,128)(2,1)S(1)} %copy-done.4) | data formatting | bytes 3145728 | tf_op jit(solution)/shard_map/optimization_barrier | solution.py:74
  93.0 14.9 %all-to-all-done.2 = bf16[64,4,2,2,768]{4,2,3,1,0:T(2,128)(2,1)S(1)} async-done(((bf16[64,4,2,2,768]{4,2,3,1,0:T(2,128)(2,1)}), bf16[64,4,2,2,768]{4,2,3,1,0:T(2,128)(2,1)S(1)}, u32[]{:S(2)}, u32[]{:S(2)}) %all-to-all-start.2) | async-done | bytes 1572896 | tf_op jit(solution)/shard_map/all_to_all | solution.py:55
  108.0 9.1 %all-to-all-start.1 = ((bf16[64,4,2,2,768]{4,2,3,1,0:T(2,128)(2,1)}), bf16[64,4,2,2,768]{4,2,3,1,0:T(2,128)(2,1)}, u32[]{:S(2)}, u32[]{:S(2)}) async-start(bf16[64,4,2,2,768]{4,2,3,1,0:T(2,128)(2,1)} %copy.82), calls=%async_computation.1 | async-start | bytes 3145728 | tf_op jit(solution)/shard_map/all_to_all | solution.py:78
  118.7 2.4 %collective-permute-start = (f32[2,256,256]{2,1,0:T(8,128)}, f32[2,256,256]{2,1,0:T(8,128)S(1)}, u32[]{:S(2)}, u32[]{:S(2)}) collective-permute-start(f32[2,256,256]{2,1,0:T(8,128)} %fusion.59), channel_id=1, source_target_pairs={{0,64},{64,0},{128,192},{192,128},{1,65},{65,1},{129,193},{193,129... | collective-permute-start | bytes 1572872 | tf_op jit(solution)/shard_map/ppermute | solution.py:22
  121.1 3.0 %fusion.13 = bf16[2,256,2,768]{1,3,2,0:T(8,128)(2,1)S(1)} fusion(bf16[2,2,256,768]{2,3,0,1:T(8,128)(2,1)} %copy.128, f32[2,768]{1,0:T(2,128)S(1)} %fusion.74, bf16[256,2,2,768]{3,1,2,0:T(2,128)(2,1)S(1)} %bitcast.169, bf16[4,256,256]{2,1,0:T(8,128)(2,1)} %param.13), kind=kOutput, calls=%fused_computation.17 | convolution fusion | flops 411303936 | bytes 4986880 | tf_op jit(solution)/shard_map/jpa,ajid->jpid/dot_general | solution.py:62
  127.0 3.9 %reshape.53 = bf16[64,4,2,2,768]{4,1,0,3,2:T(4,128)(2,1)} reshape(bf16[256,2,2,768]{3,0,2,1:T(8,128)(2,1)} %fusion.42) | data formatting | bytes 3145728 | tf_op jit(solution)/shard_map/reshape | solution.py:70
  130.9 6.4 %collective-permute-done.1 = f32[1,256,256]{2,1,0:T(8,128)} collective-permute-done((f32[1,256,256]{2,1,0:T(8,128)}, f32[1,256,256]{2,1,0:T(8,128)}, u32[]{:S(2)}, u32[]{:S(2)}) %collective-permute-start.1) | collective-permute-done | bytes 262176 | tf_op jit(solution)/shard_map/ppermute | solution.py:27
  141.1 2.8 %copy.93 = bf16[64,4,2,2,768]{4,2,3,1,0:T(2,128)(2,1)} copy(bf16[64,4,2,2,768]{4,1,0,3,2:T(4,128)(2,1)S(1)} %copy-done.2) | data formatting | bytes 3145728 | tf_op jit(solution)/shard_map/optimization_barrier | solution.py:72
  143.9 10.0 %all-to-all-done.1 = bf16[64,4,2,2,768]{4,2,3,1,0:T(2,128)(2,1)} async-done(((bf16[64,4,2,2,768]{4,2,3,1,0:T(2,128)(2,1)}), bf16[64,4,2,2,768]{4,2,3,1,0:T(2,128)(2,1)}, u32[]{:S(2)}, u32[]{:S(2)}) %all-to-all-start.1) | async-done | bytes 1572896 | tf_op jit(solution)/shard_map/all_to_all | solution.py:78
  154.0 8.6 %all-to-all-start.3 = ((bf16[64,4,2,2,768]{4,2,3,1,0:T(2,128)(2,1)}), bf16[64,4,2,2,768]{4,2,3,1,0:T(2,128)(2,1)S(1)}, u32[]{:S(2)}, u32[]{:S(2)}) async-start(bf16[64,4,2,2,768]{4,2,3,1,0:T(2,128)(2,1)} %copy.93), calls=%async_computation.3 | async-start | bytes 3145728 | tf_op jit(solution)/shard_map/all_to_all | solution.py:78
  162.6 3.6 %fusion.49 = f32[4,64,2,256]{3,1,2,0:T(8,128)S(1)} fusion(bf16[64,4,2,2,768]{4,2,3,1,0:T(2,128)(2,1)} %all-to-all-done.1, f32[2,768]{1,0:T(2,128)S(1)} %fusion.73, bf16[2,4,256,768]{3,2,1,0:T(8,128)(2,1)} %bitcast.182), kind=kOutput, calls=%fused_computation.51 | convolution fusion | flops 407371776 | bytes 5249024 | tf_op jit(solution)/shard_map/sajid,iabd->asjb/dot_general | solution.py:85
  166.2 3.3 %collective-permute-start.3 = (f32[4,64,2,256]{3,1,2,0:T(8,128)S(1)}, f32[4,64,2,256]{3,1,2,0:T(8,128)S(1)}, u32[]{:S(2)}, u32[]{:S(2)}) collective-permute-start(f32[4,64,2,256]{3,1,2,0:T(8,128)S(1)} %fusion.49), channel_id=1, source_target_pairs={{0,64},{64,0},{128,192},{192,128},{1,65},{65,1},{129,193},{193,129... | collective-permute-start | bytes 1572872 | tf_op jit(solution)/shard_map/ppermute | solution.py:22
  172.8 10.2 %collective-permute-done.4 = f32[2,64,2,256]{3,1,2,0:T(8,128)S(1)} collective-permute-done((f32[2,64,2,256]{3,1,2,0:T(8,128)S(1)}, f32[2,64,2,256]{3,1,2,0:T(8,128)S(1)}, u32[]{:S(2)}, u32[]{:S(2)}) %collective-permute-start.4) | collective-permute-done | bytes 262176 | tf_op jit(solution)/shard_map/ppermute | solution.py:27
  183.0 2.1 collective-permute-start.5
  185.1 8.9 %collective-permute-done.7 = f32[1,256,256]{2,1,0:T(8,128)S(1)} collective-permute-done((f32[1,256,256]{2,1,0:T(8,128)S(1)}, f32[1,256,256]{2,1,0:T(8,128)S(1)}, u32[]{:S(2)}, u32[]{:S(2)}) %collective-permute-start.7) | collective-permute-done | bytes 262176 | tf_op jit(solution)/shard_map/ppermute | solution.py:27
  197.8 3.1 %fusion.54 = f32[4,64,2,256]{3,1,2,0:T(8,128)S(1)} fusion(bf16[64,4,2,2,768]{4,2,3,1,0:T(2,128)(2,1)S(1)} %all-to-all-done.3, f32[2,768]{1,0:T(2,128)S(1)} %fusion.73, bf16[2,4,256,768]{3,2,1,0:T(8,128)(2,1)} %bitcast.183), kind=kOutput, calls=%fused_computation.52 | convolution fusion | flops 407371776 | bytes 5249024 | tf_op jit(solution)/shard_map/sajid,iabd->asjb/dot_general | solution.py:92
  201.0 6.9 %collective-permute-start.9 = (f32[4,64,2,256]{3,1,2,0:T(8,128)S(1)}, f32[4,64,2,256]{3,1,2,0:T(8,128)S(1)}, u32[]{:S(2)}, u32[]{:S(2)}) collective-permute-start(f32[4,64,2,256]{3,1,2,0:T(8,128)S(1)} %fusion.54), channel_id=1, source_target_pairs={{0,64},{64,0},{128,192},{192,128},{1,65},{65,1},{129,193},{193,129... | collective-permute-start | bytes 1572872 | tf_op jit(solution)/shard_map/ppermute | solution.py:22
  210.9 2.5 %fusion.33 = f32[4,2,768,256,1]{2,3,4,1,0:T(8,128)S(1)} fusion(bf16[64,4,2,2,768]{4,2,3,1,0:T(2,128)(2,1)} %all-to-all-done.1, bf16[4,64,2,256]{3,0,2,1:T(4,128)(2,1)S(1)} %copy-done.9), kind=kOutput, calls=%fused_computation.39 | convolution fusion | flops 402653184 | bytes 8126464 | tf_op jit(solution)/shard_map/asjb,sajid->iabd/dot_general | solution.py:95
  214.5 2.7 %collective-permute-done.10 = f32[2,64,2,256]{3,1,2,0:T(8,128)S(1)} collective-permute-done((f32[2,64,2,256]{3,1,2,0:T(8,128)S(1)}, f32[2,64,2,256]{3,1,2,0:T(8,128)S(1)}, u32[]{:S(2)}, u32[]{:S(2)}) %collective-permute-start.10) | collective-permute-done | bytes 262176 | tf_op jit(solution)/shard_map/ppermute | solution.py:27
  220.2 1.9 copy.97
  (75 shorter events, 30.3 us)
Async XLA Ops:
  0.6 1.7 copy-start
  2.3 3.5 %copy-start.8 = (bf16[4,64,2,256]{3,0,2,1:T(4,128)(2,1)}, bf16[4,64,2,256]{3,0,2,1:T(4,128)(2,1)S(1)}, u32[]{:S(2)}) copy-start(bf16[4,64,2,256]{3,0,2,1:T(4,128)(2,1)S(1)} %get-tuple-element.46) | copy-start | bytes 786436
  8.6 53.8 %all-to-all-start = ((bf16[64,4,2,2,768]{4,2,3,1,0:T(2,128)(2,1)}), bf16[64,4,2,2,768]{4,2,3,1,0:T(2,128)(2,1)S(1)}, u32[]{:S(2)}, u32[]{:S(2)}) async-start(bf16[64,4,2,2,768]{4,2,3,1,0:T(2,128)(2,1)} %copy.75), calls=%async_computation | async-start | bytes 3145728 | tf_op jit(solution)/shard_map/all_to_all | solution.py:55
  62.4 45.6 %all-to-all-start.2 = ((bf16[64,4,2,2,768]{4,2,3,1,0:T(2,128)(2,1)}), bf16[64,4,2,2,768]{4,2,3,1,0:T(2,128)(2,1)S(1)}, u32[]{:S(2)}, u32[]{:S(2)}) async-start(bf16[64,4,2,2,768]{4,2,3,1,0:T(2,128)(2,1)} %copy.86), calls=%async_computation.2 | async-start | bytes 3145728 | tf_op jit(solution)/shard_map/all_to_all | solution.py:55
  74.5 2.6 %copy-start.12 = (f32[16,768]{1,0:T(8,128)S(1)}, f32[16,768]{1,0:T(8,128)}, u32[]{:S(2)}) copy-start(f32[16,768]{1,0:T(8,128)} %param.11) | copy-start | bytes 147460
  74.5 2.6 %copy-start.13 = (s32[2]{0:T(128)S(1)}, s32[2]{0:T(128)}, u32[]{:S(2)}) copy-start(s32[2]{0:T(128)} %param.9) | copy-start | bytes 28
  77.3 4.2 %copy-start.10 = (bf16[4,256,256]{2,1,0:T(8,128)(2,1)S(1)}, bf16[4,256,256]{2,1,0:T(8,128)(2,1)}, u32[]{:S(2)}) copy-start(bf16[4,256,256]{2,1,0:T(8,128)(2,1)} %param.13) | copy-start | bytes 1572868
  80.3 1.1 copy-start.3
  87.2 3.1 %copy-start.4 = (bf16[64,4,2,2,768]{4,1,0,3,2:T(4,128)(2,1)S(1)}, bf16[64,4,2,2,768]{4,1,0,3,2:T(4,128)(2,1)}, u32[]{:S(2)}) copy-start(bf16[64,4,2,2,768]{4,1,0,3,2:T(4,128)(2,1)} %reshape.51) | copy-start | bytes 4718596
  90.3 26.8 %copy-start.5 = (bf16[2,2,256,768]{3,2,1,0:T(8,128)(2,1)S(1)}, bf16[2,2,256,768]{3,2,1,0:T(8,128)(2,1)}, u32[]{:S(2)}) copy-start(bf16[2,2,256,768]{3,2,1,0:T(8,128)(2,1)} %get-tuple-element.35) | copy-start | bytes 4718596
  108.0 46.0 %all-to-all-start.1 = ((bf16[64,4,2,2,768]{4,2,3,1,0:T(2,128)(2,1)}), bf16[64,4,2,2,768]{4,2,3,1,0:T(2,128)(2,1)}, u32[]{:S(2)}, u32[]{:S(2)}) async-start(bf16[64,4,2,2,768]{4,2,3,1,0:T(2,128)(2,1)} %copy.82), calls=%async_computation.1 | async-start | bytes 3145728 | tf_op jit(solution)/shard_map/all_to_all | solution.py:78
  118.7 5.4 %collective-permute-start = (f32[2,256,256]{2,1,0:T(8,128)}, f32[2,256,256]{2,1,0:T(8,128)S(1)}, u32[]{:S(2)}, u32[]{:S(2)}) collective-permute-start(f32[2,256,256]{2,1,0:T(8,128)} %fusion.59), channel_id=1, source_target_pairs={{0,64},{64,0},{128,192},{192,128},{1,65},{65,1},{129,193},{193,129... | collective-permute-start | bytes 1572872 | tf_op jit(solution)/shard_map/ppermute | solution.py:22
  121.0 3.1 %copy-start.6 = (f32[2,256,256]{2,1,0:T(8,128)S(1)}, f32[2,256,256]{2,1,0:T(8,128)}, u32[]{:S(2)}) copy-start(f32[2,256,256]{2,1,0:T(8,128)} %fusion.59) | copy-start | bytes 1572868
  121.1 4.2 %copy-start.11 = (bf16[4,256,256]{2,1,0:T(8,128)(2,1)S(1)}, bf16[4,256,256]{2,1,0:T(8,128)(2,1)}, u32[]{:S(2)}) copy-start(bf16[4,256,256]{2,1,0:T(8,128)(2,1)} %param.13) | copy-start | bytes 1572868
  124.9 12.5 %collective-permute-start.1 = (f32[1,256,256]{2,1,0:T(8,128)}, f32[1,256,256]{2,1,0:T(8,128)}, u32[]{:S(2)}, u32[]{:S(2)}) collective-permute-start(f32[1,256,256]{2,1,0:T(8,128)} %dynamic-slice_add_fusion.1), channel_id=1, source_target_pairs={{0,128},{64,192},{128,0},{192,64},{1,129},{65,193},{129,1},{193,65... | collective-permute-start | bytes 786440 | tf_op jit(solution)/shard_map/ppermute | solution.py:27
  130.9 10.2 %copy-start.2 = (bf16[64,4,2,2,768]{4,1,0,3,2:T(4,128)(2,1)S(1)}, bf16[64,4,2,2,768]{4,1,0,3,2:T(4,128)(2,1)}, u32[]{:S(2)}) copy-start(bf16[64,4,2,2,768]{4,1,0,3,2:T(4,128)(2,1)} %reshape.53) | copy-start | bytes 4718596
  138.4 2.6 %collective-permute-start.2 = (f32[1,256,256]{2,1,0:T(8,128)S(1)}, f32[1,256,256]{2,1,0:T(8,128)S(1)}, u32[]{:S(2)}, u32[]{:S(2)}) collective-permute-start(f32[1,256,256]{2,1,0:T(8,128)S(1)} %add.62), channel_id=1, source_target_pairs={{0,64},{64,0},{128,192},{192,128},{1,65},{65,1},{129,193},{193,129... | collective-permute-start | bytes 786440 | tf_op jit(solution)/shard_map/ppermute | solution.py:28
  154.0 43.9 %all-to-all-start.3 = ((bf16[64,4,2,2,768]{4,2,3,1,0:T(2,128)(2,1)}), bf16[64,4,2,2,768]{4,2,3,1,0:T(2,128)(2,1)S(1)}, u32[]{:S(2)}, u32[]{:S(2)}) async-start(bf16[64,4,2,2,768]{4,2,3,1,0:T(2,128)(2,1)} %copy.93), calls=%async_computation.3 | async-start | bytes 3145728 | tf_op jit(solution)/shard_map/all_to_all | solution.py:78
  162.6 6.9 %copy-start.7 = (f32[2,256,256]{2,1,0:T(8,128)S(1)}, f32[2,256,256]{2,1,0:T(8,128)}, u32[]{:S(2)}) copy-start(f32[2,256,256]{2,1,0:T(8,128)} %fusion.62) | copy-start | bytes 1572868
  166.2 4.8 %collective-permute-start.3 = (f32[4,64,2,256]{3,1,2,0:T(8,128)S(1)}, f32[4,64,2,256]{3,1,2,0:T(8,128)S(1)}, u32[]{:S(2)}, u32[]{:S(2)}) collective-permute-start(f32[4,64,2,256]{3,1,2,0:T(8,128)S(1)} %fusion.49), channel_id=1, source_target_pairs={{0,64},{64,0},{128,192},{192,128},{1,65},{65,1},{129,193},{193,129... | collective-permute-start | bytes 1572872 | tf_op jit(solution)/shard_map/ppermute | solution.py:22
  169.5 2.3 %collective-permute-start.6 = (f32[2,256,256]{2,1,0:T(8,128)S(1)}, f32[2,256,256]{2,1,0:T(8,128)S(1)}, u32[]{:S(2)}, u32[]{:S(2)}) collective-permute-start(f32[2,256,256]{2,1,0:T(8,128)S(1)} %copy-done.7), channel_id=1, source_target_pairs={{0,64},{64,0},{128,192},{192,128},{1,65},{65,1},{129,193},{193,129... | collective-permute-start | bytes 1572872 | tf_op jit(solution)/shard_map/ppermute | solution.py:22
  171.1 11.8 %collective-permute-start.4 = (f32[2,64,2,256]{3,1,2,0:T(8,128)S(1)}, f32[2,64,2,256]{3,1,2,0:T(8,128)S(1)}, u32[]{:S(2)}, u32[]{:S(2)}) collective-permute-start(f32[2,64,2,256]{3,1,2,0:T(8,128)S(1)} %dynamic-slice_bitcast_fusion.1), channel_id=1, source_target_pairs={{0,128},{64,192},{128,0},{192,64},{1,129},{65,193},{129,1},{193,65... | collective-permute-start | bytes 786440 | tf_op jit(solution)/shard_map/ppermute | solution.py:27
  171.8 22.2 %collective-permute-start.7 = (f32[1,256,256]{2,1,0:T(8,128)S(1)}, f32[1,256,256]{2,1,0:T(8,128)S(1)}, u32[]{:S(2)}, u32[]{:S(2)}) collective-permute-start(f32[1,256,256]{2,1,0:T(8,128)S(1)} %dynamic-slice_add_fusion), channel_id=1, source_target_pairs={{0,128},{64,192},{128,0},{192,64},{1,129},{65,193},{129,1},{193,65... | collective-permute-start | bytes 786440 | tf_op jit(solution)/shard_map/ppermute | solution.py:27
  183.0 12.2 %collective-permute-start.5 = (f32[2,64,2,256]{3,1,2,0:T(8,128)S(1)}, f32[2,64,2,256]{3,1,2,0:T(8,128)S(1)}, u32[]{:S(2)}, u32[]{:S(2)}) collective-permute-start(f32[2,64,2,256]{3,1,2,0:T(8,128)S(1)} %fusion.85), channel_id=1, source_target_pairs={{0,64},{64,0},{128,192},{192,128},{1,65},{65,1},{129,193},{193,129... | collective-permute-start | bytes 786440 | tf_op jit(solution)/shard_map/ppermute | solution.py:28
  194.0 2.3 %collective-permute-start.8 = (f32[1,256,256]{2,1,0:T(8,128)S(1)}, f32[1,256,256]{2,1,0:T(8,128)S(1)}, u32[]{:S(2)}, u32[]{:S(2)}) collective-permute-start(f32[1,256,256]{2,1,0:T(8,128)S(1)} %add.66), channel_id=1, source_target_pairs={{0,64},{64,0},{128,192},{192,128},{1,65},{65,1},{129,193},{193,129... | collective-permute-start | bytes 786440 | tf_op jit(solution)/shard_map/ppermute | solution.py:28
  197.8 13.1 %copy-start.9 = (bf16[4,64,2,256]{3,0,2,1:T(4,128)(2,1)S(1)}, bf16[4,64,2,256]{3,0,2,1:T(4,128)(2,1)}, u32[]{:S(2)}) copy-start(bf16[4,64,2,256]{3,0,2,1:T(4,128)(2,1)} %copy-done.8) | copy-start | bytes 786436
  201.0 8.4 %collective-permute-start.9 = (f32[4,64,2,256]{3,1,2,0:T(8,128)S(1)}, f32[4,64,2,256]{3,1,2,0:T(8,128)S(1)}, u32[]{:S(2)}, u32[]{:S(2)}) collective-permute-start(f32[4,64,2,256]{3,1,2,0:T(8,128)S(1)} %fusion.54), channel_id=1, source_target_pairs={{0,64},{64,0},{128,192},{192,128},{1,65},{65,1},{129,193},{193,129... | collective-permute-start | bytes 1572872 | tf_op jit(solution)/shard_map/ppermute | solution.py:22
  209.5 7.6 %collective-permute-start.10 = (f32[2,64,2,256]{3,1,2,0:T(8,128)S(1)}, f32[2,64,2,256]{3,1,2,0:T(8,128)S(1)}, u32[]{:S(2)}, u32[]{:S(2)}) collective-permute-start(f32[2,64,2,256]{3,1,2,0:T(8,128)S(1)} %dynamic-slice_bitcast_fusion), channel_id=1, source_target_pairs={{0,128},{64,192},{128,0},{192,64},{1,129},{65,193},{129,1},{193,65... | collective-permute-start | bytes 786440 | tf_op jit(solution)/shard_map/ppermute | solution.py:27
  217.2 4.9 %collective-permute-start.11 = (f32[2,64,2,256]{3,1,2,0:T(8,128)S(1)}, f32[2,64,2,256]{3,1,2,0:T(8,128)S(1)}, u32[]{:S(2)}, u32[]{:S(2)}) collective-permute-start(f32[2,64,2,256]{3,1,2,0:T(8,128)S(1)} %add.69), channel_id=1, source_target_pairs={{0,64},{64,0},{128,192},{192,128},{1,65},{65,1},{129,193},{193,129... | collective-permute-start | bytes 786440 | tf_op jit(solution)/shard_map/ppermute | solution.py:28
  222.1 2.0 copy-start.1

commit v4 on v3

--- a/solution.py
+++ b/solution.py
@@ -19,9 +19,10 @@
     if n_dp != 4 or x.shape[0] % 2:
         return dp_sum(x, n_dp), hold
     core = lax.axis_index("dp") % 2
-    x = x + lax.ppermute(x, "dp", [(i, i ^ 1) for i in range(n_dp)])
     halves = x.reshape((2, x.shape[0] // 2) + x.shape[1:])
     mine = lax.dynamic_index_in_dim(halves, core, 0, keepdims=False)
+    theirs = lax.dynamic_index_in_dim(halves, 1 - core, 0, keepdims=False)
+    mine = mine + lax.ppermute(theirs, "dp", [(i, i ^ 1) for i in range(n_dp)])
     if hold is not None:
         mine, hold = lax.optimization_barrier((mine, hold))
     mine = mine + lax.ppermute(mine, "dp", [(i, i ^ 2) for i in range(n_dp)])

time: 225 us -> 225 us (level)
  transfers between devices with their start and end apart: 16 -> 16, of which waited for: 11 -> 11; matrix products, arithmetic and copies ran while one was open for 24% -> 25% of each run, Pallas kernels for 0% -> 0%
where the time goes in v4:
time: 225 us; the launch traced here: 224 us
  waiting for transfers between devices  90.1 us (40%)
  starting transfers between devices  63.5 us (28%)
  local copies, waits for them, and re-layouts  34.4 us (15%)
  matrix products  31.3 us (14%)
  other arithmetic  3.41 us (2%)
    all_to_all x2, waiting for transfers between devices, on_device(): recv1.append(lax.all_to_all(mixed, 'seq', 0, 0, tiled=True))  48.1 us
    ppermute x4, waiting for transfers between devices, dp_sum_halves(): mine = mine + lax.ppermute(mine, 'dp', [(i, i ^ 2) for i in range(n_dp)])  27.5 us
    all_to_all x2, starting transfers between devices, on_device(): recv1.append(lax.all_to_all(mixed, 'seq', 0, 0, tiled=True))  23.4 us
    all_to_all x2, starting transfers between devices, on_device(): recv2.append(lax.all_to_all(send, 'seq', 0, 0, tiled=True))  17.7 us
    ppermute x4, starting transfers between devices, dp_sum_halves(): mine = mine + lax.ppermute(theirs, 'dp', [(i, i ^ 1) for i in range(n_dp)])  12.7 us
    all_to_all x2, waiting for transfers between devices, on_device(): recv2.append(lax.all_to_all(send, 'seq', 0, 0, tiled=True))  11.2 us
    unnamed x32, local copies, waits for them, and re-layouts  8 us
    reshape x2, local copies, waits for them, and re-layouts, on_device(): send = send.reshape(n_seq, own, per, images, width)  7.76 us
  transfers between devices with their start and end apart: 16, of which 11 were waited for; matrix products, arithmetic and copies ran while one was open for 25% of the time, Pallas kernels for 0%

profile of v4, /device:TPU:1, one launch (start us, length us, event | category | flops | bytes accessed | tf_op | source)
XLA Modules:
  0.0 223.7 jit_solution(10038438583174554443)
XLA Ops:
  3.2 2.6 %fusion.38 = bf16[64,4,2,2,768]{4,0,2,3,1:T(8,128)(2,1)S(1)} fusion(bf16[4,64,2,256]{3,0,2,1:T(4,128)(2,1)S(1)} %get-tuple-element.46, f32[2,768]{1,0:T(2,128)S(1)} %fusion.68, bf16[2,4,256,768]{3,2,1,0:T(8,128)(2,1)} %bitcast.181), kind=kOutput, calls=%fused_computation.42 | convolution fusion | flops 408158208 | bytes 4986880 | tf_op jit(solution)/shard_map/asjb,iabd->sajid/dot_general | solution.py:53
  5.9 2.8 %copy.75 = bf16[64,4,2,2,768]{4,2,3,1,0:T(2,128)(2,1)} copy(bf16[64,4,2,2,768]{4,0,2,3,1:T(8,128)(2,1)S(1)} %fusion.38) | data formatting | bytes 3145728 | tf_op jit(solution)/shard_map/convert_element_type | solution.py:55
  8.6 15.1 %all-to-all-start = ((bf16[64,4,2,2,768]{4,2,3,1,0:T(2,128)(2,1)}), bf16[64,4,2,2,768]{4,2,3,1,0:T(2,128)(2,1)S(1)}, u32[]{:S(2)}, u32[]{:S(2)}) async-start(bf16[64,4,2,2,768]{4,2,3,1,0:T(2,128)(2,1)} %copy.75), calls=%async_computation | async-start | bytes 3145728 | tf_op jit(solution)/shard_map/all_to_all | solution.py:56
  23.7 2.6 %fusion.35 = bf16[64,4,2,2,768]{4,0,2,3,1:T(8,128)(2,1)S(1)} fusion(bf16[4,64,2,256]{3,0,2,1:T(4,128)(2,1)S(1)} %get-tuple-element.45, f32[2,768]{1,0:T(2,128)S(1)} %fusion.68, bf16[2,4,256,768]{3,2,1,0:T(8,128)(2,1)} %bitcast.182), kind=kOutput, calls=%fused_computation.41 | convolution fusion | flops 408158208 | bytes 4986880 | tf_op jit(solution)/shard_map/asjb,iabd->sajid/dot_general | solution.py:53
  26.4 2.8 %copy.86 = bf16[64,4,2,2,768]{4,2,3,1,0:T(2,128)(2,1)} copy(bf16[64,4,2,2,768]{4,0,2,3,1:T(8,128)(2,1)S(1)} %fusion.35) | data formatting | bytes 3145728 | tf_op jit(solution)/shard_map/convert_element_type | solution.py:55
  29.2 33.2 %all-to-all-done = bf16[64,4,2,2,768]{4,2,3,1,0:T(2,128)(2,1)S(1)} async-done(((bf16[64,4,2,2,768]{4,2,3,1,0:T(2,128)(2,1)}), bf16[64,4,2,2,768]{4,2,3,1,0:T(2,128)(2,1)S(1)}, u32[]{:S(2)}, u32[]{:S(2)}) %all-to-all-start) | async-done | bytes 1572896 | tf_op jit(solution)/shard_map/all_to_all | solution.py:56
  62.4 8.3 %all-to-all-start.2 = ((bf16[64,4,2,2,768]{4,2,3,1,0:T(2,128)(2,1)}), bf16[64,4,2,2,768]{4,2,3,1,0:T(2,128)(2,1)S(1)}, u32[]{:S(2)}, u32[]{:S(2)}) async-start(bf16[64,4,2,2,768]{4,2,3,1,0:T(2,128)(2,1)} %copy.86), calls=%async_computation.2 | async-start | bytes 3145728 | tf_op jit(solution)/shard_map/all_to_all | solution.py:56
  70.7 3.8 %fusion.72 = (bf16[2,2,256,768]{3,2,1,0:T(8,128)(2,1)}, bf16[2,2,256,768]{3,2,1,0:T(8,128)(2,1)}) fusion(bf16[2,4,256,768]{3,2,1,0:T(8,128)(2,1)} %bitcast.174), kind=kLoop, calls=%fused_computation.90 | loop fusion | bytes 6291456 | tf_op jit(solution)/shard_map/slice | solution.py:65
  74.5 2.6 %copy.126 = bf16[2,2,256,768]{2,3,0,1:T(8,128)(2,1)} copy(bf16[2,2,256,768]{3,2,1,0:T(8,128)(2,1)} %get-tuple-element.36) | data formatting | bytes 3145728
  77.3 3.0 %fusion.23 = bf16[2,256,2,768]{1,3,2,0:T(8,128)(2,1)S(1)} fusion(bf16[2,2,256,768]{2,3,0,1:T(8,128)(2,1)} %copy.126, f32[2,768]{1,0:T(2,128)S(1)} %fusion.69, bf16[256,2,2,768]{3,1,2,0:T(2,128)(2,1)S(1)} %bitcast.171, bf16[4,256,256]{2,1,0:T(8,128)(2,1)} %param.13), kind=kOutput, calls=%fused_computation.30 | convolution fusion | flops 411303936 | bytes 4986880 | tf_op jit(solution)/shard_map/jpa,ajid->jpid/dot_general | solution.py:63
  83.3 3.9 %reshape.55 = bf16[64,4,2,2,768]{4,1,0,3,2:T(4,128)(2,1)} reshape(bf16[256,2,2,768]{3,0,2,1:T(8,128)(2,1)} %fusion.41) | data formatting | bytes 3145728 | tf_op jit(solution)/shard_map/reshape | solution.py:71
  87.2 3.1 %fusion.54 = f32[2,256,256]{2,1,0:T(8,128)} fusion(bf16[2,256,2,768]{1,3,2,0:T(8,128)(2,1)} %copy-done.3, bf16[256,2,2,768]{3,1,2,0:T(2,128)(2,1)S(1)} %bitcast.172), kind=kOutput, calls=%fused_computation.52 | convolution fusion | flops 402653184 | bytes 3670016 | tf_op jit(solution)/shard_map/jpid,ajid->jpa/dot_general | solution.py:69
  90.3 2.8 %copy.82 = bf16[64,4,2,2,768]{4,2,3,1,0:T(2,128)(2,1)} copy(bf16[64,4,2,2,768]{4,1,0,3,2:T(4,128)(2,1)S(1)} %copy-done.4) | data formatting | bytes 3145728 | tf_op jit(solution)/shard_map/optimization_barrier | solution.py:75
  93.0 14.9 %all-to-all-done.2 = bf16[64,4,2,2,768]{4,2,3,1,0:T(2,128)(2,1)S(1)} async-done(((bf16[64,4,2,2,768]{4,2,3,1,0:T(2,128)(2,1)}), bf16[64,4,2,2,768]{4,2,3,1,0:T(2,128)(2,1)S(1)}, u32[]{:S(2)}, u32[]{:S(2)}) %all-to-all-start.2) | async-done | bytes 1572896 | tf_op jit(solution)/shard_map/all_to_all | solution.py:56
  108.0 9.1 %all-to-all-start.1 = ((bf16[64,4,2,2,768]{4,2,3,1,0:T(2,128)(2,1)}), bf16[64,4,2,2,768]{4,2,3,1,0:T(2,128)(2,1)}, u32[]{:S(2)}, u32[]{:S(2)}) async-start(bf16[64,4,2,2,768]{4,2,3,1,0:T(2,128)(2,1)} %copy.82), calls=%async_computation.1 | async-start | bytes 3145728 | tf_op jit(solution)/shard_map/all_to_all | solution.py:79
  119.7 2.5 %collective-permute-start = (f32[1,256,256]{2,1,0:T(8,128)S(1)}, f32[1,256,256]{2,1,0:T(8,128)S(1)}, u32[]{:S(2)}, u32[]{:S(2)}) collective-permute-start(f32[1,256,256]{2,1,0:T(8,128)S(1)} %constant_dynamic-slice_fusion.1), channel_id=1, source_target_pairs={{0,64},{64,0},{128,192},{192,128},{1,65},{65,1},{129,193},{193,129... | collective-permute-start | bytes 786440 | tf_op jit(solution)/shard_map/ppermute | solution.py:25
  122.1 3.0 %fusion.13 = bf16[2,256,2,768]{1,3,2,0:T(8,128)(2,1)S(1)} fusion(bf16[2,2,256,768]{2,3,0,1:T(8,128)(2,1)} %copy.128, f32[2,768]{1,0:T(2,128)S(1)} %fusion.69, bf16[256,2,2,768]{3,1,2,0:T(2,128)(2,1)S(1)} %bitcast.169, bf16[4,256,256]{2,1,0:T(8,128)(2,1)} %param.13), kind=kOutput, calls=%fused_computation.17 | convolution fusion | flops 411303936 | bytes 4986880 | tf_op jit(solution)/shard_map/jpa,ajid->jpid/dot_general | solution.py:63
  128.1 3.9 %reshape.57 = bf16[64,4,2,2,768]{4,1,0,3,2:T(4,128)(2,1)} reshape(bf16[256,2,2,768]{3,0,2,1:T(8,128)(2,1)} %fusion.42) | data formatting | bytes 3145728 | tf_op jit(solution)/shard_map/reshape | solution.py:71
  132.0 6.0 %collective-permute-done.1 = f32[1,256,256]{2,1,0:T(8,128)} collective-permute-done((f32[1,256,256]{2,1,0:T(8,128)}, f32[1,256,256]{2,1,0:T(8,128)}, u32[]{:S(2)}, u32[]{:S(2)}) %collective-permute-start.1) | collective-permute-done | bytes 262176 | tf_op jit(solution)/shard_map/ppermute | solution.py:28
  141.9 2.8 %copy.93 = bf16[64,4,2,2,768]{4,2,3,1,0:T(2,128)(2,1)} copy(bf16[64,4,2,2,768]{4,1,0,3,2:T(4,128)(2,1)S(1)} %copy-done.2) | data formatting | bytes 3145728 | tf_op jit(solution)/shard_map/optimization_barrier | solution.py:73
  144.6 9.3 %all-to-all-done.1 = bf16[64,4,2,2,768]{4,2,3,1,0:T(2,128)(2,1)} async-done(((bf16[64,4,2,2,768]{4,2,3,1,0:T(2,128)(2,1)}), bf16[64,4,2,2,768]{4,2,3,1,0:T(2,128)(2,1)}, u32[]{:S(2)}, u32[]{:S(2)}) %all-to-all-start.1) | async-done | bytes 1572896 | tf_op jit(solution)/shard_map/all_to_all | solution.py:79
  154.0 8.6 %all-to-all-start.3 = ((bf16[64,4,2,2,768]{4,2,3,1,0:T(2,128)(2,1)}), bf16[64,4,2,2,768]{4,2,3,1,0:T(2,128)(2,1)S(1)}, u32[]{:S(2)}, u32[]{:S(2)}) async-start(bf16[64,4,2,2,768]{4,2,3,1,0:T(2,128)(2,1)} %copy.93), calls=%async_computation.3 | async-start | bytes 3145728 | tf_op jit(solution)/shard_map/all_to_all | solution.py:79
  162.6 3.6 %fusion.49 = f32[4,64,2,256]{3,1,2,0:T(8,128)S(1)} fusion(bf16[64,4,2,2,768]{4,2,3,1,0:T(2,128)(2,1)} %all-to-all-done.1, f32[2,768]{1,0:T(2,128)S(1)} %fusion.68, bf16[2,4,256,768]{3,2,1,0:T(8,128)(2,1)} %bitcast.183), kind=kOutput, calls=%fused_computation.51 | convolution fusion | flops 407371776 | bytes 5249024 | tf_op jit(solution)/shard_map/sajid,iabd->asjb/dot_general | solution.py:86
  166.3 3.3 %collective-permute-start.6 = (f32[1,256,256]{2,1,0:T(8,128)S(1)}, f32[1,256,256]{2,1,0:T(8,128)S(1)}, u32[]{:S(2)}, u32[]{:S(2)}) collective-permute-start(f32[1,256,256]{2,1,0:T(8,128)S(1)} %constant_dynamic-slice_fusion), channel_id=1, source_target_pairs={{0,64},{64,0},{128,192},{192,128},{1,65},{65,1},{129,193},{193,129... | collective-permute-start | bytes 786440 | tf_op jit(solution)/shard_map/ppermute | solution.py:25
  172.4 10.1 %collective-permute-done.7 = f32[1,256,256]{2,1,0:T(8,128)S(1)} collective-permute-done((f32[1,256,256]{2,1,0:T(8,128)S(1)}, f32[1,256,256]{2,1,0:T(8,128)S(1)}, u32[]{:S(2)}, u32[]{:S(2)}) %collective-permute-start.7) | collective-permute-done | bytes 262176 | tf_op jit(solution)/shard_map/ppermute | solution.py:28
  182.5 2.2 collective-permute-start.8
  184.7 8.8 %collective-permute-done.4 = f32[2,64,2,256]{3,1,2,0:T(8,128)S(1)} collective-permute-done((f32[2,64,2,256]{3,1,2,0:T(8,128)S(1)}, f32[2,64,2,256]{3,1,2,0:T(8,128)S(1)}, u32[]{:S(2)}, u32[]{:S(2)}) %collective-permute-start.4) | collective-permute-done | bytes 262176 | tf_op jit(solution)/shard_map/ppermute | solution.py:28
  197.8 3.1 %fusion.4 = f32[4,64,2,256,1]{3,1,4,2,0:T(8,128)S(1)} fusion(bf16[64,4,2,2,768]{4,2,3,1,0:T(2,128)(2,1)S(1)} %all-to-all-done.3, f32[2,768]{1,0:T(2,128)S(1)} %fusion.68, bf16[2,4,256,768]{3,2,1,0:T(8,128)(2,1)} %bitcast.184), kind=kOutput, calls=%fused_computation.6 | convolution fusion | flops 407371776 | bytes 5249024 | tf_op jit(solution)/shard_map/sajid,iabd->asjb/dot_general | solution.py:93
  201.0 6.9 %collective-permute-start.9 = (f32[2,64,2,256]{3,1,2,0:T(8,128)S(1)}, f32[2,64,2,256]{3,1,2,0:T(8,128)S(1)}, u32[]{:S(2)}, u32[]{:S(2)}) collective-permute-start(f32[2,64,2,256]{3,1,2,0:T(8,128)S(1)} %dynamic-slice_bitcast_fusion), channel_id=1, source_target_pairs={{0,64},{64,0},{128,192},{192,128},{1,65},{65,1},{129,193},{193,129... | collective-permute-start | bytes 786440 | tf_op jit(solution)/shard_map/ppermute | solution.py:25
  210.5 2.5 %fusion.33 = f32[4,2,768,256,1]{2,3,4,1,0:T(8,128)S(1)} fusion(bf16[64,4,2,2,768]{4,2,3,1,0:T(2,128)(2,1)} %all-to-all-done.1, bf16[4,64,2,256]{3,0,2,1:T(4,128)(2,1)S(1)} %copy-done.9), kind=kOutput, calls=%fused_computation.39 | convolution fusion | flops 402653184 | bytes 8126464 | tf_op jit(solution)/shard_map/asjb,sajid->iabd/dot_general | solution.py:96
  214.1 2.7 %collective-permute-done.10 = f32[2,64,2,256]{3,1,2,0:T(8,128)S(1)} collective-permute-done((f32[2,64,2,256]{3,1,2,0:T(8,128)S(1)}, f32[2,64,2,256]{3,1,2,0:T(8,128)S(1)}, u32[]{:S(2)}, u32[]{:S(2)}) %collective-permute-start.10) | collective-permute-done | bytes 262176 | tf_op jit(solution)/shard_map/ppermute | solution.py:28
  219.8 1.9 copy.97
  (77 shorter events, 31.0 us)
Async XLA Ops:
  0.6 1.7 copy-start
  2.3 3.5 %copy-start.8 = (bf16[4,64,2,256]{3,0,2,1:T(4,128)(2,1)}, bf16[4,64,2,256]{3,0,2,1:T(4,128)(2,1)S(1)}, u32[]{:S(2)}) copy-start(bf16[4,64,2,256]{3,0,2,1:T(4,128)(2,1)S(1)} %get-tuple-element.46) | copy-start | bytes 786436
  8.6 53.8 %all-to-all-start = ((bf16[64,4,2,2,768]{4,2,3,1,0:T(2,128)(2,1)}), bf16[64,4,2,2,768]{4,2,3,1,0:T(2,128)(2,1)S(1)}, u32[]{:S(2)}, u32[]{:S(2)}) async-start(bf16[64,4,2,2,768]{4,2,3,1,0:T(2,128)(2,1)} %copy.75), calls=%async_computation | async-start | bytes 3145728 | tf_op jit(solution)/shard_map/all_to_all | solution.py:56
  62.4 45.6 %all-to-all-start.2 = ((bf16[64,4,2,2,768]{4,2,3,1,0:T(2,128)(2,1)}), bf16[64,4,2,2,768]{4,2,3,1,0:T(2,128)(2,1)S(1)}, u32[]{:S(2)}, u32[]{:S(2)}) async-start(bf16[64,4,2,2,768]{4,2,3,1,0:T(2,128)(2,1)} %copy.86), calls=%async_computation.2 | async-start | bytes 3145728 | tf_op jit(solution)/shard_map/all_to_all | solution.py:56
  74.5 2.6 %copy-start.12 = (f32[16,768]{1,0:T(8,128)S(1)}, f32[16,768]{1,0:T(8,128)}, u32[]{:S(2)}) copy-start(f32[16,768]{1,0:T(8,128)} %param.11) | copy-start | bytes 147460
  74.5 2.6 %copy-start.13 = (s32[2]{0:T(128)S(1)}, s32[2]{0:T(128)}, u32[]{:S(2)}) copy-start(s32[2]{0:T(128)} %param.9) | copy-start | bytes 28
  77.3 4.2 %copy-start.10 = (bf16[4,256,256]{2,1,0:T(8,128)(2,1)S(1)}, bf16[4,256,256]{2,1,0:T(8,128)(2,1)}, u32[]{:S(2)}) copy-start(bf16[4,256,256]{2,1,0:T(8,128)(2,1)} %param.13) | copy-start | bytes 1572868
  80.3 1.1 copy-start.3
  87.2 3.1 %copy-start.4 = (bf16[64,4,2,2,768]{4,1,0,3,2:T(4,128)(2,1)S(1)}, bf16[64,4,2,2,768]{4,1,0,3,2:T(4,128)(2,1)}, u32[]{:S(2)}) copy-start(bf16[64,4,2,2,768]{4,1,0,3,2:T(4,128)(2,1)} %reshape.55) | copy-start | bytes 4718596
  90.3 26.8 %copy-start.5 = (bf16[2,2,256,768]{3,2,1,0:T(8,128)(2,1)S(1)}, bf16[2,2,256,768]{3,2,1,0:T(8,128)(2,1)}, u32[]{:S(2)}) copy-start(bf16[2,2,256,768]{3,2,1,0:T(8,128)(2,1)} %get-tuple-element.35) | copy-start | bytes 4718596
  108.0 46.0 %all-to-all-start.1 = ((bf16[64,4,2,2,768]{4,2,3,1,0:T(2,128)(2,1)}), bf16[64,4,2,2,768]{4,2,3,1,0:T(2,128)(2,1)}, u32[]{:S(2)}, u32[]{:S(2)}) async-start(bf16[64,4,2,2,768]{4,2,3,1,0:T(2,128)(2,1)} %copy.82), calls=%async_computation.1 | async-start | bytes 3145728 | tf_op jit(solution)/shard_map/all_to_all | solution.py:79
  119.7 5.5 %collective-permute-start = (f32[1,256,256]{2,1,0:T(8,128)S(1)}, f32[1,256,256]{2,1,0:T(8,128)S(1)}, u32[]{:S(2)}, u32[]{:S(2)}) collective-permute-start(f32[1,256,256]{2,1,0:T(8,128)S(1)} %constant_dynamic-slice_fusion.1), channel_id=1, source_target_pairs={{0,64},{64,0},{128,192},{192,128},{1,65},{65,1},{129,193},{193,129... | collective-permute-start | bytes 786440 | tf_op jit(solution)/shard_map/ppermute | solution.py:25
  122.1 3.1 %copy-start.6 = (f32[2,256,256]{2,1,0:T(8,128)S(1)}, f32[2,256,256]{2,1,0:T(8,128)}, u32[]{:S(2)}) copy-start(f32[2,256,256]{2,1,0:T(8,128)} %fusion.54) | copy-start | bytes 1572868
  122.1 4.2 %copy-start.11 = (bf16[4,256,256]{2,1,0:T(8,128)(2,1)S(1)}, bf16[4,256,256]{2,1,0:T(8,128)(2,1)}, u32[]{:S(2)}) copy-start(bf16[4,256,256]{2,1,0:T(8,128)(2,1)} %param.13) | copy-start | bytes 1572868
  125.9 12.1 %collective-permute-start.1 = (f32[1,256,256]{2,1,0:T(8,128)}, f32[1,256,256]{2,1,0:T(8,128)}, u32[]{:S(2)}, u32[]{:S(2)}) collective-permute-start(f32[1,256,256]{2,1,0:T(8,128)} %dynamic-slice_add_fusion.1), channel_id=1, source_target_pairs={{0,128},{64,192},{128,0},{192,64},{1,129},{65,193},{129,1},{193,65... | collective-permute-start | bytes 786440 | tf_op jit(solution)/shard_map/ppermute | solution.py:28
  132.0 9.9 %copy-start.2 = (bf16[64,4,2,2,768]{4,1,0,3,2:T(4,128)(2,1)S(1)}, bf16[64,4,2,2,768]{4,1,0,3,2:T(4,128)(2,1)}, u32[]{:S(2)}) copy-start(bf16[64,4,2,2,768]{4,1,0,3,2:T(4,128)(2,1)} %reshape.57) | copy-start | bytes 4718596
  139.1 2.7 %collective-permute-start.2 = (f32[1,256,256]{2,1,0:T(8,128)S(1)}, f32[1,256,256]{2,1,0:T(8,128)S(1)}, u32[]{:S(2)}, u32[]{:S(2)}) collective-permute-start(f32[1,256,256]{2,1,0:T(8,128)S(1)} %add.70), channel_id=1, source_target_pairs={{0,64},{64,0},{128,192},{192,128},{1,65},{65,1},{129,193},{193,129... | collective-permute-start | bytes 786440 | tf_op jit(solution)/shard_map/ppermute | solution.py:29
  154.0 43.9 %all-to-all-start.3 = ((bf16[64,4,2,2,768]{4,2,3,1,0:T(2,128)(2,1)}), bf16[64,4,2,2,768]{4,2,3,1,0:T(2,128)(2,1)S(1)}, u32[]{:S(2)}, u32[]{:S(2)}) async-start(bf16[64,4,2,2,768]{4,2,3,1,0:T(2,128)(2,1)} %copy.93), calls=%async_computation.3 | async-start | bytes 3145728 | tf_op jit(solution)/shard_map/all_to_all | solution.py:79
  162.6 3.6 %copy-start.7 = (f32[2,256,256]{2,1,0:T(8,128)S(1)}, f32[2,256,256]{2,1,0:T(8,128)}, u32[]{:S(2)}) copy-start(f32[2,256,256]{2,1,0:T(8,128)} %fusion.57) | copy-start | bytes 1572868
  166.3 4.4 %collective-permute-start.6 = (f32[1,256,256]{2,1,0:T(8,128)S(1)}, f32[1,256,256]{2,1,0:T(8,128)S(1)}, u32[]{:S(2)}, u32[]{:S(2)}) collective-permute-start(f32[1,256,256]{2,1,0:T(8,128)S(1)} %constant_dynamic-slice_fusion), channel_id=1, source_target_pairs={{0,64},{64,0},{128,192},{192,128},{1,65},{65,1},{129,193},{193,129... | collective-permute-start | bytes 786440 | tf_op jit(solution)/shard_map/ppermute | solution.py:25
  169.5 1.8 collective-permute-start.3
  170.7 11.8 %collective-permute-start.7 = (f32[1,256,256]{2,1,0:T(8,128)S(1)}, f32[1,256,256]{2,1,0:T(8,128)S(1)}, u32[]{:S(2)}, u32[]{:S(2)}) collective-permute-start(f32[1,256,256]{2,1,0:T(8,128)S(1)} %dynamic-slice_add_fusion), channel_id=1, source_target_pairs={{0,128},{64,192},{128,0},{192,64},{1,129},{65,193},{129,1},{193,65... | collective-permute-start | bytes 786440 | tf_op jit(solution)/shard_map/ppermute | solution.py:28
  171.3 22.1 %collective-permute-start.4 = (f32[2,64,2,256]{3,1,2,0:T(8,128)S(1)}, f32[2,64,2,256]{3,1,2,0:T(8,128)S(1)}, u32[]{:S(2)}, u32[]{:S(2)}) collective-permute-start(f32[2,64,2,256]{3,1,2,0:T(8,128)S(1)} %bitcast_add_fusion.2), channel_id=1, source_target_pairs={{0,128},{64,192},{128,0},{192,64},{1,129},{65,193},{129,1},{193,65... | collective-permute-start | bytes 786440 | tf_op jit(solution)/shard_map/ppermute | solution.py:28
  182.5 12.2 %collective-permute-start.8 = (f32[1,256,256]{2,1,0:T(8,128)S(1)}, f32[1,256,256]{2,1,0:T(8,128)S(1)}, u32[]{:S(2)}, u32[]{:S(2)}) collective-permute-start(f32[1,256,256]{2,1,0:T(8,128)S(1)} %add.74), channel_id=1, source_target_pairs={{0,64},{64,0},{128,192},{192,128},{1,65},{65,1},{129,193},{193,129... | collective-permute-start | bytes 786440 | tf_op jit(solution)/shard_map/ppermute | solution.py:29
  193.5 2.4 %collective-permute-start.5 = (f32[2,64,2,256]{3,1,2,0:T(8,128)S(1)}, f32[2,64,2,256]{3,1,2,0:T(8,128)S(1)}, u32[]{:S(2)}, u32[]{:S(2)}) collective-permute-start(f32[2,64,2,256]{3,1,2,0:T(8,128)S(1)} %add.72), channel_id=1, source_target_pairs={{0,64},{64,0},{128,192},{192,128},{1,65},{65,1},{129,193},{193,129... | collective-permute-start | bytes 786440 | tf_op jit(solution)/shard_map/ppermute | solution.py:29
  197.8 12.7 %copy-start.9 = (bf16[4,64,2,256]{3,0,2,1:T(4,128)(2,1)S(1)}, bf16[4,64,2,256]{3,0,2,1:T(4,128)(2,1)}, u32[]{:S(2)}) copy-start(bf16[4,64,2,256]{3,0,2,1:T(4,128)(2,1)} %copy-done.8) | copy-start | bytes 786436
  201.0 8.1 %collective-permute-start.9 = (f32[2,64,2,256]{3,1,2,0:T(8,128)S(1)}, f32[2,64,2,256]{3,1,2,0:T(8,128)S(1)}, u32[]{:S(2)}, u32[]{:S(2)}) collective-permute-start(f32[2,64,2,256]{3,1,2,0:T(8,128)S(1)} %dynamic-slice_bitcast_fusion), channel_id=1, source_target_pairs={{0,64},{64,0},{128,192},{192,128},{1,65},{65,1},{129,193},{193,129... | collective-permute-start | bytes 786440 | tf_op jit(solution)/shard_map/ppermute | solution.py:25
  209.1 7.6 %collective-permute-start.10 = (f32[2,64,2,256]{3,1,2,0:T(8,128)S(1)}, f32[2,64,2,256]{3,1,2,0:T(8,128)S(1)}, u32[]{:S(2)}, u32[]{:S(2)}) collective-permute-start(f32[2,64,2,256]{3,1,2,0:T(8,128)S(1)} %bitcast_add_fusion.1), channel_id=1, source_target_pairs={{0,128},{64,192},{128,0},{192,64},{1,129},{65,193},{129,1},{193,65... | collective-permute-start | bytes 786440 | tf_op jit(solution)/shard_map/ppermute | solution.py:28
  216.8 4.9 %collective-permute-start.11 = (f32[2,64,2,256]{3,1,2,0:T(8,128)S(1)}, f32[2,64,2,256]{3,1,2,0:T(8,128)S(1)}, u32[]{:S(2)}, u32[]{:S(2)}) collective-permute-start(f32[2,64,2,256]{3,1,2,0:T(8,128)S(1)} %add.77), channel_id=1, source_target_pairs={{0,64},{64,0},{128,192},{192,128},{1,65},{65,1},{129,193},{193,129... | collective-permute-start | bytes 786440 | tf_op jit(solution)/shard_map/ppermute | solution.py:29
  221.7 2.0 copy-start.1

commit v5 on v3

--- a/solution.py
+++ b/solution.py
@@ -52,7 +52,10 @@
         mixed = jnp.einsum(
             "asjb,iabd->sajid", f1[:, :, k * per:(k + 1) * per, :], scaled, preferred_element_type=f32
         ).astype(bf16)
-        recv1.append(lax.all_to_all(mixed, "seq", 0, 0, tiled=True))
+        flat = mixed.reshape(n_seq, own * per * images, width)
+        recv1.append(
+            lax.all_to_all(flat, "seq", 0, 0, tiled=True).reshape(n_seq, own, per, images, width)
+        )
 
     recv2 = []
     sfg = []

time: 225 us -> 224 us (level)
  waiting for transfers between devices: 91.8 us -> 88.4 us
    convert_element_type x2, local copies, waits for them, and re-layouts: 5.57 us -> 0.27 us  [on_device(): mixed = jnp.einsum('asjb,iabd->sajid', f1[:, :, k * per:(k + 1) * per, :]...]
    reshape x0 -> x2, local copies, waits for them, and re-layouts: none -> 4.06 us  [on_device(): flat = mixed.reshape(n_seq, own * per * images, width)]
    unnamed x32 -> x34, local copies, waits for them, and re-layouts: 8 us -> 8 us
  transfers between devices with their start and end apart: 16 -> 16, of which waited for: 11 -> 11; matrix products, arithmetic and copies ran while one was open for 24% -> 25% of each run, Pallas kernels for 0% -> 0%
where the time goes in v5:
time: 224 us; the launch traced here: 223 us
  waiting for transfers between devices  88.4 us (39%)
  starting transfers between devices  63.5 us (28%)
  local copies, waits for them, and re-layouts  34.3 us (15%)
  matrix products  31.9 us (14%)
  other arithmetic  4.43 us (2%)
    all_to_all x2, waiting for transfers between devices, on_device(): lax.all_to_all(flat, 'seq', 0, 0, tiled=True)  46.7 us
    ppermute x4, waiting for transfers between devices, dp_sum_halves(): mine = mine + lax.ppermute(mine, 'dp', [(i, i ^ 2) for i in range(n_dp)])  27.7 us
    all_to_all x2, starting transfers between devices, on_device(): lax.all_to_all(flat, 'seq', 0, 0, tiled=True)  23.5 us
    all_to_all x2, starting transfers between devices, on_device(): recv2.append(lax.all_to_all(send, 'seq', 0, 0, tiled=True))  17.7 us
    ppermute x4, starting transfers between devices, dp_sum_halves(): x = x + lax.ppermute(x, 'dp', [(i, i ^ 1) for i in range(n_dp)])  12.6 us
    all_to_all x2, waiting for transfers between devices, on_device(): recv2.append(lax.all_to_all(send, 'seq', 0, 0, tiled=True))  9.9 us
    unnamed x34, local copies, waits for them, and re-layouts  8 us
    reshape x2, local copies, waits for them, and re-layouts, on_device(): send = send.reshape(n_seq, own, per, images, width)  7.75 us
  transfers between devices with their start and end apart: 16, of which 11 were waited for; matrix products, arithmetic and copies ran while one was open for 25% of the time, Pallas kernels for 0%

profile of v5, /device:TPU:1, one launch (start us, length us, event | category | flops | bytes accessed | tf_op | source)
XLA Modules:
  0.0 223.5 jit_solution(18336905462993660394)
XLA Ops:
  3.2 2.6 %fusion.38 = bf16[64,4,2,2,768]{4,0,2,3,1:T(8,128)(2,1)S(1)} fusion(bf16[4,64,2,256]{3,0,2,1:T(4,128)(2,1)S(1)} %get-tuple-element.46, f32[2,768]{1,0:T(2,128)S(1)} %fusion.73, bf16[2,4,256,768]{3,2,1,0:T(8,128)(2,1)} %bitcast.174), kind=kOutput, calls=%fused_computation.42 | convolution fusion | flops 408158208 | bytes 4986880 | tf_op jit(solution)/shard_map/asjb,iabd->sajid/dot_general | solution.py:52
  6.0 2.0 copy.80
  8.0 15.1 %all-to-all-start = ((bf16[64,16,768]{2,1,0:T(8,128)(2,1)}), bf16[64,16,768]{2,1,0:T(8,128)(2,1)S(1)}, u32[]{:S(2)}, u32[]{:S(2)}) async-start(bf16[64,16,768]{2,1,0:T(8,128)(2,1)} %copy.80), calls=%async_computation | async-start | bytes 3145728 | tf_op jit(solution)/shard_map/all_to_all | solution.py:57
  23.1 2.6 %fusion.35 = bf16[64,4,2,2,768]{4,0,2,3,1:T(8,128)(2,1)S(1)} fusion(bf16[4,64,2,256]{3,0,2,1:T(4,128)(2,1)S(1)} %get-tuple-element.45, f32[2,768]{1,0:T(2,128)S(1)} %fusion.73, bf16[2,4,256,768]{3,2,1,0:T(8,128)(2,1)} %bitcast.175), kind=kOutput, calls=%fused_computation.41 | convolution fusion | flops 408158208 | bytes 4986880 | tf_op jit(solution)/shard_map/asjb,iabd->sajid/dot_general | solution.py:52
  25.9 2.1 copy.91
  28.0 33.8 %all-to-all-done = bf16[64,16,768]{2,1,0:T(8,128)(2,1)S(1)} async-done(((bf16[64,16,768]{2,1,0:T(8,128)(2,1)}), bf16[64,16,768]{2,1,0:T(8,128)(2,1)S(1)}, u32[]{:S(2)}, u32[]{:S(2)}) %all-to-all-start) | async-done | bytes 1572896 | tf_op jit(solution)/shard_map/all_to_all | solution.py:57
  61.8 8.3 %all-to-all-start.2 = ((bf16[64,16,768]{2,1,0:T(8,128)(2,1)}), bf16[64,16,768]{2,1,0:T(8,128)(2,1)S(1)}, u32[]{:S(2)}, u32[]{:S(2)}) async-start(bf16[64,16,768]{2,1,0:T(8,128)(2,1)} %copy.91), calls=%async_computation.2 | async-start | bytes 3145728 | tf_op jit(solution)/shard_map/all_to_all | solution.py:57
  70.1 3.8 %fusion.77 = (bf16[2,2,256,768]{3,2,1,0:T(8,128)(2,1)}, bf16[2,2,256,768]{3,2,1,0:T(8,128)(2,1)}) fusion(bf16[2,4,256,768]{3,2,1,0:T(8,128)(2,1)} %bitcast.168), kind=kLoop, calls=%fused_computation.87 | loop fusion | bytes 6291456 | tf_op jit(solution)/shard_map/slice | solution.py:67
  73.9 2.6 %copy.126 = bf16[2,2,256,768]{2,3,0,1:T(8,128)(2,1)} copy(bf16[2,2,256,768]{3,2,1,0:T(8,128)(2,1)} %get-tuple-element.36) | data formatting | bytes 3145728
  78.2 3.7 %fusion.23 = bf16[2,256,2,768]{1,3,2,0:T(8,128)(2,1)S(1)} fusion(bf16[2,2,256,768]{2,3,0,1:T(8,128)(2,1)} %copy.126, f32[2,768]{1,0:T(2,128)S(1)} %fusion.74, bf16[256,2,2,768]{3,2,1,0:T(2,128)(2,1)} %reshape_reshape.6, bf16[4,256,256]{2,1,0:T(8,128)(2,1)} %param.13), kind=kOutput, calls=%fused_computation.30 | convolution fusion | flops 411303936 | bytes 4986880 | tf_op jit(solution)/shard_map/jpa,ajid->jpid/dot_general | solution.py:65
  84.8 3.9 %reshape.51 = bf16[64,4,2,2,768]{4,1,0,3,2:T(4,128)(2,1)} reshape(bf16[256,2,2,768]{3,0,2,1:T(8,128)(2,1)} %fusion.41) | data formatting | bytes 3145728 | tf_op jit(solution)/shard_map/reshape | solution.py:73
  88.7 3.1 %fusion.59 = f32[2,256,256]{2,1,0:T(8,128)} fusion(bf16[2,256,2,768]{1,3,2,0:T(8,128)(2,1)} %copy-done.4, bf16[256,2,2,768]{3,2,1,0:T(2,128)(2,1)S(1)} %copy-done.3), kind=kOutput, calls=%fused_computation.53 | convolution fusion | flops 402653184 | bytes 3670016 | tf_op jit(solution)/shard_map/jpid,ajid->jpa/dot_general | solution.py:71
  91.7 2.8 %copy.86 = bf16[64,4,2,2,768]{4,2,3,1,0:T(2,128)(2,1)} copy(bf16[64,4,2,2,768]{4,1,0,3,2:T(4,128)(2,1)S(1)} %copy-done.5) | data formatting | bytes 3145728 | tf_op jit(solution)/shard_map/optimization_barrier | solution.py:77
  94.5 12.9 %all-to-all-done.2 = bf16[64,16,768]{2,1,0:T(8,128)(2,1)S(1)} async-done(((bf16[64,16,768]{2,1,0:T(8,128)(2,1)}), bf16[64,16,768]{2,1,0:T(8,128)(2,1)S(1)}, u32[]{:S(2)}, u32[]{:S(2)}) %all-to-all-start.2) | async-done | bytes 1572896 | tf_op jit(solution)/shard_map/all_to_all | solution.py:57
  107.4 9.1 %all-to-all-start.1 = ((bf16[64,4,2,2,768]{4,2,3,1,0:T(2,128)(2,1)}), bf16[64,4,2,2,768]{4,2,3,1,0:T(2,128)(2,1)}, u32[]{:S(2)}, u32[]{:S(2)}) async-start(bf16[64,4,2,2,768]{4,2,3,1,0:T(2,128)(2,1)} %copy.86), calls=%async_computation.1 | async-start | bytes 3145728 | tf_op jit(solution)/shard_map/all_to_all | solution.py:81
  118.1 2.4 %collective-permute-start = (f32[2,256,256]{2,1,0:T(8,128)}, f32[2,256,256]{2,1,0:T(8,128)}, u32[]{:S(2)}, u32[]{:S(2)}) collective-permute-start(f32[2,256,256]{2,1,0:T(8,128)} %fusion.59), channel_id=1, source_target_pairs={{0,64},{64,0},{128,192},{192,128},{1,65},{65,1},{129,193},{193,129... | collective-permute-start | bytes 1572872 | tf_op jit(solution)/shard_map/ppermute | solution.py:22
  121.1 3.1 %fusion.13 = bf16[2,256,2,768]{1,3,2,0:T(8,128)(2,1)S(1)} fusion(bf16[2,2,256,768]{2,3,0,1:T(8,128)(2,1)} %copy.128, f32[2,768]{1,0:T(2,128)S(1)} %fusion.74, bf16[256,2,2,768]{3,2,1,0:T(2,128)(2,1)S(1)} %reshape_reshape.7, bf16[4,256,256]{2,1,0:T(8,128)(2,1)} %param.13), kind=kOutput, calls=%fused_computation.17 | convolution fusion | flops 411303936 | bytes 4986880 | tf_op jit(solution)/shard_map/jpa,ajid->jpid/dot_general | solution.py:65
  128.0 3.9 %reshape.53 = bf16[64,4,2,2,768]{4,1,0,3,2:T(4,128)(2,1)} reshape(bf16[256,2,2,768]{3,0,2,1:T(8,128)(2,1)} %fusion.42) | data formatting | bytes 3145728 | tf_op jit(solution)/shard_map/reshape | solution.py:73
  131.9 6.0 %collective-permute-done.1 = f32[1,256,256]{2,1,0:T(8,128)} collective-permute-done((f32[1,256,256]{2,1,0:T(8,128)}, f32[1,256,256]{2,1,0:T(8,128)}, u32[]{:S(2)}, u32[]{:S(2)}) %collective-permute-start.1) | collective-permute-done | bytes 262176 | tf_op jit(solution)/shard_map/ppermute | solution.py:27
  142.1 2.8 %copy.97 = bf16[64,4,2,2,768]{4,2,3,1,0:T(2,128)(2,1)} copy(bf16[64,4,2,2,768]{4,1,0,3,2:T(4,128)(2,1)S(1)} %copy-done.2) | data formatting | bytes 3145728 | tf_op jit(solution)/shard_map/optimization_barrier | solution.py:75
  144.9 8.5 %all-to-all-done.1 = bf16[64,4,2,2,768]{4,2,3,1,0:T(2,128)(2,1)} async-done(((bf16[64,4,2,2,768]{4,2,3,1,0:T(2,128)(2,1)}), bf16[64,4,2,2,768]{4,2,3,1,0:T(2,128)(2,1)}, u32[]{:S(2)}, u32[]{:S(2)}) %all-to-all-start.1) | async-done | bytes 1572896 | tf_op jit(solution)/shard_map/all_to_all | solution.py:81
  153.3 8.6 %all-to-all-start.3 = ((bf16[64,4,2,2,768]{4,2,3,1,0:T(2,128)(2,1)}), bf16[64,4,2,2,768]{4,2,3,1,0:T(2,128)(2,1)S(1)}, u32[]{:S(2)}, u32[]{:S(2)}) async-start(bf16[64,4,2,2,768]{4,2,3,1,0:T(2,128)(2,1)} %copy.97), calls=%async_computation.3 | async-start | bytes 3145728 | tf_op jit(solution)/shard_map/all_to_all | solution.py:81
  162.0 3.6 %fusion.49 = f32[4,64,2,256]{3,1,2,0:T(8,128)S(1)} fusion(bf16[64,4,2,2,768]{4,2,3,1,0:T(2,128)(2,1)} %all-to-all-done.1, f32[2,768]{1,0:T(2,128)S(1)} %fusion.73, bf16[2,4,256,768]{3,2,1,0:T(8,128)(2,1)} %bitcast.176), kind=kOutput, calls=%fused_computation.51 | convolution fusion | flops 407371776 | bytes 5249024 | tf_op jit(solution)/shard_map/sajid,iabd->asjb/dot_general | solution.py:88
  165.6 3.3 %collective-permute-start.3 = (f32[4,64,2,256]{3,1,2,0:T(8,128)S(1)}, f32[4,64,2,256]{3,1,2,0:T(8,128)S(1)}, u32[]{:S(2)}, u32[]{:S(2)}) collective-permute-start(f32[4,64,2,256]{3,1,2,0:T(8,128)S(1)} %fusion.49), channel_id=1, source_target_pairs={{0,64},{64,0},{128,192},{192,128},{1,65},{65,1},{129,193},{193,129... | collective-permute-start | bytes 1572872 | tf_op jit(solution)/shard_map/ppermute | solution.py:22
  172.2 10.2 %collective-permute-done.4 = f32[2,64,2,256]{3,1,2,0:T(8,128)S(1)} collective-permute-done((f32[2,64,2,256]{3,1,2,0:T(8,128)S(1)}, f32[2,64,2,256]{3,1,2,0:T(8,128)S(1)}, u32[]{:S(2)}, u32[]{:S(2)}) %collective-permute-start.4) | collective-permute-done | bytes 262176 | tf_op jit(solution)/shard_map/ppermute | solution.py:27
  182.4 2.1 collective-permute-start.5
  184.5 8.9 %collective-permute-done.7 = f32[1,256,256]{2,1,0:T(8,128)S(1)} collective-permute-done((f32[1,256,256]{2,1,0:T(8,128)S(1)}, f32[1,256,256]{2,1,0:T(8,128)S(1)}, u32[]{:S(2)}, u32[]{:S(2)}) %collective-permute-start.7) | collective-permute-done | bytes 262176 | tf_op jit(solution)/shard_map/ppermute | solution.py:27
  197.2 3.1 %fusion.54 = f32[4,64,2,256]{3,1,2,0:T(8,128)S(1)} fusion(bf16[64,4,2,2,768]{4,2,3,1,0:T(2,128)(2,1)S(1)} %all-to-all-done.3, f32[2,768]{1,0:T(2,128)S(1)} %fusion.73, bf16[2,4,256,768]{3,2,1,0:T(8,128)(2,1)} %bitcast.177), kind=kOutput, calls=%fused_computation.52 | convolution fusion | flops 407371776 | bytes 5249024 | tf_op jit(solution)/shard_map/sajid,iabd->asjb/dot_general | solution.py:95
  200.4 6.9 %collective-permute-start.9 = (f32[4,64,2,256]{3,1,2,0:T(8,128)S(1)}, f32[4,64,2,256]{3,1,2,0:T(8,128)S(1)}, u32[]{:S(2)}, u32[]{:S(2)}) collective-permute-start(f32[4,64,2,256]{3,1,2,0:T(8,128)S(1)} %fusion.54), channel_id=1, source_target_pairs={{0,64},{64,0},{128,192},{192,128},{1,65},{65,1},{129,193},{193,129... | collective-permute-start | bytes 1572872 | tf_op jit(solution)/shard_map/ppermute | solution.py:22
  210.3 2.5 %fusion.33 = f32[4,2,768,256,1]{2,3,4,1,0:T(8,128)S(1)} fusion(bf16[64,4,2,2,768]{4,2,3,1,0:T(2,128)(2,1)} %all-to-all-done.1, bf16[4,64,2,256]{3,0,2,1:T(4,128)(2,1)S(1)} %copy-done.10), kind=kOutput, calls=%fused_computation.39 | convolution fusion | flops 402653184 | bytes 8126464 | tf_op jit(solution)/shard_map/asjb,sajid->iabd/dot_general | solution.py:98
  213.9 2.7 %collective-permute-done.10 = f32[2,64,2,256]{3,1,2,0:T(8,128)S(1)} collective-permute-done((f32[2,64,2,256]{3,1,2,0:T(8,128)S(1)}, f32[2,64,2,256]{3,1,2,0:T(8,128)S(1)}, u32[]{:S(2)}, u32[]{:S(2)}) %collective-permute-start.10) | collective-permute-done | bytes 262176 | tf_op jit(solution)/shard_map/ppermute | solution.py:27
  219.6 1.9 copy.101
  (81 shorter events, 34.0 us)
Async XLA Ops:
  0.6 1.7 copy-start
  2.3 3.5 %copy-start.9 = (bf16[4,64,2,256]{3,0,2,1:T(4,128)(2,1)}, bf16[4,64,2,256]{3,0,2,1:T(4,128)(2,1)S(1)}, u32[]{:S(2)}) copy-start(bf16[4,64,2,256]{3,0,2,1:T(4,128)(2,1)S(1)} %get-tuple-element.46) | copy-start | bytes 786436
  8.0 53.8 %all-to-all-start = ((bf16[64,16,768]{2,1,0:T(8,128)(2,1)}), bf16[64,16,768]{2,1,0:T(8,128)(2,1)S(1)}, u32[]{:S(2)}, u32[]{:S(2)}) async-start(bf16[64,16,768]{2,1,0:T(8,128)(2,1)} %copy.80), calls=%async_computation | async-start | bytes 3145728 | tf_op jit(solution)/shard_map/all_to_all | solution.py:57
  61.8 45.6 %all-to-all-start.2 = ((bf16[64,16,768]{2,1,0:T(8,128)(2,1)}), bf16[64,16,768]{2,1,0:T(8,128)(2,1)S(1)}, u32[]{:S(2)}, u32[]{:S(2)}) async-start(bf16[64,16,768]{2,1,0:T(8,128)(2,1)} %copy.91), calls=%async_computation.2 | async-start | bytes 3145728 | tf_op jit(solution)/shard_map/all_to_all | solution.py:57
  73.9 2.6 %copy-start.13 = (f32[16,768]{1,0:T(8,128)S(1)}, f32[16,768]{1,0:T(8,128)}, u32[]{:S(2)}) copy-start(f32[16,768]{1,0:T(8,128)} %param.11) | copy-start | bytes 147460
  73.9 2.6 %copy-start.14 = (s32[2]{0:T(128)S(1)}, s32[2]{0:T(128)}, u32[]{:S(2)}) copy-start(s32[2]{0:T(128)} %param.9) | copy-start | bytes 28
  78.2 4.8 %copy-start.11 = (bf16[4,256,256]{2,1,0:T(8,128)(2,1)S(1)}, bf16[4,256,256]{2,1,0:T(8,128)(2,1)}, u32[]{:S(2)}) copy-start(bf16[4,256,256]{2,1,0:T(8,128)(2,1)} %param.13) | copy-start | bytes 1572868
  81.8 1.1 copy-start.4
  83.0 5.7 %copy-start.3 = (bf16[256,2,2,768]{3,2,1,0:T(2,128)(2,1)S(1)}, bf16[256,2,2,768]{3,2,1,0:T(2,128)(2,1)}, u32[]{:S(2)}) copy-start(bf16[256,2,2,768]{3,2,1,0:T(2,128)(2,1)} %reshape_reshape.6) | copy-start | bytes 4718596
  88.7 3.1 %copy-start.5 = (bf16[64,4,2,2,768]{4,1,0,3,2:T(4,128)(2,1)S(1)}, bf16[64,4,2,2,768]{4,1,0,3,2:T(4,128)(2,1)}, u32[]{:S(2)}) copy-start(bf16[64,4,2,2,768]{4,1,0,3,2:T(4,128)(2,1)} %reshape.51) | copy-start | bytes 4718596
  91.7 24.8 %copy-start.6 = (bf16[2,2,256,768]{3,2,1,0:T(8,128)(2,1)S(1)}, bf16[2,2,256,768]{3,2,1,0:T(8,128)(2,1)}, u32[]{:S(2)}) copy-start(bf16[2,2,256,768]{3,2,1,0:T(8,128)(2,1)} %get-tuple-element.35) | copy-start | bytes 4718596
  107.4 46.0 %all-to-all-start.1 = ((bf16[64,4,2,2,768]{4,2,3,1,0:T(2,128)(2,1)}), bf16[64,4,2,2,768]{4,2,3,1,0:T(2,128)(2,1)}, u32[]{:S(2)}, u32[]{:S(2)}) async-start(bf16[64,4,2,2,768]{4,2,3,1,0:T(2,128)(2,1)} %copy.86), calls=%async_computation.1 | async-start | bytes 3145728 | tf_op jit(solution)/shard_map/all_to_all | solution.py:81
  118.1 6.1 %collective-permute-start = (f32[2,256,256]{2,1,0:T(8,128)}, f32[2,256,256]{2,1,0:T(8,128)}, u32[]{:S(2)}, u32[]{:S(2)}) collective-permute-start(f32[2,256,256]{2,1,0:T(8,128)} %fusion.59), channel_id=1, source_target_pairs={{0,64},{64,0},{128,192},{192,128},{1,65},{65,1},{129,193},{193,129... | collective-permute-start | bytes 1572872 | tf_op jit(solution)/shard_map/ppermute | solution.py:22
  121.1 3.1 %copy-start.7 = (f32[2,256,256]{2,1,0:T(8,128)S(1)}, f32[2,256,256]{2,1,0:T(8,128)}, u32[]{:S(2)}) copy-start(f32[2,256,256]{2,1,0:T(8,128)} %fusion.59) | copy-start | bytes 1572868
  121.1 5.2 %copy-start.12 = (bf16[4,256,256]{2,1,0:T(8,128)(2,1)S(1)}, bf16[4,256,256]{2,1,0:T(8,128)(2,1)}, u32[]{:S(2)}) copy-start(bf16[4,256,256]{2,1,0:T(8,128)(2,1)} %param.13) | copy-start | bytes 1572868
  125.9 12.0 %collective-permute-start.1 = (f32[1,256,256]{2,1,0:T(8,128)}, f32[1,256,256]{2,1,0:T(8,128)}, u32[]{:S(2)}, u32[]{:S(2)}) collective-permute-start(f32[1,256,256]{2,1,0:T(8,128)} %dynamic-slice_add_fusion.1), channel_id=1, source_target_pairs={{0,128},{64,192},{128,0},{192,64},{1,129},{65,193},{129,1},{193,65... | collective-permute-start | bytes 786440 | tf_op jit(solution)/shard_map/ppermute | solution.py:27
  131.9 10.2 %copy-start.2 = (bf16[64,4,2,2,768]{4,1,0,3,2:T(4,128)(2,1)S(1)}, bf16[64,4,2,2,768]{4,1,0,3,2:T(4,128)(2,1)}, u32[]{:S(2)}) copy-start(bf16[64,4,2,2,768]{4,1,0,3,2:T(4,128)(2,1)} %reshape.53) | copy-start | bytes 4718596
  139.0 3.0 %collective-permute-start.2 = (f32[1,256,256]{2,1,0:T(8,128)S(1)}, f32[1,256,256]{2,1,0:T(8,128)S(1)}, u32[]{:S(2)}, u32[]{:S(2)}) collective-permute-start(f32[1,256,256]{2,1,0:T(8,128)S(1)} %add.62), channel_id=1, source_target_pairs={{0,64},{64,0},{128,192},{192,128},{1,65},{65,1},{129,193},{193,129... | collective-permute-start | bytes 786440 | tf_op jit(solution)/shard_map/ppermute | solution.py:28
  153.3 43.9 %all-to-all-start.3 = ((bf16[64,4,2,2,768]{4,2,3,1,0:T(2,128)(2,1)}), bf16[64,4,2,2,768]{4,2,3,1,0:T(2,128)(2,1)S(1)}, u32[]{:S(2)}, u32[]{:S(2)}) async-start(bf16[64,4,2,2,768]{4,2,3,1,0:T(2,128)(2,1)} %copy.97), calls=%async_computation.3 | async-start | bytes 3145728 | tf_op jit(solution)/shard_map/all_to_all | solution.py:81
  162.0 6.9 %copy-start.8 = (f32[2,256,256]{2,1,0:T(8,128)S(1)}, f32[2,256,256]{2,1,0:T(8,128)}, u32[]{:S(2)}) copy-start(f32[2,256,256]{2,1,0:T(8,128)} %fusion.62) | copy-start | bytes 1572868
  165.6 4.8 %collective-permute-start.3 = (f32[4,64,2,256]{3,1,2,0:T(8,128)S(1)}, f32[4,64,2,256]{3,1,2,0:T(8,128)S(1)}, u32[]{:S(2)}, u32[]{:S(2)}) collective-permute-start(f32[4,64,2,256]{3,1,2,0:T(8,128)S(1)} %fusion.49), channel_id=1, source_target_pairs={{0,64},{64,0},{128,192},{192,128},{1,65},{65,1},{129,193},{193,129... | collective-permute-start | bytes 1572872 | tf_op jit(solution)/shard_map/ppermute | solution.py:22
  168.9 2.3 %collective-permute-start.6 = (f32[2,256,256]{2,1,0:T(8,128)S(1)}, f32[2,256,256]{2,1,0:T(8,128)S(1)}, u32[]{:S(2)}, u32[]{:S(2)}) collective-permute-start(f32[2,256,256]{2,1,0:T(8,128)S(1)} %copy-done.8), channel_id=1, source_target_pairs={{0,64},{64,0},{128,192},{192,128},{1,65},{65,1},{129,193},{193,129... | collective-permute-start | bytes 1572872 | tf_op jit(solution)/shard_map/ppermute | solution.py:22
  170.5 11.8 %collective-permute-start.4 = (f32[2,64,2,256]{3,1,2,0:T(8,128)S(1)}, f32[2,64,2,256]{3,1,2,0:T(8,128)S(1)}, u32[]{:S(2)}, u32[]{:S(2)}) collective-permute-start(f32[2,64,2,256]{3,1,2,0:T(8,128)S(1)} %dynamic-slice_bitcast_fusion.1), channel_id=1, source_target_pairs={{0,128},{64,192},{128,0},{192,64},{1,129},{65,193},{129,1},{193,65... | collective-permute-start | bytes 786440 | tf_op jit(solution)/shard_map/ppermute | solution.py:27
  171.2 22.2 %collective-permute-start.7 = (f32[1,256,256]{2,1,0:T(8,128)S(1)}, f32[1,256,256]{2,1,0:T(8,128)S(1)}, u32[]{:S(2)}, u32[]{:S(2)}) collective-permute-start(f32[1,256,256]{2,1,0:T(8,128)S(1)} %dynamic-slice_add_fusion), channel_id=1, source_target_pairs={{0,128},{64,192},{128,0},{192,64},{1,129},{65,193},{129,1},{193,65... | collective-permute-start | bytes 786440 | tf_op jit(solution)/shard_map/ppermute | solution.py:27
  182.4 12.2 %collective-permute-start.5 = (f32[2,64,2,256]{3,1,2,0:T(8,128)S(1)}, f32[2,64,2,256]{3,1,2,0:T(8,128)S(1)}, u32[]{:S(2)}, u32[]{:S(2)}) collective-permute-start(f32[2,64,2,256]{3,1,2,0:T(8,128)S(1)} %fusion.85), channel_id=1, source_target_pairs={{0,64},{64,0},{128,192},{192,128},{1,65},{65,1},{129,193},{193,129... | collective-permute-start | bytes 786440 | tf_op jit(solution)/shard_map/ppermute | solution.py:28
  193.4 2.3 %collective-permute-start.8 = (f32[1,256,256]{2,1,0:T(8,128)S(1)}, f32[1,256,256]{2,1,0:T(8,128)S(1)}, u32[]{:S(2)}, u32[]{:S(2)}) collective-permute-start(f32[1,256,256]{2,1,0:T(8,128)S(1)} %add.66), channel_id=1, source_target_pairs={{0,64},{64,0},{128,192},{192,128},{1,65},{65,1},{129,193},{193,129... | collective-permute-start | bytes 786440 | tf_op jit(solution)/shard_map/ppermute | solution.py:28
  197.2 13.1 %copy-start.10 = (bf16[4,64,2,256]{3,0,2,1:T(4,128)(2,1)S(1)}, bf16[4,64,2,256]{3,0,2,1:T(4,128)(2,1)}, u32[]{:S(2)}) copy-start(bf16[4,64,2,256]{3,0,2,1:T(4,128)(2,1)} %copy-done.9) | copy-start | bytes 786436
  200.4 8.4 %collective-permute-start.9 = (f32[4,64,2,256]{3,1,2,0:T(8,128)S(1)}, f32[4,64,2,256]{3,1,2,0:T(8,128)S(1)}, u32[]{:S(2)}, u32[]{:S(2)}) collective-permute-start(f32[4,64,2,256]{3,1,2,0:T(8,128)S(1)} %fusion.54), channel_id=1, source_target_pairs={{0,64},{64,0},{128,192},{192,128},{1,65},{65,1},{129,193},{193,129... | collective-permute-start | bytes 1572872 | tf_op jit(solution)/shard_map/ppermute | solution.py:22
  208.9 7.6 %collective-permute-start.10 = (f32[2,64,2,256]{3,1,2,0:T(8,128)S(1)}, f32[2,64,2,256]{3,1,2,0:T(8,128)S(1)}, u32[]{:S(2)}, u32[]{:S(2)}) collective-permute-start(f32[2,64,2,256]{3,1,2,0:T(8,128)S(1)} %dynamic-slice_bitcast_fusion), channel_id=1, source_target_pairs={{0,128},{64,192},{128,0},{192,64},{1,129},{65,193},{129,1},{193,65... | collective-permute-start | bytes 786440 | tf_op jit(solution)/shard_map/ppermute | solution.py:27
  216.6 4.9 %collective-permute-start.11 = (f32[2,64,2,256]{3,1,2,0:T(8,128)S(1)}, f32[2,64,2,256]{3,1,2,0:T(8,128)S(1)}, u32[]{:S(2)}, u32[]{:S(2)}) collective-permute-start(f32[2,64,2,256]{3,1,2,0:T(8,128)S(1)} %add.69), channel_id=1, source_target_pairs={{0,64},{64,0},{128,192},{192,128},{1,65},{65,1},{129,193},{193,129... | collective-permute-start | bytes 786440 | tf_op jit(solution)/shard_map/ppermute | solution.py:28
  221.5 2.0 copy-start.1

commit v6 on v5

--- a/solution.py
+++ b/solution.py
@@ -93,16 +93,37 @@
         else:
             got, grad_one[:], sfg[:] = lax.optimization_barrier((got, list(grad_one), list(sfg)))
             part = jnp.einsum("sajid,iabd->asjb", got, scaled, preferred_element_type=f32)
+            if n_dp == 4 and own % 2 == 0:
+                core = lax.axis_index("dp") % 2
+                x = part + lax.ppermute(part, "dp", [(i, i ^ 1) for i in range(n_dp)])
+                halves = x.reshape((2, x.shape[0] // 2) + x.shape[1:])
+                mine = lax.dynamic_index_in_dim(halves, core, 0, keepdims=False)
+                mine, got = lax.optimization_barrier((mine, got))
+                mine = mine + lax.ppermute(mine, "dp", [(i, i ^ 2) for i in range(n_dp)])
+                term = jnp.einsum(
+                    "asjb,sajid->iabd", f1[:, :, k * per:, :], got, preferred_element_type=f32
+                )
+                back_sum = back_sum + term
+                grad_inputs = (
+                    (back_sum * gate_in[:, None, None, :]).astype(bf16).reshape(images, rows, width)
+                )
+                mine, grad_inputs = lax.optimization_barrier((mine, grad_inputs))
+                other = lax.ppermute(mine, "dp", [(i, i ^ 1) for i in range(n_dp)])
+                first = jnp.where(core == 0, mine, other)
+                second = jnp.where(core == 0, other, mine)
+                grad_one.append(jnp.concatenate([first, second], axis=0))
+                break
             reduced, got = dp_sum_halves(part, n_dp, hold=got)
             grad_one.append(reduced)
         term = jnp.einsum(
             "asjb,sajid->iabd", f1[:, :, k * per:(k + 1) * per, :], got, preferred_element_type=f32
         )
         back_sum = term if back_sum is None else back_sum + term
+    else:
+        grad_inputs = (
+            (back_sum * gate_in[:, None, None, :]).astype(bf16).reshape(images, rows, width)
+        )
     grad_one = jnp.concatenate(grad_one, axis=2).reshape(own, blocks, blocks)
-    grad_inputs = (
-        (back_sum * gate_in[:, None, None, :]).astype(bf16).reshape(images, rows, width)
-    )
     second_factor_gradient = jnp.concatenate(sfg, axis=0)
     return (grad_inputs, grad_one, second_factor_gradient)
 

time: 224 us -> 223 us (level)
    ppermute x0 -> x3, starting transfers between devices: none -> 9.45 us  [the longest x1 6.91 us: on_device(): x = part + lax.ppermute(part, 'dp', [(i, i ^ 1) for i in range(n_dp)])]
    ppermute x4 -> x3, starting transfers between devices: 12.6 us -> 5.73 us  [dp_sum_halves(): x = x + lax.ppermute(x, 'dp', [(i, i ^ 1) for i in range(n_dp)])]
    ppermute x0 -> x3, waiting for transfers between devices: none -> 3.37 us  [the longest x1 3.25 us: on_device(): mine = mine + lax.ppermute(mine, 'dp', [(i, i ^ 2) for i in range(n_dp)])]
    ppermute x4 -> x3, waiting for transfers between devices: 27.7 us -> 25.6 us  [dp_sum_halves(): mine = mine + lax.ppermute(mine, 'dp', [(i, i ^ 2) for i in range(n_dp)])]
    ppermute x4 -> x3, starting transfers between devices: 6.29 us -> 4.32 us  [dp_sum_halves(): other = lax.ppermute(mine, 'dp', [(i, i ^ 1) for i in range(n_dp)])]
  transfers between devices with their start and end apart: 16 -> 16, of which waited for: 11 -> 11; matrix products, arithmetic and copies ran while one was open for 25% -> 26% of each run, Pallas kernels for 0% -> 0%
where the time goes in v6:
time: 223 us; the launch traced here: 222 us
  waiting for transfers between devices  87.9 us (39%)
  starting transfers between devices  62.7 us (28%)
  local copies, waits for them, and re-layouts  34.3 us (15%)
  matrix products  32 us (14%)
  other arithmetic  4.43 us (2%)
    all_to_all x2, waiting for transfers between devices, on_device(): lax.all_to_all(flat, 'seq', 0, 0, tiled=True)  46.7 us
    ppermute x3, waiting for transfers between devices, dp_sum_halves(): mine = mine + lax.ppermute(mine, 'dp', [(i, i ^ 2) for i in range(n_dp)])  25.6 us
    all_to_all x2, starting transfers between devices, on_device(): lax.all_to_all(flat, 'seq', 0, 0, tiled=True)  23.5 us
    all_to_all x2, starting transfers between devices, on_device(): recv2.append(lax.all_to_all(send, 'seq', 0, 0, tiled=True))  17.7 us
    all_to_all x2, waiting for transfers between devices, on_device(): recv2.append(lax.all_to_all(send, 'seq', 0, 0, tiled=True))  9.62 us
    unnamed x34, local copies, waits for them, and re-layouts  8.01 us
    reshape x2, local copies, waits for them, and re-layouts, on_device(): send = send.reshape(n_seq, own, per, images, width)  7.76 us
    ppermute x1, starting transfers between devices, on_device(): x = part + lax.ppermute(part, 'dp', [(i, i ^ 1) for i in range(n_dp)])  6.91 us
  transfers between devices with their start and end apart: 16, of which 11 were waited for; matrix products, arithmetic and copies ran while one was open for 26% of the time, Pallas kernels for 0%

profile of v6, /device:TPU:1, one launch (start us, length us, event | category | flops | bytes accessed | tf_op | source)
XLA Modules:
  0.0 222.2 jit_solution(5535275538479243994)
XLA Ops:
  3.2 2.6 %fusion.35 = bf16[64,4,2,2,768]{4,0,2,3,1:T(8,128)(2,1)S(1)} fusion(bf16[4,64,2,256]{3,0,2,1:T(4,128)(2,1)S(1)} %get-tuple-element.49, f32[2,768]{1,0:T(2,128)S(1)} %fusion.73, bf16[2,4,256,768]{3,2,1,0:T(8,128)(2,1)} %bitcast.174), kind=kOutput, calls=%fused_computation.41 | convolution fusion | flops 408158208 | bytes 4986880 | tf_op jit(solution)/shard_map/asjb,iabd->sajid/dot_general | solution.py:52
  6.0 2.0 copy.89
  8.0 15.1 %all-to-all-start.1 = ((bf16[64,16,768]{2,1,0:T(8,128)(2,1)}), bf16[64,16,768]{2,1,0:T(8,128)(2,1)S(1)}, u32[]{:S(2)}, u32[]{:S(2)}) async-start(bf16[64,16,768]{2,1,0:T(8,128)(2,1)} %copy.89), calls=%async_computation.1 | async-start | bytes 3145728 | tf_op jit(solution)/shard_map/all_to_all | solution.py:57
  23.1 2.6 %fusion.38 = bf16[64,4,2,2,768]{4,0,2,3,1:T(8,128)(2,1)S(1)} fusion(bf16[4,64,2,256]{3,0,2,1:T(4,128)(2,1)S(1)} %get-tuple-element.50, f32[2,768]{1,0:T(2,128)S(1)} %fusion.73, bf16[2,4,256,768]{3,2,1,0:T(8,128)(2,1)} %bitcast.175), kind=kOutput, calls=%fused_computation.42 | convolution fusion | flops 408158208 | bytes 4986880 | tf_op jit(solution)/shard_map/asjb,iabd->sajid/dot_general | solution.py:52
  25.9 2.1 copy.80
  28.0 33.8 %all-to-all-done.1 = bf16[64,16,768]{2,1,0:T(8,128)(2,1)S(1)} async-done(((bf16[64,16,768]{2,1,0:T(8,128)(2,1)}), bf16[64,16,768]{2,1,0:T(8,128)(2,1)S(1)}, u32[]{:S(2)}, u32[]{:S(2)}) %all-to-all-start.1) | async-done | bytes 1572896 | tf_op jit(solution)/shard_map/all_to_all | solution.py:57
  61.8 8.3 %all-to-all-start = ((bf16[64,16,768]{2,1,0:T(8,128)(2,1)}), bf16[64,16,768]{2,1,0:T(8,128)(2,1)S(1)}, u32[]{:S(2)}, u32[]{:S(2)}) async-start(bf16[64,16,768]{2,1,0:T(8,128)(2,1)} %copy.80), calls=%async_computation | async-start | bytes 3145728 | tf_op jit(solution)/shard_map/all_to_all | solution.py:57
  70.1 3.8 %fusion.77 = (bf16[2,2,256,768]{3,2,1,0:T(8,128)(2,1)}, bf16[2,2,256,768]{3,2,1,0:T(8,128)(2,1)}) fusion(bf16[2,4,256,768]{3,2,1,0:T(8,128)(2,1)} %bitcast.168), kind=kLoop, calls=%fused_computation.87 | loop fusion | bytes 6291456 | tf_op jit(solution)/shard_map/slice | solution.py:67
  73.9 2.6 %copy.128 = bf16[2,2,256,768]{2,3,0,1:T(8,128)(2,1)} copy(bf16[2,2,256,768]{3,2,1,0:T(8,128)(2,1)} %get-tuple-element.39) | data formatting | bytes 3145728
  78.2 3.7 %fusion.13 = bf16[2,256,2,768]{1,3,2,0:T(8,128)(2,1)S(1)} fusion(bf16[2,2,256,768]{2,3,0,1:T(8,128)(2,1)} %copy.128, f32[2,768]{1,0:T(2,128)S(1)} %fusion.74, bf16[256,2,2,768]{3,2,1,0:T(2,128)(2,1)} %reshape_reshape.7, bf16[4,256,256]{2,1,0:T(8,128)(2,1)} %param.13), kind=kOutput, calls=%fused_computation.17 | convolution fusion | flops 411303936 | bytes 4986880 | tf_op jit(solution)/shard_map/jpa,ajid->jpid/dot_general | solution.py:65
  83.0 1.8 fusion.42
  84.7 3.9 %reshape.53 = bf16[64,4,2,2,768]{4,1,0,3,2:T(4,128)(2,1)} reshape(bf16[256,2,2,768]{3,0,2,1:T(8,128)(2,1)} %fusion.42) | data formatting | bytes 3145728 | tf_op jit(solution)/shard_map/reshape | solution.py:73
  88.6 3.1 %fusion.62 = f32[2,256,256]{2,1,0:T(8,128)} fusion(bf16[2,256,2,768]{1,3,2,0:T(8,128)(2,1)} %copy-done.4, bf16[256,2,2,768]{3,2,1,0:T(2,128)(2,1)S(1)} %copy-done.3), kind=kOutput, calls=%fused_computation.54 | convolution fusion | flops 402653184 | bytes 3670016 | tf_op jit(solution)/shard_map/jpid,ajid->jpa/dot_general | solution.py:71
  91.7 2.8 %copy.96 = bf16[64,4,2,2,768]{4,3,2,1,0:T(2,128)(2,1)} copy(bf16[64,4,2,2,768]{4,1,0,3,2:T(4,128)(2,1)S(1)} %copy-done.5) | data formatting | bytes 3145728 | tf_op jit(solution)/shard_map/optimization_barrier | solution.py:77
  94.5 12.9 %all-to-all-done = bf16[64,16,768]{2,1,0:T(8,128)(2,1)S(1)} async-done(((bf16[64,16,768]{2,1,0:T(8,128)(2,1)}), bf16[64,16,768]{2,1,0:T(8,128)(2,1)S(1)}, u32[]{:S(2)}, u32[]{:S(2)}) %all-to-all-start) | async-done | bytes 1572896 | tf_op jit(solution)/shard_map/all_to_all | solution.py:57
  107.4 9.1 %all-to-all-start.3 = ((bf16[64,4,2,2,768]{4,3,2,1,0:T(2,128)(2,1)}), bf16[64,4,2,2,768]{4,3,2,1,0:T(2,128)(2,1)}, u32[]{:S(2)}, u32[]{:S(2)}) async-start(bf16[64,4,2,2,768]{4,3,2,1,0:T(2,128)(2,1)} %copy.96), calls=%async_computation.3 | async-start | bytes 3145728 | tf_op jit(solution)/shard_map/all_to_all | solution.py:81
  118.1 2.4 %collective-permute-start = (f32[2,256,256]{2,1,0:T(8,128)}, f32[2,256,256]{2,1,0:T(8,128)}, u32[]{:S(2)}, u32[]{:S(2)}) collective-permute-start(f32[2,256,256]{2,1,0:T(8,128)} %fusion.62), channel_id=1, source_target_pairs={{0,64},{64,0},{128,192},{192,128},{1,65},{65,1},{129,193},{193,129... | collective-permute-start | bytes 1572872 | tf_op jit(solution)/shard_map/ppermute | solution.py:22
  121.1 3.1 %fusion.23 = bf16[2,256,2,768]{1,3,2,0:T(8,128)(2,1)S(1)} fusion(bf16[2,2,256,768]{2,3,0,1:T(8,128)(2,1)} %copy.126, f32[2,768]{1,0:T(2,128)S(1)} %fusion.74, bf16[256,2,2,768]{3,2,1,0:T(2,128)(2,1)S(1)} %reshape_reshape.6, bf16[4,256,256]{2,1,0:T(8,128)(2,1)} %param.13), kind=kOutput, calls=%fused_computation.30 | convolution fusion | flops 411303936 | bytes 4986880 | tf_op jit(solution)/shard_map/jpa,ajid->jpid/dot_general | solution.py:65
  128.1 3.9 %reshape.51 = bf16[64,4,2,2,768]{4,1,0,3,2:T(4,128)(2,1)} reshape(bf16[256,2,2,768]{3,0,2,1:T(8,128)(2,1)} %fusion.41) | data formatting | bytes 3145728 | tf_op jit(solution)/shard_map/reshape | solution.py:73
  131.9 6.0 %collective-permute-done.1 = f32[1,256,256]{2,1,0:T(8,128)} collective-permute-done((f32[1,256,256]{2,1,0:T(8,128)}, f32[1,256,256]{2,1,0:T(8,128)}, u32[]{:S(2)}, u32[]{:S(2)}) %collective-permute-start.1) | collective-permute-done | bytes 262176 | tf_op jit(solution)/shard_map/ppermute | solution.py:27
  142.1 2.8 %copy.95 = bf16[64,4,2,2,768]{4,2,3,1,0:T(2,128)(2,1)} copy(bf16[64,4,2,2,768]{4,1,0,3,2:T(4,128)(2,1)S(1)} %copy-done.2) | data formatting | bytes 3145728 | tf_op jit(solution)/shard_map/optimization_barrier | solution.py:75
  144.9 8.5 %all-to-all-done.3 = bf16[64,4,2,2,768]{4,3,2,1,0:T(2,128)(2,1)} async-done(((bf16[64,4,2,2,768]{4,3,2,1,0:T(2,128)(2,1)}), bf16[64,4,2,2,768]{4,3,2,1,0:T(2,128)(2,1)}, u32[]{:S(2)}, u32[]{:S(2)}) %all-to-all-start.3) | async-done | bytes 1572896 | tf_op jit(solution)/shard_map/all_to_all | solution.py:81
  153.3 8.6 %all-to-all-start.2 = ((bf16[64,4,2,2,768]{4,2,3,1,0:T(2,128)(2,1)}), bf16[64,4,2,2,768]{4,2,3,1,0:T(2,128)(2,1)S(1)}, u32[]{:S(2)}, u32[]{:S(2)}) async-start(bf16[64,4,2,2,768]{4,2,3,1,0:T(2,128)(2,1)} %copy.95), calls=%async_computation.2 | async-start | bytes 3145728 | tf_op jit(solution)/shard_map/all_to_all | solution.py:81
  162.0 3.7 %fusion.49 = f32[4,64,2,256]{3,1,2,0:T(8,128)S(1)} fusion(bf16[64,4,2,2,768]{4,3,2,1,0:T(2,128)(2,1)} %all-to-all-done.3, f32[2,768]{1,0:T(2,128)S(1)} %fusion.73, bf16[2,4,256,768]{3,2,1,0:T(8,128)(2,1)} %bitcast.176), kind=kOutput, calls=%fused_computation.51 | convolution fusion | flops 407371776 | bytes 5249024 | tf_op jit(solution)/shard_map/sajid,iabd->asjb/dot_general | solution.py:88
  165.7 3.3 %collective-permute-start.3 = (f32[4,64,2,256]{3,1,2,0:T(8,128)S(1)}, f32[4,64,2,256]{3,1,2,0:T(8,128)S(1)}, u32[]{:S(2)}, u32[]{:S(2)}) collective-permute-start(f32[4,64,2,256]{3,1,2,0:T(8,128)S(1)} %fusion.49), channel_id=1, source_target_pairs={{0,64},{64,0},{128,192},{192,128},{1,65},{65,1},{129,193},{193,129... | collective-permute-start | bytes 1572872 | tf_op jit(solution)/shard_map/ppermute | solution.py:22
  172.3 10.4 %collective-permute-done.4 = f32[2,64,2,256]{3,1,2,0:T(8,128)S(1)} collective-permute-done((f32[2,64,2,256]{3,1,2,0:T(8,128)S(1)}, f32[2,64,2,256]{3,1,2,0:T(8,128)S(1)}, u32[]{:S(2)}, u32[]{:S(2)}) %collective-permute-start.4) | collective-permute-done | bytes 262176 | tf_op jit(solution)/shard_map/ppermute | solution.py:27
  184.5 9.2 %collective-permute-done.7 = f32[1,256,256]{2,1,0:T(8,128)S(1)} collective-permute-done((f32[1,256,256]{2,1,0:T(8,128)S(1)}, f32[1,256,256]{2,1,0:T(8,128)S(1)}, u32[]{:S(2)}, u32[]{:S(2)}) %collective-permute-start.7) | collective-permute-done | bytes 262176 | tf_op jit(solution)/shard_map/ppermute | solution.py:27
  197.2 3.1 %fusion.54 = f32[4,64,2,256]{3,1,2,0:T(8,128)S(1)} fusion(bf16[64,4,2,2,768]{4,2,3,1,0:T(2,128)(2,1)S(1)} %all-to-all-done.2, f32[2,768]{1,0:T(2,128)S(1)} %fusion.73, bf16[2,4,256,768]{3,2,1,0:T(8,128)(2,1)} %bitcast.177), kind=kOutput, calls=%fused_computation.52 | convolution fusion | flops 407371776 | bytes 5249024 | tf_op jit(solution)/shard_map/sajid,iabd->asjb/dot_general | solution.py:95
  200.4 6.9 %collective-permute-start.9 = (f32[4,64,2,256]{3,1,2,0:T(8,128)S(1)}, f32[4,64,2,256]{3,1,2,0:T(8,128)S(1)}, u32[]{:S(2)}, u32[]{:S(2)}) collective-permute-start(f32[4,64,2,256]{3,1,2,0:T(8,128)S(1)} %fusion.54), channel_id=1, source_target_pairs={{0,64},{64,0},{128,192},{192,128},{1,65},{65,1},{129,193},{193,129... | collective-permute-start | bytes 1572872 | tf_op jit(solution)/shard_map/ppermute | solution.py:98
  207.3 2.5 %fusion.31 = f32[4,2,768,256,1]{2,3,4,1,0:T(8,128)S(1)} fusion(bf16[64,4,2,2,768]{4,3,2,1,0:T(2,128)(2,1)} %all-to-all-done.3, bf16[4,64,2,256]{3,0,2,1:T(4,128)(2,1)S(1)} %copy-done.10), kind=kOutput, calls=%fused_computation.37 | convolution fusion | flops 402653184 | bytes 8126464 | tf_op jit(solution)/shard_map/asjb,sajid->iabd/dot_general | solution.py:118
  213.0 1.9 copy.101
  214.9 3.2 %collective-permute-done.10 = f32[2,64,2,256]{3,1,2,0:T(8,128)S(1)} collective-permute-done((f32[2,64,2,256]{3,1,2,0:T(8,128)S(1)}, f32[2,64,2,256]{3,1,2,0:T(8,128)S(1)}, u32[]{:S(2)}, u32[]{:S(2)}) %collective-permute-start.10) | collective-permute-done | bytes 262176 | tf_op jit(solution)/shard_map/ppermute | solution.py:102
  (81 shorter events, 31.8 us)
Async XLA Ops:
  0.6 1.7 copy-start
  2.3 3.5 %copy-start.9 = (bf16[4,64,2,256]{3,0,2,1:T(4,128)(2,1)}, bf16[4,64,2,256]{3,0,2,1:T(4,128)(2,1)S(1)}, u32[]{:S(2)}) copy-start(bf16[4,64,2,256]{3,0,2,1:T(4,128)(2,1)S(1)} %get-tuple-element.49) | copy-start | bytes 786436
  8.0 53.8 %all-to-all-start.1 = ((bf16[64,16,768]{2,1,0:T(8,128)(2,1)}), bf16[64,16,768]{2,1,0:T(8,128)(2,1)S(1)}, u32[]{:S(2)}, u32[]{:S(2)}) async-start(bf16[64,16,768]{2,1,0:T(8,128)(2,1)} %copy.89), calls=%async_computation.1 | async-start | bytes 3145728 | tf_op jit(solution)/shard_map/all_to_all | solution.py:57
  61.8 45.6 %all-to-all-start = ((bf16[64,16,768]{2,1,0:T(8,128)(2,1)}), bf16[64,16,768]{2,1,0:T(8,128)(2,1)S(1)}, u32[]{:S(2)}, u32[]{:S(2)}) async-start(bf16[64,16,768]{2,1,0:T(8,128)(2,1)} %copy.80), calls=%async_computation | async-start | bytes 3145728 | tf_op jit(solution)/shard_map/all_to_all | solution.py:57
  73.9 2.6 %copy-start.13 = (f32[16,768]{1,0:T(8,128)S(1)}, f32[16,768]{1,0:T(8,128)}, u32[]{:S(2)}) copy-start(f32[16,768]{1,0:T(8,128)} %param.11) | copy-start | bytes 147460
  73.9 2.6 %copy-start.14 = (s32[2]{0:T(128)S(1)}, s32[2]{0:T(128)}, u32[]{:S(2)}) copy-start(s32[2]{0:T(128)} %param.9) | copy-start | bytes 28
  78.1 4.8 %copy-start.11 = (bf16[4,256,256]{2,1,0:T(8,128)(2,1)S(1)}, bf16[4,256,256]{2,1,0:T(8,128)(2,1)}, u32[]{:S(2)}) copy-start(bf16[4,256,256]{2,1,0:T(8,128)(2,1)} %param.13) | copy-start | bytes 1572868
  81.8 1.1 copy-start.4
  83.0 5.7 %copy-start.3 = (bf16[256,2,2,768]{3,2,1,0:T(2,128)(2,1)S(1)}, bf16[256,2,2,768]{3,2,1,0:T(2,128)(2,1)}, u32[]{:S(2)}) copy-start(bf16[256,2,2,768]{3,2,1,0:T(2,128)(2,1)} %reshape_reshape.7) | copy-start | bytes 4718596
  88.6 3.1 %copy-start.5 = (bf16[64,4,2,2,768]{4,1,0,3,2:T(4,128)(2,1)S(1)}, bf16[64,4,2,2,768]{4,1,0,3,2:T(4,128)(2,1)}, u32[]{:S(2)}) copy-start(bf16[64,4,2,2,768]{4,1,0,3,2:T(4,128)(2,1)} %reshape.53) | copy-start | bytes 4718596
  91.7 24.8 %copy-start.6 = (bf16[2,2,256,768]{3,2,1,0:T(8,128)(2,1)S(1)}, bf16[2,2,256,768]{3,2,1,0:T(8,128)(2,1)}, u32[]{:S(2)}) copy-start(bf16[2,2,256,768]{3,2,1,0:T(8,128)(2,1)} %get-tuple-element.40) | copy-start | bytes 4718596
  107.4 46.0 %all-to-all-start.3 = ((bf16[64,4,2,2,768]{4,3,2,1,0:T(2,128)(2,1)}), bf16[64,4,2,2,768]{4,3,2,1,0:T(2,128)(2,1)}, u32[]{:S(2)}, u32[]{:S(2)}) async-start(bf16[64,4,2,2,768]{4,3,2,1,0:T(2,128)(2,1)} %copy.96), calls=%async_computation.3 | async-start | bytes 3145728 | tf_op jit(solution)/shard_map/all_to_all | solution.py:81
  118.1 6.1 %collective-permute-start = (f32[2,256,256]{2,1,0:T(8,128)}, f32[2,256,256]{2,1,0:T(8,128)}, u32[]{:S(2)}, u32[]{:S(2)}) collective-permute-start(f32[2,256,256]{2,1,0:T(8,128)} %fusion.62), channel_id=1, source_target_pairs={{0,64},{64,0},{128,192},{192,128},{1,65},{65,1},{129,193},{193,129... | collective-permute-start | bytes 1572872 | tf_op jit(solution)/shard_map/ppermute | solution.py:22
  121.1 3.1 %copy-start.7 = (f32[2,256,256]{2,1,0:T(8,128)S(1)}, f32[2,256,256]{2,1,0:T(8,128)}, u32[]{:S(2)}) copy-start(f32[2,256,256]{2,1,0:T(8,128)} %fusion.62) | copy-start | bytes 1572868
  121.1 5.2 %copy-start.12 = (bf16[4,256,256]{2,1,0:T(8,128)(2,1)S(1)}, bf16[4,256,256]{2,1,0:T(8,128)(2,1)}, u32[]{:S(2)}) copy-start(bf16[4,256,256]{2,1,0:T(8,128)(2,1)} %param.13) | copy-start | bytes 1572868
  125.9 12.0 %collective-permute-start.1 = (f32[1,256,256]{2,1,0:T(8,128)}, f32[1,256,256]{2,1,0:T(8,128)}, u32[]{:S(2)}, u32[]{:S(2)}) collective-permute-start(f32[1,256,256]{2,1,0:T(8,128)} %dynamic-slice_add_fusion.1), channel_id=1, source_target_pairs={{0,128},{64,192},{128,0},{192,64},{1,129},{65,193},{129,1},{193,65... | collective-permute-start | bytes 786440 | tf_op jit(solution)/shard_map/ppermute | solution.py:27
  131.9 10.2 %copy-start.2 = (bf16[64,4,2,2,768]{4,1,0,3,2:T(4,128)(2,1)S(1)}, bf16[64,4,2,2,768]{4,1,0,3,2:T(4,128)(2,1)}, u32[]{:S(2)}) copy-start(bf16[64,4,2,2,768]{4,1,0,3,2:T(4,128)(2,1)} %reshape.51) | copy-start | bytes 4718596
  139.0 3.0 %collective-permute-start.2 = (f32[1,256,256]{2,1,0:T(8,128)S(1)}, f32[1,256,256]{2,1,0:T(8,128)S(1)}, u32[]{:S(2)}, u32[]{:S(2)}) collective-permute-start(f32[1,256,256]{2,1,0:T(8,128)S(1)} %add.62), channel_id=1, source_target_pairs={{0,64},{64,0},{128,192},{192,128},{1,65},{65,1},{129,193},{193,129... | collective-permute-start | bytes 786440 | tf_op jit(solution)/shard_map/ppermute | solution.py:28
  153.3 43.9 %all-to-all-start.2 = ((bf16[64,4,2,2,768]{4,2,3,1,0:T(2,128)(2,1)}), bf16[64,4,2,2,768]{4,2,3,1,0:T(2,128)(2,1)S(1)}, u32[]{:S(2)}, u32[]{:S(2)}) async-start(bf16[64,4,2,2,768]{4,2,3,1,0:T(2,128)(2,1)} %copy.95), calls=%async_computation.2 | async-start | bytes 3145728 | tf_op jit(solution)/shard_map/all_to_all | solution.py:81
  162.0 7.0 %copy-start.8 = (f32[2,256,256]{2,1,0:T(8,128)S(1)}, f32[2,256,256]{2,1,0:T(8,128)}, u32[]{:S(2)}) copy-start(f32[2,256,256]{2,1,0:T(8,128)} %fusion.59) | copy-start | bytes 1572868
  165.7 4.8 %collective-permute-start.3 = (f32[4,64,2,256]{3,1,2,0:T(8,128)S(1)}, f32[4,64,2,256]{3,1,2,0:T(8,128)S(1)}, u32[]{:S(2)}, u32[]{:S(2)}) collective-permute-start(f32[4,64,2,256]{3,1,2,0:T(8,128)S(1)} %fusion.49), channel_id=1, source_target_pairs={{0,64},{64,0},{128,192},{192,128},{1,65},{65,1},{129,193},{193,129... | collective-permute-start | bytes 1572872 | tf_op jit(solution)/shard_map/ppermute | solution.py:22
  169.0 2.3 %collective-permute-start.6 = (f32[2,256,256]{2,1,0:T(8,128)S(1)}, f32[2,256,256]{2,1,0:T(8,128)S(1)}, u32[]{:S(2)}, u32[]{:S(2)}) collective-permute-start(f32[2,256,256]{2,1,0:T(8,128)S(1)} %copy-done.8), channel_id=1, source_target_pairs={{0,64},{64,0},{128,192},{192,128},{1,65},{65,1},{129,193},{193,129... | collective-permute-start | bytes 1572872 | tf_op jit(solution)/shard_map/ppermute | solution.py:22
  170.6 12.1 %collective-permute-start.4 = (f32[2,64,2,256]{3,1,2,0:T(8,128)S(1)}, f32[2,64,2,256]{3,1,2,0:T(8,128)S(1)}, u32[]{:S(2)}, u32[]{:S(2)}) collective-permute-start(f32[2,64,2,256]{3,1,2,0:T(8,128)S(1)} %dynamic-slice_bitcast_fusion.1), channel_id=1, source_target_pairs={{0,128},{64,192},{128,0},{192,64},{1,129},{65,193},{129,1},{193,65... | collective-permute-start | bytes 786440 | tf_op jit(solution)/shard_map/ppermute | solution.py:27
  171.3 22.4 %collective-permute-start.7 = (f32[1,256,256]{2,1,0:T(8,128)S(1)}, f32[1,256,256]{2,1,0:T(8,128)S(1)}, u32[]{:S(2)}, u32[]{:S(2)}) collective-permute-start(f32[1,256,256]{2,1,0:T(8,128)S(1)} %dynamic-slice_add_fusion), channel_id=1, source_target_pairs={{0,128},{64,192},{128,0},{192,64},{1,129},{65,193},{129,1},{193,65... | collective-permute-start | bytes 786440 | tf_op jit(solution)/shard_map/ppermute | solution.py:27
  182.8 12.1 %collective-permute-start.5 = (f32[2,64,2,256]{3,1,2,0:T(8,128)S(1)}, f32[2,64,2,256]{3,1,2,0:T(8,128)S(1)}, u32[]{:S(2)}, u32[]{:S(2)}) collective-permute-start(f32[2,64,2,256]{3,1,2,0:T(8,128)S(1)} %fusion.85), channel_id=1, source_target_pairs={{0,64},{64,0},{128,192},{192,128},{1,65},{65,1},{129,193},{193,129... | collective-permute-start | bytes 786440 | tf_op jit(solution)/shard_map/ppermute | solution.py:28
  193.7 2.3 %collective-permute-start.8 = (f32[1,256,256]{2,1,0:T(8,128)S(1)}, f32[1,256,256]{2,1,0:T(8,128)S(1)}, u32[]{:S(2)}, u32[]{:S(2)}) collective-permute-start(f32[1,256,256]{2,1,0:T(8,128)S(1)} %add.66), channel_id=1, source_target_pairs={{0,64},{64,0},{128,192},{192,128},{1,65},{65,1},{129,193},{193,129... | collective-permute-start | bytes 786440 | tf_op jit(solution)/shard_map/ppermute | solution.py:28
  197.2 10.0 %copy-start.10 = (bf16[4,64,2,256]{3,0,2,1:T(4,128)(2,1)S(1)}, bf16[4,64,2,256]{3,0,2,1:T(4,128)(2,1)}, u32[]{:S(2)}) copy-start(bf16[4,64,2,256]{3,0,2,1:T(4,128)(2,1)} %copy-done.9) | copy-start | bytes 786436
  200.4 9.4 %collective-permute-start.9 = (f32[4,64,2,256]{3,1,2,0:T(8,128)S(1)}, f32[4,64,2,256]{3,1,2,0:T(8,128)S(1)}, u32[]{:S(2)}, u32[]{:S(2)}) collective-permute-start(f32[4,64,2,256]{3,1,2,0:T(8,128)S(1)} %fusion.54), channel_id=1, source_target_pairs={{0,64},{64,0},{128,192},{192,128},{1,65},{65,1},{129,193},{193,129... | collective-permute-start | bytes 1572872 | tf_op jit(solution)/shard_map/ppermute | solution.py:98
  209.9 8.3 %collective-permute-start.10 = (f32[2,64,2,256]{3,1,2,0:T(8,128)S(1)}, f32[2,64,2,256]{3,1,2,0:T(8,128)S(1)}, u32[]{:S(2)}, u32[]{:S(2)}) collective-permute-start(f32[2,64,2,256]{3,1,2,0:T(8,128)S(1)} %dynamic-slice_bitcast_fusion), channel_id=1, source_target_pairs={{0,128},{64,192},{128,0},{192,64},{1,129},{65,193},{129,1},{193,65... | collective-permute-start | bytes 786440 | tf_op jit(solution)/shard_map/ppermute | solution.py:102
  218.2 2.1 collective-permute-start.11
  220.3 2.0 copy-start.1

commit v7 on v6

--- a/solution.py
+++ b/solution.py
@@ -1,6 +1,7 @@
 import jax
 import jax.numpy as jnp
 from jax import lax
+from jax.experimental.layout import Layout, with_layout_constraint
 from jax.sharding import PartitionSpec as P
 
 CHUNKS = 2
@@ -123,7 +124,9 @@
         grad_inputs = (
             (back_sum * gate_in[:, None, None, :]).astype(bf16).reshape(images, rows, width)
         )
-    grad_one = jnp.concatenate(grad_one, axis=2).reshape(own, blocks, blocks)
+    grad_one = jnp.concatenate(grad_one, axis=2)
+    grad_one = with_layout_constraint(grad_one, Layout(major_to_minor=(0, 1, 2, 3)))
+    grad_one = grad_one.reshape(own, blocks, blocks)
     second_factor_gradient = jnp.concatenate(sfg, axis=0)
     return (grad_inputs, grad_one, second_factor_gradient)
 

time: 223 us -> 223 us (level)
    unnamed x34 -> x35, local copies, waits for them, and re-layouts: 8.01 us -> 7.26 us
where the time goes in v7:
time: 223 us; the launch traced here: 222 us
  waiting for transfers between devices  87.6 us (39%)
  starting transfers between devices  62.3 us (28%)
  local copies, waits for them, and re-layouts  34.2 us (15%)
  matrix products  32 us (14%)
  other arithmetic  5.35 us (2%)
    all_to_all x2, waiting for transfers between devices, on_device(): lax.all_to_all(flat, 'seq', 0, 0, tiled=True)  46.7 us
    ppermute x3, waiting for transfers between devices, dp_sum_halves(): mine = mine + lax.ppermute(mine, 'dp', [(i, i ^ 2) for i in range(n_dp)])  25.8 us
    all_to_all x2, starting transfers between devices, on_device(): lax.all_to_all(flat, 'seq', 0, 0, tiled=True)  23.5 us
    all_to_all x2, starting transfers between devices, on_device(): recv2.append(lax.all_to_all(send, 'seq', 0, 0, tiled=True))  17.7 us
    all_to_all x2, waiting for transfers between devices, on_device(): recv2.append(lax.all_to_all(send, 'seq', 0, 0, tiled=True))  9.44 us
    reshape x2, local copies, waits for them, and re-layouts, on_device(): send = send.reshape(n_seq, own, per, images, width)  7.76 us
    unnamed x35, local copies, waits for them, and re-layouts  7.26 us
    ppermute x1, starting transfers between devices, on_device(): x = part + lax.ppermute(part, 'dp', [(i, i ^ 1) for i in range(n_dp)])  7.17 us
  transfers between devices with their start and end apart: 16, of which 11 were waited for; matrix products, arithmetic and copies ran while one was open for 26% of the time, Pallas kernels for 0%

profile of v7, /device:TPU:1, one launch (start us, length us, event | category | flops | bytes accessed | tf_op | source)
XLA Modules:
  0.0 222.4 jit_solution(1200815450499665683)
XLA Ops:
  3.2 2.6 %fusion.35 = bf16[64,4,2,2,768]{4,0,2,3,1:T(8,128)(2,1)S(1)} fusion(bf16[4,64,2,256]{3,0,2,1:T(4,128)(2,1)S(1)} %get-tuple-element.43, f32[2,768]{1,0:T(2,128)S(1)} %fusion.73, bf16[2,4,256,768]{3,2,1,0:T(8,128)(2,1)} %bitcast.192), kind=kOutput, calls=%fused_computation.41 | convolution fusion | flops 408158208 | bytes 4986880 | tf_op jit(solution)/shard_map/asjb,iabd->sajid/dot_general | solution.py:53
  6.0 2.0 copy.66
  8.0 15.1 %all-to-all-start.1 = ((bf16[64,16,768]{2,1,0:T(8,128)(2,1)}), bf16[64,16,768]{2,1,0:T(8,128)(2,1)S(1)}, u32[]{:S(2)}, u32[]{:S(2)}) async-start(bf16[64,16,768]{2,1,0:T(8,128)(2,1)} %copy.66), calls=%async_computation.1 | async-start | bytes 3145728 | tf_op jit(solution)/shard_map/all_to_all | solution.py:58
  23.1 2.6 %fusion.38 = bf16[64,4,2,2,768]{4,0,2,3,1:T(8,128)(2,1)S(1)} fusion(bf16[4,64,2,256]{3,0,2,1:T(4,128)(2,1)S(1)} %get-tuple-element.44, f32[2,768]{1,0:T(2,128)S(1)} %fusion.73, bf16[2,4,256,768]{3,2,1,0:T(8,128)(2,1)} %bitcast.193), kind=kOutput, calls=%fused_computation.42 | convolution fusion | flops 408158208 | bytes 4986880 | tf_op jit(solution)/shard_map/asjb,iabd->sajid/dot_general | solution.py:53
  25.9 2.1 copy.57
  28.0 33.8 %all-to-all-done.1 = bf16[64,16,768]{2,1,0:T(8,128)(2,1)S(1)} async-done(((bf16[64,16,768]{2,1,0:T(8,128)(2,1)}), bf16[64,16,768]{2,1,0:T(8,128)(2,1)S(1)}, u32[]{:S(2)}, u32[]{:S(2)}) %all-to-all-start.1) | async-done | bytes 1572896 | tf_op jit(solution)/shard_map/all_to_all | solution.py:58
  61.8 8.3 %all-to-all-start = ((bf16[64,16,768]{2,1,0:T(8,128)(2,1)}), bf16[64,16,768]{2,1,0:T(8,128)(2,1)S(1)}, u32[]{:S(2)}, u32[]{:S(2)}) async-start(bf16[64,16,768]{2,1,0:T(8,128)(2,1)} %copy.57), calls=%async_computation | async-start | bytes 3145728 | tf_op jit(solution)/shard_map/all_to_all | solution.py:58
  70.1 3.8 %fusion.78 = (bf16[2,2,256,768]{3,2,1,0:T(8,128)(2,1)}, bf16[2,2,256,768]{3,2,1,0:T(8,128)(2,1)}) fusion(bf16[2,4,256,768]{3,2,1,0:T(8,128)(2,1)} %bitcast.176), kind=kLoop, calls=%fused_computation.90 | loop fusion | bytes 6291456 | tf_op jit(solution)/shard_map/slice | solution.py:68
  73.9 2.6 %copy.105 = bf16[2,2,256,768]{2,3,0,1:T(8,128)(2,1)} copy(bf16[2,2,256,768]{3,2,1,0:T(8,128)(2,1)} %get-tuple-element.33) | data formatting | bytes 3145728
  78.2 3.7 %fusion.13 = bf16[2,256,2,768]{1,3,2,0:T(8,128)(2,1)S(1)} fusion(bf16[2,2,256,768]{2,3,0,1:T(8,128)(2,1)} %copy.105, f32[2,768]{1,0:T(2,128)S(1)} %fusion.74, bf16[256,2,2,768]{3,2,1,0:T(2,128)(2,1)} %reshape_reshape.7, bf16[4,256,256]{2,1,0:T(8,128)(2,1)} %param.13), kind=kOutput, calls=%fused_computation.17 | convolution fusion | flops 411303936 | bytes 4986880 | tf_op jit(solution)/shard_map/jpa,ajid->jpid/dot_general | solution.py:66
  83.0 1.8 fusion.42
  84.7 3.9 %reshape.53 = bf16[64,4,2,2,768]{4,1,0,3,2:T(4,128)(2,1)} reshape(bf16[256,2,2,768]{3,0,2,1:T(8,128)(2,1)} %fusion.42) | data formatting | bytes 3145728 | tf_op jit(solution)/shard_map/reshape | solution.py:74
  88.6 3.1 %fusion.62 = f32[2,256,256]{2,1,0:T(8,128)} fusion(bf16[2,256,2,768]{1,3,2,0:T(8,128)(2,1)} %copy-done.4, bf16[256,2,2,768]{3,2,1,0:T(2,128)(2,1)S(1)} %copy-done.3), kind=kOutput, calls=%fused_computation.54 | convolution fusion | flops 402653184 | bytes 3670016 | tf_op jit(solution)/shard_map/jpid,ajid->jpa/dot_general | solution.py:72
  91.7 2.8 %copy.73 = bf16[64,4,2,2,768]{4,3,2,1,0:T(2,128)(2,1)} copy(bf16[64,4,2,2,768]{4,1,0,3,2:T(4,128)(2,1)S(1)} %copy-done.5) | data formatting | bytes 3145728 | tf_op jit(solution)/shard_map/optimization_barrier | solution.py:78
  94.5 12.9 %all-to-all-done = bf16[64,16,768]{2,1,0:T(8,128)(2,1)S(1)} async-done(((bf16[64,16,768]{2,1,0:T(8,128)(2,1)}), bf16[64,16,768]{2,1,0:T(8,128)(2,1)S(1)}, u32[]{:S(2)}, u32[]{:S(2)}) %all-to-all-start) | async-done | bytes 1572896 | tf_op jit(solution)/shard_map/all_to_all | solution.py:58
  107.4 9.1 %all-to-all-start.3 = ((bf16[64,4,2,2,768]{4,3,2,1,0:T(2,128)(2,1)}), bf16[64,4,2,2,768]{4,3,2,1,0:T(2,128)(2,1)}, u32[]{:S(2)}, u32[]{:S(2)}) async-start(bf16[64,4,2,2,768]{4,3,2,1,0:T(2,128)(2,1)} %copy.73), calls=%async_computation.3 | async-start | bytes 3145728 | tf_op jit(solution)/shard_map/all_to_all | solution.py:82
  118.1 2.4 %collective-permute-start = (f32[2,256,256]{2,1,0:T(8,128)}, f32[2,256,256]{2,1,0:T(8,128)}, u32[]{:S(2)}, u32[]{:S(2)}) collective-permute-start(f32[2,256,256]{2,1,0:T(8,128)} %fusion.62), channel_id=1, source_target_pairs={{0,64},{64,0},{128,192},{192,128},{1,65},{65,1},{129,193},{193,129... | collective-permute-start | bytes 1572872 | tf_op jit(solution)/shard_map/ppermute | solution.py:23
  121.1 3.1 %fusion.23 = bf16[2,256,2,768]{1,3,2,0:T(8,128)(2,1)S(1)} fusion(bf16[2,2,256,768]{2,3,0,1:T(8,128)(2,1)} %copy.103, f32[2,768]{1,0:T(2,128)S(1)} %fusion.74, bf16[256,2,2,768]{3,2,1,0:T(2,128)(2,1)S(1)} %reshape_reshape.6, bf16[4,256,256]{2,1,0:T(8,128)(2,1)} %param.13), kind=kOutput, calls=%fused_computation.30 | convolution fusion | flops 411303936 | bytes 4986880 | tf_op jit(solution)/shard_map/jpa,ajid->jpid/dot_general | solution.py:66
  128.1 3.9 %reshape.51 = bf16[64,4,2,2,768]{4,1,0,3,2:T(4,128)(2,1)} reshape(bf16[256,2,2,768]{3,0,2,1:T(8,128)(2,1)} %fusion.41) | data formatting | bytes 3145728 | tf_op jit(solution)/shard_map/reshape | solution.py:74
  131.9 6.0 %collective-permute-done.1 = f32[1,256,256]{2,1,0:T(8,128)} collective-permute-done((f32[1,256,256]{2,1,0:T(8,128)}, f32[1,256,256]{2,1,0:T(8,128)}, u32[]{:S(2)}, u32[]{:S(2)}) %collective-permute-start.1) | collective-permute-done | bytes 262176 | tf_op jit(solution)/shard_map/ppermute | solution.py:28
  142.1 2.8 %copy.72 = bf16[64,4,2,2,768]{4,2,3,1,0:T(2,128)(2,1)} copy(bf16[64,4,2,2,768]{4,1,0,3,2:T(4,128)(2,1)S(1)} %copy-done.2) | data formatting | bytes 3145728 | tf_op jit(solution)/shard_map/optimization_barrier | solution.py:76
  144.9 8.5 %all-to-all-done.3 = bf16[64,4,2,2,768]{4,3,2,1,0:T(2,128)(2,1)} async-done(((bf16[64,4,2,2,768]{4,3,2,1,0:T(2,128)(2,1)}), bf16[64,4,2,2,768]{4,3,2,1,0:T(2,128)(2,1)}, u32[]{:S(2)}, u32[]{:S(2)}) %all-to-all-start.3) | async-done | bytes 1572896 | tf_op jit(solution)/shard_map/all_to_all | solution.py:82
  153.3 8.6 %all-to-all-start.2 = ((bf16[64,4,2,2,768]{4,2,3,1,0:T(2,128)(2,1)}), bf16[64,4,2,2,768]{4,2,3,1,0:T(2,128)(2,1)S(1)}, u32[]{:S(2)}, u32[]{:S(2)}) async-start(bf16[64,4,2,2,768]{4,2,3,1,0:T(2,128)(2,1)} %copy.72), calls=%async_computation.2 | async-start | bytes 3145728 | tf_op jit(solution)/shard_map/all_to_all | solution.py:82
  162.0 3.7 %fusion.49 = f32[4,64,2,256]{3,1,2,0:T(8,128)S(1)} fusion(bf16[64,4,2,2,768]{4,3,2,1,0:T(2,128)(2,1)} %all-to-all-done.3, f32[2,768]{1,0:T(2,128)S(1)} %fusion.73, bf16[2,4,256,768]{3,2,1,0:T(8,128)(2,1)} %bitcast.194), kind=kOutput, calls=%fused_computation.51 | convolution fusion | flops 407371776 | bytes 5249024 | tf_op jit(solution)/shard_map/sajid,iabd->asjb/dot_general | solution.py:89
  165.7 3.3 %collective-permute-start.3 = (f32[4,64,2,256]{3,1,2,0:T(8,128)S(1)}, f32[4,64,2,256]{3,1,2,0:T(8,128)S(1)}, u32[]{:S(2)}, u32[]{:S(2)}) collective-permute-start(f32[4,64,2,256]{3,1,2,0:T(8,128)S(1)} %fusion.49), channel_id=1, source_target_pairs={{0,64},{64,0},{128,192},{192,128},{1,65},{65,1},{129,193},{193,129... | collective-permute-start | bytes 1572872 | tf_op jit(solution)/shard_map/ppermute | solution.py:23
  172.5 10.6 %collective-permute-done.4 = f32[2,64,2,256]{3,2,1,0:T(2,128)S(1)} collective-permute-done((f32[2,64,2,256]{3,2,1,0:T(2,128)S(1)}, f32[2,64,2,256]{3,2,1,0:T(2,128)S(1)}, u32[]{:S(2)}, u32[]{:S(2)}) %collective-permute-start.4) | collective-permute-done | bytes 262176 | tf_op jit(solution)/shard_map/ppermute | solution.py:28
  184.8 9.1 %collective-permute-done.7 = f32[1,256,256]{2,1,0:T(8,128)S(1)} collective-permute-done((f32[1,256,256]{2,1,0:T(8,128)S(1)}, f32[1,256,256]{2,1,0:T(8,128)S(1)}, u32[]{:S(2)}, u32[]{:S(2)}) %collective-permute-start.7) | collective-permute-done | bytes 262176 | tf_op jit(solution)/shard_map/ppermute | solution.py:28
  197.2 3.1 %fusion.54 = f32[4,64,2,256]{3,1,2,0:T(8,128)S(1)} fusion(bf16[64,4,2,2,768]{4,2,3,1,0:T(2,128)(2,1)S(1)} %all-to-all-done.2, f32[2,768]{1,0:T(2,128)S(1)} %fusion.73, bf16[2,4,256,768]{3,2,1,0:T(8,128)(2,1)} %bitcast.195), kind=kOutput, calls=%fused_computation.52 | convolution fusion | flops 407371776 | bytes 5249024 | tf_op jit(solution)/shard_map/sajid,iabd->asjb/dot_general | solution.py:96
  200.4 7.2 %collective-permute-start.9 = (f32[4,64,2,256]{3,1,2,0:T(8,128)S(1)}, f32[4,64,2,256]{3,1,2,0:T(8,128)S(1)}, u32[]{:S(2)}, u32[]{:S(2)}) collective-permute-start(f32[4,64,2,256]{3,1,2,0:T(8,128)S(1)} %fusion.54), channel_id=1, source_target_pairs={{0,64},{64,0},{128,192},{192,128},{1,65},{65,1},{129,193},{193,129... | collective-permute-start | bytes 1572872 | tf_op jit(solution)/shard_map/ppermute | solution.py:99
  207.5 2.5 %fusion.31 = f32[4,2,768,256,1]{2,3,4,1,0:T(8,128)S(1)} fusion(bf16[64,4,2,2,768]{4,3,2,1,0:T(2,128)(2,1)} %all-to-all-done.3, bf16[4,64,2,256]{3,0,2,1:T(4,128)(2,1)S(1)} %copy-done.10), kind=kOutput, calls=%fused_computation.37 | convolution fusion | flops 402653184 | bytes 8126464 | tf_op jit(solution)/shard_map/asjb,sajid->iabd/dot_general | solution.py:119
  213.2 1.9 copy.80
  215.1 3.2 %collective-permute-done.10 = f32[2,64,2,256]{3,2,1,0:T(2,128)S(1)} collective-permute-done((f32[2,64,2,256]{3,2,1,0:T(2,128)S(1)}, f32[2,64,2,256]{3,2,1,0:T(2,128)S(1)}, u32[]{:S(2)}, u32[]{:S(2)}) %collective-permute-start.10) | collective-permute-done | bytes 262176 | tf_op jit(solution)/shard_map/ppermute | solution.py:103
  (82 shorter events, 31.5 us)
Async XLA Ops:
  0.6 1.7 copy-start
  2.3 3.5 %copy-start.9 = (bf16[4,64,2,256]{3,0,2,1:T(4,128)(2,1)}, bf16[4,64,2,256]{3,0,2,1:T(4,128)(2,1)S(1)}, u32[]{:S(2)}) copy-start(bf16[4,64,2,256]{3,0,2,1:T(4,128)(2,1)S(1)} %get-tuple-element.43) | copy-start | bytes 786436
  8.0 53.8 %all-to-all-start.1 = ((bf16[64,16,768]{2,1,0:T(8,128)(2,1)}), bf16[64,16,768]{2,1,0:T(8,128)(2,1)S(1)}, u32[]{:S(2)}, u32[]{:S(2)}) async-start(bf16[64,16,768]{2,1,0:T(8,128)(2,1)} %copy.66), calls=%async_computation.1 | async-start | bytes 3145728 | tf_op jit(solution)/shard_map/all_to_all | solution.py:58
  61.8 45.6 %all-to-all-start = ((bf16[64,16,768]{2,1,0:T(8,128)(2,1)}), bf16[64,16,768]{2,1,0:T(8,128)(2,1)S(1)}, u32[]{:S(2)}, u32[]{:S(2)}) async-start(bf16[64,16,768]{2,1,0:T(8,128)(2,1)} %copy.57), calls=%async_computation | async-start | bytes 3145728 | tf_op jit(solution)/shard_map/all_to_all | solution.py:58
  73.9 2.6 %copy-start.13 = (f32[16,768]{1,0:T(8,128)S(1)}, f32[16,768]{1,0:T(8,128)}, u32[]{:S(2)}) copy-start(f32[16,768]{1,0:T(8,128)} %param.11) | copy-start | bytes 147460
  73.9 2.6 %copy-start.14 = (s32[2]{0:T(128)S(1)}, s32[2]{0:T(128)}, u32[]{:S(2)}) copy-start(s32[2]{0:T(128)} %param.9) | copy-start | bytes 28
  78.1 4.8 %copy-start.11 = (bf16[4,256,256]{2,1,0:T(8,128)(2,1)S(1)}, bf16[4,256,256]{2,1,0:T(8,128)(2,1)}, u32[]{:S(2)}) copy-start(bf16[4,256,256]{2,1,0:T(8,128)(2,1)} %param.13) | copy-start | bytes 1572868
  81.8 1.1 copy-start.4
  83.0 5.7 %copy-start.3 = (bf16[256,2,2,768]{3,2,1,0:T(2,128)(2,1)S(1)}, bf16[256,2,2,768]{3,2,1,0:T(2,128)(2,1)}, u32[]{:S(2)}) copy-start(bf16[256,2,2,768]{3,2,1,0:T(2,128)(2,1)} %reshape_reshape.7) | copy-start | bytes 4718596
  88.6 3.1 %copy-start.5 = (bf16[64,4,2,2,768]{4,1,0,3,2:T(4,128)(2,1)S(1)}, bf16[64,4,2,2,768]{4,1,0,3,2:T(4,128)(2,1)}, u32[]{:S(2)}) copy-start(bf16[64,4,2,2,768]{4,1,0,3,2:T(4,128)(2,1)} %reshape.53) | copy-start | bytes 4718596
  91.7 24.8 %copy-start.6 = (bf16[2,2,256,768]{3,2,1,0:T(8,128)(2,1)S(1)}, bf16[2,2,256,768]{3,2,1,0:T(8,128)(2,1)}, u32[]{:S(2)}) copy-start(bf16[2,2,256,768]{3,2,1,0:T(8,128)(2,1)} %get-tuple-element.34) | copy-start | bytes 4718596
  107.4 46.0 %all-to-all-start.3 = ((bf16[64,4,2,2,768]{4,3,2,1,0:T(2,128)(2,1)}), bf16[64,4,2,2,768]{4,3,2,1,0:T(2,128)(2,1)}, u32[]{:S(2)}, u32[]{:S(2)}) async-start(bf16[64,4,2,2,768]{4,3,2,1,0:T(2,128)(2,1)} %copy.73), calls=%async_computation.3 | async-start | bytes 3145728 | tf_op jit(solution)/shard_map/all_to_all | solution.py:82
  118.1 6.1 %collective-permute-start = (f32[2,256,256]{2,1,0:T(8,128)}, f32[2,256,256]{2,1,0:T(8,128)}, u32[]{:S(2)}, u32[]{:S(2)}) collective-permute-start(f32[2,256,256]{2,1,0:T(8,128)} %fusion.62), channel_id=1, source_target_pairs={{0,64},{64,0},{128,192},{192,128},{1,65},{65,1},{129,193},{193,129... | collective-permute-start | bytes 1572872 | tf_op jit(solution)/shard_map/ppermute | solution.py:23
  121.1 3.1 %copy-start.7 = (f32[2,256,256]{2,1,0:T(8,128)S(1)}, f32[2,256,256]{2,1,0:T(8,128)}, u32[]{:S(2)}) copy-start(f32[2,256,256]{2,1,0:T(8,128)} %fusion.62) | copy-start | bytes 1572868
  121.1 5.2 %copy-start.12 = (bf16[4,256,256]{2,1,0:T(8,128)(2,1)S(1)}, bf16[4,256,256]{2,1,0:T(8,128)(2,1)}, u32[]{:S(2)}) copy-start(bf16[4,256,256]{2,1,0:T(8,128)(2,1)} %param.13) | copy-start | bytes 1572868
  125.9 12.0 %collective-permute-start.1 = (f32[1,256,256]{2,1,0:T(8,128)}, f32[1,256,256]{2,1,0:T(8,128)}, u32[]{:S(2)}, u32[]{:S(2)}) collective-permute-start(f32[1,256,256]{2,1,0:T(8,128)} %dynamic-slice_add_fusion.1), channel_id=1, source_target_pairs={{0,128},{64,192},{128,0},{192,64},{1,129},{65,193},{129,1},{193,65... | collective-permute-start | bytes 786440 | tf_op jit(solution)/shard_map/ppermute | solution.py:28
  131.9 10.2 %copy-start.2 = (bf16[64,4,2,2,768]{4,1,0,3,2:T(4,128)(2,1)S(1)}, bf16[64,4,2,2,768]{4,1,0,3,2:T(4,128)(2,1)}, u32[]{:S(2)}) copy-start(bf16[64,4,2,2,768]{4,1,0,3,2:T(4,128)(2,1)} %reshape.51) | copy-start | bytes 4718596
  139.0 3.0 %collective-permute-start.2 = (f32[1,256,256]{2,1,0:T(8,128)S(1)}, f32[1,256,256]{2,1,0:T(8,128)S(1)}, u32[]{:S(2)}, u32[]{:S(2)}) collective-permute-start(f32[1,256,256]{2,1,0:T(8,128)S(1)} %add.62), channel_id=1, source_target_pairs={{0,64},{64,0},{128,192},{192,128},{1,65},{65,1},{129,193},{193,129... | collective-permute-start | bytes 786440 | tf_op jit(solution)/shard_map/ppermute | solution.py:29
  153.3 43.9 %all-to-all-start.2 = ((bf16[64,4,2,2,768]{4,2,3,1,0:T(2,128)(2,1)}), bf16[64,4,2,2,768]{4,2,3,1,0:T(2,128)(2,1)S(1)}, u32[]{:S(2)}, u32[]{:S(2)}) async-start(bf16[64,4,2,2,768]{4,2,3,1,0:T(2,128)(2,1)} %copy.72), calls=%async_computation.2 | async-start | bytes 3145728 | tf_op jit(solution)/shard_map/all_to_all | solution.py:82
  162.0 7.0 %copy-start.8 = (f32[2,256,256]{2,1,0:T(8,128)S(1)}, f32[2,256,256]{2,1,0:T(8,128)}, u32[]{:S(2)}) copy-start(f32[2,256,256]{2,1,0:T(8,128)} %fusion.59) | copy-start | bytes 1572868
  165.7 4.8 %collective-permute-start.3 = (f32[4,64,2,256]{3,1,2,0:T(8,128)S(1)}, f32[4,64,2,256]{3,1,2,0:T(8,128)S(1)}, u32[]{:S(2)}, u32[]{:S(2)}) collective-permute-start(f32[4,64,2,256]{3,1,2,0:T(8,128)S(1)} %fusion.49), channel_id=1, source_target_pairs={{0,64},{64,0},{128,192},{192,128},{1,65},{65,1},{129,193},{193,129... | collective-permute-start | bytes 1572872 | tf_op jit(solution)/shard_map/ppermute | solution.py:23
  169.0 2.5 %collective-permute-start.6 = (f32[2,256,256]{2,1,0:T(8,128)S(1)}, f32[2,256,256]{2,1,0:T(8,128)S(1)}, u32[]{:S(2)}, u32[]{:S(2)}) collective-permute-start(f32[2,256,256]{2,1,0:T(8,128)S(1)} %copy-done.8), channel_id=1, source_target_pairs={{0,64},{64,0},{128,192},{192,128},{1,65},{65,1},{129,193},{193,129... | collective-permute-start | bytes 1572872 | tf_op jit(solution)/shard_map/ppermute | solution.py:23
  170.8 12.3 %collective-permute-start.4 = (f32[2,64,2,256]{3,2,1,0:T(2,128)S(1)}, f32[2,64,2,256]{3,2,1,0:T(2,128)S(1)}, u32[]{:S(2)}, u32[]{:S(2)}) collective-permute-start(f32[2,64,2,256]{3,2,1,0:T(2,128)S(1)} %bitcast.189), channel_id=1, source_target_pairs={{0,128},{64,192},{128,0},{192,64},{1,129},{65,193},{129,1},{193,65... | collective-permute-start | bytes 786440 | tf_op jit(solution)/shard_map/ppermute | solution.py:28
  171.5 22.5 %collective-permute-start.7 = (f32[1,256,256]{2,1,0:T(8,128)S(1)}, f32[1,256,256]{2,1,0:T(8,128)S(1)}, u32[]{:S(2)}, u32[]{:S(2)}) collective-permute-start(f32[1,256,256]{2,1,0:T(8,128)S(1)} %dynamic-slice_add_fusion), channel_id=1, source_target_pairs={{0,128},{64,192},{128,0},{192,64},{1,129},{65,193},{129,1},{193,65... | collective-permute-start | bytes 786440 | tf_op jit(solution)/shard_map/ppermute | solution.py:28
  183.4 11.6 %collective-permute-start.5 = (f32[2,64,2,256]{3,2,1,0:T(2,128)S(1)}, f32[2,64,2,256]{3,2,1,0:T(2,128)S(1)}, u32[]{:S(2)}, u32[]{:S(2)}) collective-permute-start(f32[2,64,2,256]{3,2,1,0:T(2,128)S(1)} %fusion.77), channel_id=1, source_target_pairs={{0,64},{64,0},{128,192},{192,128},{1,65},{65,1},{129,193},{193,129... | collective-permute-start | bytes 786440 | tf_op jit(solution)/shard_map/ppermute | solution.py:29
  194.0 2.2 collective-permute-start.8
  197.2 10.3 %copy-start.10 = (bf16[4,64,2,256]{3,0,2,1:T(4,128)(2,1)S(1)}, bf16[4,64,2,256]{3,0,2,1:T(4,128)(2,1)}, u32[]{:S(2)}) copy-start(bf16[4,64,2,256]{3,0,2,1:T(4,128)(2,1)} %copy-done.9) | copy-start | bytes 786436
  200.4 9.6 %collective-permute-start.9 = (f32[4,64,2,256]{3,1,2,0:T(8,128)S(1)}, f32[4,64,2,256]{3,1,2,0:T(8,128)S(1)}, u32[]{:S(2)}, u32[]{:S(2)}) collective-permute-start(f32[4,64,2,256]{3,1,2,0:T(8,128)S(1)} %fusion.54), channel_id=1, source_target_pairs={{0,64},{64,0},{128,192},{192,128},{1,65},{65,1},{129,193},{193,129... | collective-permute-start | bytes 1572872 | tf_op jit(solution)/shard_map/ppermute | solution.py:99
  210.4 8.0 %collective-permute-start.10 = (f32[2,64,2,256]{3,2,1,0:T(2,128)S(1)}, f32[2,64,2,256]{3,2,1,0:T(2,128)S(1)}, u32[]{:S(2)}, u32[]{:S(2)}) collective-permute-start(f32[2,64,2,256]{3,2,1,0:T(2,128)S(1)} %bitcast.181), channel_id=1, source_target_pairs={{0,128},{64,192},{128,0},{192,64},{1,129},{65,193},{129,1},{193,65... | collective-permute-start | bytes 786440 | tf_op jit(solution)/shard_map/ppermute | solution.py:103
  218.5 2.1 collective-permute-start.11
  219.4 3.0 %copy-start.1 = (f32[16,768]{1,0:T(8,128)S(1)}, f32[16,768]{1,0:T(8,128)}, u32[]{:S(2)}) copy-start(f32[16,768]{1,0:T(8,128)} %param.10) | copy-start | bytes 147460
